TPU v7x, 512 devices: a whole 4x8x8 slice. The times are simulated.
512 devices in a mesh: atom: 64 (over y, x, z_hi), ka: 8 (over z_lo, core).
Axes of the slice: x: 4, y: 8, z: 8 (z_hi: 2, z_lo: 4; z = z_hi * 4 + z_lo), core: 2. Of those that a mesh axis runs over, the one named last changes fastest.
Arguments:
- features: bfloat16 [131072, 256], P('atom'), may hold values from -6 to 6
- positions: float32 [3, 131072], P(None, 'atom'), may hold values from 0 to 1
- k_indices: int32 [3, 4096], P(None, 'ka'), may hold values from -8 to 8
- species: int32 [131072], P('atom'), may hold values from 0 to 7
- brick_counts: int32 [64], P('atom'), may hold values from 1024 to 2048, as said below
- smearing: float32 [256], replicated, may hold values from 0.01 to 0.03
- teacher_charge: float32 [256], replicated, may hold values from -0.375 to 0.375
- norm_gain: float32 [256], replicated, may hold values from 0.5 to 1.5
- w_mix: bfloat16 [256, 256], replicated, may hold values from -0.375 to 0.375
- w_read: float32 [256], replicated, may hold values from -0.375 to 0.375
- w_student: bfloat16 [256, 128], replicated, may hold values from -0.375 to 0.375
- species_embed: float32 [8, 128], replicated, may hold values from -3 to 3
- w_charge: float32 [128], replicated, may hold values from -0.5 to 0.5
- species_bias: float32 [8], replicated, may hold values from -3 to 3
- student_smear: float32 [1], replicated, may hold values from 0.05 to 0.15
Outputs:
- teacher_features: bfloat16 [131072, 256], P(('atom', 'ka'))
- teacher_forces: float32 [3, 131072], P(None, ('atom', 'ka'))
- student_forces: float32 [3, 131072], P(None, ('atom', 'ka'))
- student_energy: float32 [131072], P(('atom', 'ka'))
- distill_loss: float32 [], replicated
Inputs may be any that keep to these rules, and one draw needn't show every extreme that they name: The first brick_counts[b] atom slots of brick b hold real atoms and the rest are padding; some brick is full in every draw.
All inputs are finite; a program needn't handle non-finite values.
Results may differ from a plain program's by a relative error of at most 0.0075.
Values sent between devices are 32-bit elements; how exact they have to be, the bound alone decides.
No kernel may reach another device: no remote copies, remote signals or barrier semaphores. Data moves between devices by JAX's collectives and lax.ppermute only.
A program may use at most 64 MiB of HBM per device.

v0:
```python
import math

import jax
import jax.numpy as jnp
from jax import lax
from jax.sharding import PartitionSpec as P

TWO_PI = 2.0 * math.pi
SCREEN = 20.0
HIGHEST_PRECISION = lax.Precision.HIGHEST


def phase_table(positions, k_indices):
    k_float = k_indices.astype(jnp.float32)
    products = (
        positions[0][:, None] * k_float[0][None, :]
        + positions[1][:, None] * k_float[1][None, :]
        + positions[2][:, None] * k_float[2][None, :]
    )
    angles = TWO_PI * products
    return jnp.concatenate([jnp.cos(angles), jnp.sin(angles)], axis=1).astype(jnp.bfloat16)


def k_geometry(k_indices):
    k_vectors = TWO_PI * k_indices.astype(jnp.float32)
    k_square = (
        k_vectors[0] * k_vectors[0] + k_vectors[1] * k_vectors[1] + k_vectors[2] * k_vectors[2]
    )
    return (k_vectors, k_square)


def teacher_kernel(k_square, smearing, inv_root):
    spread = (smearing * smearing)[None, :]
    return jnp.exp(-0.5 * k_square[:, None] * spread) / (k_square[:, None] + SCREEN) * inv_root


def student_table(k_vectors, k_square, sums, student_smear, inv_root, k_width):
    spread = student_smear[0] * student_smear[0]
    kernel = jnp.exp(-0.5 * k_square * spread) / (k_square + SCREEN) * inv_root
    cos_part = kernel * sums[:k_width]
    sin_part = kernel * sums[k_width:]
    upper_rows = jnp.stack(
        [
            cos_part,
            -(k_vectors[0] * sin_part),
            -(k_vectors[1] * sin_part),
            -(k_vectors[2] * sin_part),
        ],
        axis=1,
    )
    lower_rows = jnp.stack(
        [sin_part, k_vectors[0] * cos_part, k_vectors[1] * cos_part, k_vectors[2] * cos_part],
        axis=1,
    )
    return jnp.concatenate([upper_rows, lower_rows], axis=0).astype(jnp.bfloat16)


def student_charge(features, species, live_mask, w_student, species_embed, w_charge, species_bias):
    onehot = (
        species[:, None] == jnp.arange(species_embed.shape[0], dtype=jnp.int32)[None, :]
    ).astype(jnp.float32)
    inner_sum = jnp.dot(features, w_student, preferred_element_type=jnp.float32) + jnp.dot(
        onehot, species_embed, precision=HIGHEST_PRECISION
    )
    hidden = jax.nn.silu(inner_sum)
    return (
        jnp.dot(hidden, w_charge, precision=HIGHEST_PRECISION)
        + jnp.dot(onehot, species_bias, precision=HIGHEST_PRECISION)
    ) * live_mask


def finish(
    potential, teacher_force, student_part, features, charge, live_mask, norm_gain, w_mix, w_read
):
    mean_square = jnp.mean(potential * potential, axis=1, keepdims=True)
    normed = (potential * lax.rsqrt(mean_square + 1e-06) * norm_gain[None, :]).astype(jnp.bfloat16)
    update = jax.nn.silu(jnp.dot(normed, w_mix, preferred_element_type=jnp.float32))
    combined = features.astype(jnp.float32) + update
    teacher_energy = jnp.dot(combined, w_read, precision=HIGHEST_PRECISION)
    student_energy = 0.5 * charge * student_part[:, 0]
    forces = charge[:, None] * student_part[:, 1:4]
    misfit = (student_energy - teacher_energy) ** 2 + jnp.sum(
        (forces - teacher_force) ** 2, axis=1
    ) / 3.0
    return (
        combined.astype(jnp.bfloat16),
        teacher_force,
        forces,
        student_energy,
        live_mask * misfit,
    )


def local(
    features,
    positions,
    k_indices,
    species,
    brick_counts,
    smearing,
    teacher_charge,
    norm_gain,
    w_mix,
    w_read,
    w_student,
    species_embed,
    w_charge,
    species_bias,
    student_smear,
):
    atom_rows = features.shape[0]
    k_width = k_indices.shape[1]
    inv_root = 1.0 / math.sqrt(atom_rows * lax.axis_size("atom"))
    live_mask = (jnp.arange(atom_rows, dtype=jnp.int32) < brick_counts[0]).astype(jnp.float32)
    masked = features * live_mask.astype(jnp.bfloat16)[:, None]
    charge = student_charge(
        features, species, live_mask, w_student, species_embed, w_charge, species_bias
    )
    charge_low = charge.astype(jnp.bfloat16)
    phases = phase_table(positions, k_indices)
    factor = lax.dot_general(
        phases, masked, (((0,), (0,)), ((), ())), preferred_element_type=jnp.float32
    )
    charge_sum = jnp.dot(charge_low, phases, preferred_element_type=jnp.float32)
    factor, charge_sum = lax.psum((factor, charge_sum), "atom")
    k_vectors, k_square = k_geometry(k_indices)
    kernel = teacher_kernel(k_square, smearing, inv_root)
    weighted = (jnp.concatenate([kernel, kernel], axis=0) * factor).astype(jnp.bfloat16)
    potential = jnp.dot(phases, weighted, preferred_element_type=jnp.float32)
    charged = (features.astype(jnp.float32) * teacher_charge[None, :]).astype(jnp.bfloat16)
    contracted = lax.dot_general(
        charged, weighted, (((1,), (1,)), ((), ())), preferred_element_type=jnp.float32
    )
    cosines = phases[:, :k_width].astype(jnp.float32)
    sines = phases[:, k_width:].astype(jnp.float32)
    force_terms = sines * contracted[:, :k_width] - cosines * contracted[:, k_width:]
    teacher_force = jnp.dot(force_terms, k_vectors.T, precision=HIGHEST_PRECISION)
    table = student_table(k_vectors, k_square, charge_sum, student_smear, inv_root, k_width)
    student_part = jnp.dot(phases, table, preferred_element_type=jnp.float32)
    share_rows = atom_rows // lax.axis_size("ka")
    row_start = lax.axis_index("ka") * share_rows

    def own_rows(values):
        return lax.dynamic_slice_in_dim(values, row_start, share_rows, 0)

    potential, teacher_force, student_part = lax.psum(
        (potential, teacher_force, student_part), "ka"
    )
    whole_rows = finish(
        potential,
        teacher_force,
        student_part,
        features,
        charge,
        live_mask,
        norm_gain,
        w_mix,
        w_read,
    )
    outputs = (
        own_rows(whole_rows[0]),
        own_rows(whole_rows[1]),
        own_rows(whole_rows[2]),
        own_rows(whole_rows[3]),
        own_rows(whole_rows[4]),
    )
    teacher_features, teacher_out, forces, student_energy, misfit = outputs
    loss_sum, live_sum = lax.psum((jnp.sum(misfit), jnp.sum(own_rows(live_mask))), ("atom", "ka"))
    return (teacher_features, teacher_out.T, forces.T, student_energy, loss_sum / live_sum)


def solution(mesh):
    in_specs = (
        P("atom", None),
        P(None, "atom"),
        P(None, "ka"),
        P("atom"),
        P("atom"),
        P(),
        P(),
        P(),
        P(),
        P(),
        P(),
        P(),
        P(),
        P(),
        P(),
    )
    out_specs = (
        P(("atom", "ka"), None),
        P(None, ("atom", "ka")),
        P(None, ("atom", "ka")),
        P(("atom", "ka")),
        P(),
    )
    return jax.shard_map(local, mesh=mesh, in_specs=in_specs, out_specs=out_specs, check_vma=False)
```

profile of v0, /device:TPU:1, one launch (start us, length us, event | category | flops | bytes accessed | tf_op | source)
XLA Modules:
  0.0 1086.3 jit_solution(1658053746841825445)
XLA Ops:
  8.0 0.7 convert_element_type.47
  8.7 0.9 fusion.58
  9.6 17.6 %cosine_convert_fusion = (bf16[2048,512]{1,0:T(8,128)(2,1)S(1)}, bf16[2048,512]{1,0:T(8,128)(2,1)S(1)}) fusion(f32[512]{0:T(512)S(1)} %bitcast.54, f32[2048]{0:T(1024)S(1)} %bitcast.39, f32[512]{0:T(512)S(1)} %bitcast.56, f32[2048]{0:T(1024)S(1)} %bitcast.41, f32[512]{0:T(512)S(1)} %bitcast.52, f32[2048]{0:T(1024)S(1)} %bitcast.37), kind=kLoop, calls=%fused_computation.8 | loop fusion | flops 8388608 | bytes 4225024 | tf_op jit(solution)/shard_map/slice | solution.py:134
  27.3 1.3 copy-done.3
  28.6 2.6 fusion.20
  32.4 0.7 fusion.16
  33.2 1.0 convolution_add_fusion
  34.2 1.2 fusion.10
  35.4 0.6 fusion.55
  36.0 203.7 %psum.52 = f32[1024]{0:T(1024)S(1)} all-reduce(f32[1024]{0:T(1024)S(1)} %bitcast.60), channel_id=1, replica_groups=mesh['atom'=64,'ka'=8] {'atom'}, use_global_device_ids=true, to_apply=%region_4.5 | all-reduce | flops 1024 | bytes 8192 | tf_op jit(solution)/shard_map/psum | solution.py:125
  240.0 599.3 %all-reduce.5.cloned.1.call-done = f32[1024,256]{1,0:T(8,128)} async-done(((f32[1024,256]{1,0:T(8,128)}), f32[1024,256]{1,0:T(8,128)}) %all-reduce.5.cloned.1.call-update) | async-done | bytes 1048592 | tf_op jit(solution)/shard_map/psum | solution.py:125
  839.4 5.1 fusion.53
  844.6 0.7 dynamic-slice_reduce_fusion
  845.3 3.5 fusion.26
  848.8 1.3 fusion.7
  850.1 20.6 %fusion.1 = f32[2048,3]{0,1:T(4,128)S(1)} fusion(f32[2048,1024]{1,0:T(8,128)S(1)} %fusion.7, s32[3,512]{1,0:T(4,128)S(1)} %copy-done.7, f32[512]{0:T(512)S(1)} %bitcast.55, f32[2048]{0:T(1024)S(1)} %bitcast.40, f32[512]{0:T(512)S(1)} %bitcast.57, f32[2048]{0:T(1024)S(1)} %bitcast.42, f32[512]{0:T(512)S(1)} %bitcast.53, f32[2048]{0:T(1024)S(1)} %bitcast.38), kind=kOutput, calls=%fused_computation.2 | convolution fusion | flops 51383296 | bytes 8450048 | tf_op jit(solution)/shard_map/dot_general | solution.py:137
  870.8 68.6 %all-reduce.1 = (f32[2048,3]{0,1:T(4,128)S(1)}, f32[2048,4]{0,1:T(4,128)S(1)}) all-reduce(f32[2048,3]{0,1:T(4,128)S(1)} %fusion.1, f32[2048,4]{0,1:T(4,128)S(1)} %fusion.26), channel_id=1, replica_groups=mesh['atom'=64,'ka'=8] {'ka'}, use_global_device_ids=true, to_apply=%region_3.4 | all-reduce | flops 14336 | bytes 114688 | tf_op jit(solution)/shard_map/psum | solution.py:146
  940.0 28.5 %all-reduce.7.cloned.1.call-done = f32[2048,256]{1,0:T(8,128)} async-done(((f32[2048,256]{1,0:T(8,128)}), f32[2048,256]{1,0:T(8,128)}) %all-reduce.7.cloned.1.call-update) | async-done | bytes 2097168 | tf_op jit(solution)/shard_map/psum | solution.py:146
  968.6 1.9 multiply_reduce_fusion
  970.5 2.4 convert_add_fusion
  973.0 0.7 dynamic-slice_convert_fusion
  973.7 1.9 fusion.62
  975.5 1.3 fusion.45
  976.8 100.2 %all-reduce = (f32[]{:T(128)}, f32[]{:T(128)}) all-reduce(f32[]{:T(128)} %get-tuple-element.9, f32[]{:T(128)} %dynamic-slice_reduce_fusion), channel_id=1, replica_groups=mesh['atom'=64,'ka'=8] {'atom','ka'}, use_global_device_ids=true, to_apply=%region_8.9 | all-reduce | flops 2 | bytes 16 | tf_op jit(solution)/shard_map/psum | solution.py:168
  (61 shorter events, 1.6 us)
Async XLA Ops:
  7.2 963.4 %copy-start = (bf16[256,256]{1,0:T(8,128)(2,1)S(1)}, bf16[256,256]{1,0:T(8,128)(2,1)}, u32[]{:S(2)}) copy-start(bf16[256,256]{1,0:T(8,128)(2,1)} %param.23) | copy-start | bytes 393220
  7.2 21.4 %copy-start.1 = (bf16[2048,256]{1,0:T(8,128)(2,1)S(1)}, bf16[2048,256]{1,0:T(8,128)(2,1)}, u32[]{:S(2)}) copy-start(bf16[2048,256]{1,0:T(8,128)(2,1)} %param.15) | copy-start | bytes 3145732
  7.2 832.2 %all-reduce.5.cloned.1.call-start = ((), (), s32[]{:S(2)}) async-start(), calls=%async_computation | async-start | bytes 2097152 | tf_op jit(solution)/shard_map/psum | solution.py:125
  27.2 1.3 copy-start.3
  27.2 8.1 copy-start.2
  28.6 3.4 copy-start.10
  28.6 3.4 copy-start.6
  28.6 3.8 copy-start.8
  28.6 3.9 copy-start.14
  28.6 4.6 copy-start.9
  31.2 2.9 copy-start.15
  31.3 937.3 %all-reduce.7.cloned.1.call-start = ((), (), s32[]{:S(2)}) async-start(), calls=%async_computation.1 | async-start | bytes 4194304 | tf_op jit(solution)/shard_map/psum | solution.py:146
  32.0 3.4 copy-start.4
  34.1 205.6 %copy-start.7 = (s32[3,512]{1,0:T(4,128)S(1)}, s32[3,512]{1,0:T(4,128)}, u32[]{:S(2)}) copy-start(s32[3,512]{1,0:T(4,128)} %param.17) | copy-start | bytes 18436
  845.3 3.5 copy-start.5
  845.3 3.5 copy-start.11
  850.1 120.4 %copy-start.13 = (f32[256]{0:T(256)S(1)}, f32[256]{0:T(256)}, u32[]{:S(2)}) copy-start(f32[256]{0:T(256)} %param.22) | copy-start | bytes 3076
  970.5 3.1 copy-start.12
Sparse Core Ops, SparseCore 0:
  31.4 807.9 all-reduce.4
  844.6 123.9 all-reduce.6
where the time goes:
time: 1090 us
  waiting for transfers between devices  628 us (58%)
  blocking collectives  372 us (34%)
  matrix products  41.4 us (4%)
  other arithmetic  22.5 us (2%)
  between operations  18.2 us (2%)
    psum x1, waiting for transfers between devices, local(): factor, charge_sum = lax.psum((factor, charge_sum), 'atom')  599 us
    psum x1, blocking collectives, local(): factor, charge_sum = lax.psum((factor, charge_sum), 'atom')  204 us
    psum x1, blocking collectives, local(): lax.psum((jnp.sum(misfit), jnp.sum(own_rows(live_mask))), ('atom', 'ka'))  100 us
    psum x1, blocking collectives, local(): lax.psum((potential, teacher_force, student_part), 'ka')  68.6 us
    psum x1, waiting for transfers between devices, local(): lax.psum((potential, teacher_force, student_part), 'ka')  28.5 us
  transfers between devices with their start and end apart: 2, of which 2 were waited for; matrix products, arithmetic and copies ran while one was open for 3% of the time, Pallas kernels for 0%

commit v1 on v0

--- a/solution.py
+++ b/solution.py
@@ -1,13 +1,20 @@
+import functools
 import math
 
 import jax
 import jax.numpy as jnp
 from jax import lax
+from jax.sharding import Mesh
 from jax.sharding import PartitionSpec as P
 
 TWO_PI = 2.0 * math.pi
 SCREEN = 20.0
 HIGHEST_PRECISION = lax.Precision.HIGHEST
+
+ATOM_AXES = ("y", "x", "zh")
+KA_AXES = ("zl", "core")
+ALL_AXES = ATOM_AXES + KA_AXES
+PAD_ROWS = 256
 
 
 def phase_table(positions, k_indices):
@@ -91,6 +98,14 @@
     )
 
 
+def sum_over_atoms(payload):
+    part = lax.psum_scatter(payload, "y", scatter_dimension=0, tiled=True)
+    part = lax.psum_scatter(part, "x", scatter_dimension=0, tiled=True)
+    part = lax.psum(part, "zh")
+    part = lax.all_gather(part, "x", axis=0, tiled=True)
+    return lax.all_gather(part, "y", axis=0, tiled=True)
+
+
 def local(
     features,
     positions,
@@ -110,7 +125,14 @@
 ):
     atom_rows = features.shape[0]
     k_width = k_indices.shape[1]
-    inv_root = 1.0 / math.sqrt(atom_rows * lax.axis_size("atom"))
+    channels = features.shape[1]
+    atom_groups = 1
+    for axis in ATOM_AXES:
+        atom_groups *= lax.axis_size(axis)
+    ka_groups = 1
+    for axis in KA_AXES:
+        ka_groups *= lax.axis_size(axis)
+    inv_root = 1.0 / math.sqrt(atom_rows * atom_groups)
     live_mask = (jnp.arange(atom_rows, dtype=jnp.int32) < brick_counts[0]).astype(jnp.float32)
     masked = features * live_mask.astype(jnp.bfloat16)[:, None]
     charge = student_charge(
@@ -122,7 +144,18 @@
         phases, masked, (((0,), (0,)), ((), ())), preferred_element_type=jnp.float32
     )
     charge_sum = jnp.dot(charge_low, phases, preferred_element_type=jnp.float32)
-    factor, charge_sum = lax.psum((factor, charge_sum), "atom")
+    extra = jnp.concatenate(
+        [
+            charge_sum,
+            brick_counts.astype(jnp.float32),
+            jnp.zeros((PAD_ROWS * channels - 2 * k_width - 1,), jnp.float32),
+        ]
+    ).reshape(PAD_ROWS, channels)
+    summed = sum_over_atoms(jnp.concatenate([factor, extra], axis=0))
+    factor = summed[: 2 * k_width]
+    extra = summed[2 * k_width :].reshape(-1)
+    charge_sum = extra[: 2 * k_width]
+    live_total = extra[2 * k_width]
     k_vectors, k_square = k_geometry(k_indices)
     kernel = teacher_kernel(k_square, smearing, inv_root)
     weighted = (jnp.concatenate([kernel, kernel], axis=0) * factor).astype(jnp.bfloat16)
@@ -137,45 +170,51 @@
     teacher_force = jnp.dot(force_terms, k_vectors.T, precision=HIGHEST_PRECISION)
     table = student_table(k_vectors, k_square, charge_sum, student_smear, inv_root, k_width)
     student_part = jnp.dot(phases, table, preferred_element_type=jnp.float32)
-    share_rows = atom_rows // lax.axis_size("ka")
-    row_start = lax.axis_index("ka") * share_rows
+    packed = jnp.concatenate(
+        [potential, teacher_force, student_part, jnp.zeros((atom_rows, 1), jnp.float32)], axis=1
+    )
+    own = lax.psum_scatter(packed, KA_AXES, scatter_dimension=0, tiled=True)
+    share_rows = atom_rows // ka_groups
+    ka_index = lax.axis_index(KA_AXES)
+    row_start = ka_index * share_rows
 
     def own_rows(values):
         return lax.dynamic_slice_in_dim(values, row_start, share_rows, 0)
 
-    potential, teacher_force, student_part = lax.psum(
-        (potential, teacher_force, student_part), "ka"
-    )
-    whole_rows = finish(
-        potential,
-        teacher_force,
-        student_part,
-        features,
-        charge,
-        live_mask,
+    teacher_features, teacher_out, forces, student_energy, misfit = finish(
+        own[:, :channels],
+        own[:, channels : channels + 3],
+        own[:, channels + 3 : channels + 7],
+        own_rows(features),
+        own_rows(charge),
+        own_rows(live_mask),
         norm_gain,
         w_mix,
         w_read,
     )
-    outputs = (
-        own_rows(whole_rows[0]),
-        own_rows(whole_rows[1]),
-        own_rows(whole_rows[2]),
-        own_rows(whole_rows[3]),
-        own_rows(whole_rows[4]),
-    )
-    teacher_features, teacher_out, forces, student_energy, misfit = outputs
-    loss_sum, live_sum = lax.psum((jnp.sum(misfit), jnp.sum(own_rows(live_mask))), ("atom", "ka"))
-    return (teacher_features, teacher_out.T, forces.T, student_energy, loss_sum / live_sum)
+    loss_sum = functools.reduce(lambda v, axis: lax.psum(v, axis), ALL_AXES, jnp.sum(misfit))
+    return (teacher_features, teacher_out.T, forces.T, student_energy, loss_sum / live_total)
 
 
 def solution(mesh):
+    sizes = dict(mesh.shape)
+    ka = sizes["ka"]
+    atom = sizes["atom"]
+    cores = 2
+    z_lo = ka // cores
+    devices = mesh.devices.reshape(-1)
+    y_size = 8 if atom % 8 == 0 else 1
+    rest = atom // y_size
+    zh = 2 if rest % 2 == 0 else 1
+    x_size = rest // zh
+    fine = Mesh(devices.reshape(y_size, x_size, zh, z_lo, cores), ALL_AXES)
+    atom_spec = ATOM_AXES
     in_specs = (
-        P("atom", None),
-        P(None, "atom"),
-        P(None, "ka"),
-        P("atom"),
-        P("atom"),
+        P(atom_spec, None),
+        P(None, atom_spec),
+        P(None, KA_AXES),
+        P(atom_spec),
+        P(atom_spec),
         P(),
         P(),
         P(),
@@ -188,10 +227,10 @@
         P(),
     )
     out_specs = (
-        P(("atom", "ka"), None),
-        P(None, ("atom", "ka")),
-        P(None, ("atom", "ka")),
-        P(("atom", "ka")),
-        P(),
-    )
-    return jax.shard_map(local, mesh=mesh, in_specs=in_specs, out_specs=out_specs, check_vma=False)
+        P(ALL_AXES, None),
+        P(None, ALL_AXES),
+        P(None, ALL_AXES),
+        P(ALL_AXES),
+        P(),
+    )
+    return jax.shard_map(local, mesh=fine, in_specs=in_specs, out_specs=out_specs, check_vma=False)

time: 1090 us -> 327 us (0.30)
  waiting for transfers between devices: 628 us -> 154 us
  blocking collectives: 372 us -> 79 us
    psum x2 -> x0, waiting for transfers between devices: 628 us -> none  [the longest x1 599 us: local(): factor, charge_sum = lax.psum((factor, charge_sum), 'atom')]
    psum x3 -> x6, blocking collectives: 372 us -> 69.1 us  [the longest x5 53 us: local(): lax.psum(v, axis)]
    reduce_scatter x0 -> x3, waiting for transfers between devices: none -> 117 us  [the longest x1 44.2 us: local(): own = lax.psum_scatter(packed, KA_AXES, scatter_dimension=0, tiled=True)]
    all_gather x0 -> x1, waiting for transfers between devices: none -> 36.9 us  [sum_over_atoms(): return lax.all_gather(part, 'y', axis=0, tiled=True)]
  transfers between devices with their start and end apart: 2 -> 4, of which waited for: 2 -> 4; matrix products, arithmetic and copies ran while one was open for 3% -> 1% of each run, Pallas kernels for 0% -> 0%
where the time goes in v1:
time: 327 us; the launch traced here: 326 us
  waiting for transfers between devices  154 us (47%)
  blocking collectives  79 us (24%)
  matrix products  37.7 us (12%)
  other arithmetic  27.7 us (8%)
  between operations  17.9 us (5%)
  local copies, waits for them, and re-layouts  9.57 us (3%)
    psum x5, blocking collectives, local(): lax.psum(v, axis)  53 us
    reduce_scatter x1, waiting for transfers between devices, local(): own = lax.psum_scatter(packed, KA_AXES, scatter_dimension=0, tiled=True)  44.2 us
    reduce_scatter x1, waiting for transfers between devices, sum_over_atoms(): part = lax.psum_scatter(payload, 'y', scatter_dimension=0, tiled=True)  43.4 us
    all_gather x1, waiting for transfers between devices, sum_over_atoms(): return lax.all_gather(part, 'y', axis=0, tiled=True)  36.9 us
    reduce_scatter x1, waiting for transfers between devices, sum_over_atoms(): part = lax.psum_scatter(part, 'x', scatter_dimension=0, tiled=True)  29.4 us
    dot_general x1, matrix products, local(): jnp.dot(force_terms, k_vectors.T, precision=HIGHEST_PRECISION)  20.6 us
    slice x1, other arithmetic, local(): cosines = phases[:, :k_width].astype(jnp.float32)  17.6 us
    psum x1, blocking collectives, sum_over_atoms(): part = lax.psum(part, 'zh')  16.1 us
  transfers between devices with their start and end apart: 4, of which 4 were waited for; matrix products, arithmetic and copies ran while one was open for 1% of the time, Pallas kernels for 0%

profile of v1, /device:TPU:1, one launch (start us, length us, event | category | flops | bytes accessed | tf_op | source)
XLA Modules:
  0.0 326.0 jit_solution(14616286438022679318)
XLA Ops:
  9.5 1.6 fusion.69
  11.2 1.4 fusion.14
  12.6 1.7 convolution_add_fusion
  16.2 17.6 %cosine_convert_fusion = (bf16[2048,512]{1,0:T(8,128)(2,1)S(1)}, bf16[2048,512]{1,0:T(8,128)(2,1)S(1)}) fusion(f32[512]{0:T(512)S(1)} %bitcast.109, f32[2048]{0:T(1024)S(1)} %bitcast.101, f32[512]{0:T(512)S(1)} %bitcast.111, f32[2048]{0:T(1024)S(1)} %bitcast.103, f32[512]{0:T(512)S(1)} %bitcast.107, f32[2048]{0:T(1024)S(1)} %bitcast.99), kind=kLoop, calls=%fused_computation.8 | loop fusion | flops 8388608 | bytes 4225024 | tf_op jit(solution)/shard_map/slice | solution.py:167
  35.8 3.0 concatenate.22
  39.9 3.2 fusion.15
  44.4 43.4 %reduce-scatter.4.cloned.1.call-done = f32[160,256]{1,0:T(8,128)} async-done(((f32[1280,256]{1,0:T(8,128)}), f32[160,256]{1,0:T(8,128)}) %reduce-scatter.4.cloned.1.call-update) | async-done | bytes 163856 | tf_op jit(solution)/shard_map/reduce_scatter | solution.py:102
  87.8 29.4 %reduce-scatter.6.cloned.1.call-done = f32[40,256]{1,0:T(8,128)} async-done(((f32[160,256]{1,0:T(8,128)}), f32[40,256]{1,0:T(8,128)}) %reduce-scatter.6.cloned.1.call-update) | async-done | bytes 40976 | tf_op jit(solution)/shard_map/reduce_scatter | solution.py:103
  117.2 16.1 %psum.42 = f32[40,256]{1,0:T(8,128)S(1)} all-reduce(f32[40,256]{1,0:T(8,128)} %reduce-scatter.6.cloned.1.call-done), channel_id=1, replica_groups=mesh['y'=8,'x'=4,'zh'=2,'zl'=4,'core'=2] {'zh'}, use_global_device_ids=true, to_apply=%region_2.3 | all-reduce | flops 10240 | bytes 81920 | tf_op jit(solution)/shard_map/psum | solution.py:104
  133.3 9.9 %all_gather.6 = f32[160,256]{1,0:T(8,128)} all-gather(f32[40,256]{1,0:T(8,128)S(1)} %psum.42), channel_id=1, replica_groups=mesh['y'=8,'x'=4,'zh'=2,'zl'=4,'core'=2] {'x'}, dimensions={0}, use_global_device_ids=true | all-gather | bytes 204800 | tf_op jit(solution)/shard_map/all_gather | solution.py:105
  145.9 36.9 %all-gather.2.cloned.1.call-done = f32[1280,256]{1,0:T(8,128)} async-done(((f32[160,256]{1,0:T(8,128)}), f32[1280,256]{1,0:T(8,128)}) %all-gather.2.cloned.1.call-update) | async-done | bytes 1310736 | tf_op jit(solution)/shard_map/all_gather | solution.py:106
  183.7 2.5 fusion.5
  186.3 20.6 %fusion.1 = f32[2048,3]{0,1:T(4,128)S(1)} fusion(f32[2048,1024]{1,0:T(8,128)S(1)} %fusion.5, s32[3,512]{1,0:T(4,128)S(1)} %copy-done.9, f32[512]{0:T(512)S(1)} %bitcast.110, f32[2048]{0:T(1024)S(1)} %bitcast.102, f32[512]{0:T(512)S(1)} %bitcast.112, f32[2048]{0:T(1024)S(1)} %bitcast.104, f32[512]{0:T(512)S(1)} %bitcast.108, f32[2048]{0:T(1024)S(1)} %bitcast.100), kind=kOutput, calls=%fused_computation.2 | convolution fusion | flops 51383296 | bytes 8450048 | tf_op jit(solution)/shard_map/dot_general | solution.py:170
  208.3 1.3 fusion.59
  209.7 1.6 maximum_maximum_fusion
  212.0 44.2 %reduce-scatter.8.cloned.1.call-done = f32[256,264]{0,1:T(8,128)} async-done(((f32[2048,264]{0,1:T(8,128)}), f32[256,264]{0,1:T(8,128)}) %reduce-scatter.8.cloned.1.call-update) | async-done | bytes 270352 | tf_op jit(solution)/shard_map/reduce_scatter | solution.py:176
  257.2 2.0 fusion.68
  260.2 1.4 multiply_reduce_fusion.1
  261.6 1.9 multiply_reduce_fusion.2
  263.5 13.9 %psum.43 = f32[]{:T(128)} all-reduce(f32[]{:T(128)} %get-tuple-element.5), channel_id=1, replica_groups=mesh['y'=8,'x'=4,'zh'=2,'zl'=4,'core'=2] {'y'}, use_global_device_ids=true, to_apply=%region_7.8 | all-reduce | flops 1 | bytes 8 | tf_op jit(solution)/shard_map/psum | solution.py:195
  277.4 9.0 %psum.44 = f32[]{:T(128)} all-reduce(f32[]{:T(128)} %psum.43), channel_id=1, replica_groups=mesh['y'=8,'x'=4,'zh'=2,'zl'=4,'core'=2] {'x'}, use_global_device_ids=true, to_apply=%region_8.9 | all-reduce | flops 1 | bytes 8 | tf_op jit(solution)/shard_map/psum | solution.py:195
  286.5 8.3 %psum.45 = f32[]{:T(128)} all-reduce(f32[]{:T(128)} %psum.44), channel_id=1, replica_groups=mesh['y'=8,'x'=4,'zh'=2,'zl'=4,'core'=2] {'zh'}, use_global_device_ids=true, to_apply=%region_9.10 | all-reduce | flops 1 | bytes 8 | tf_op jit(solution)/shard_map/psum | solution.py:195
  294.9 11.2 %psum.46 = f32[]{:T(128)} all-reduce(f32[]{:T(128)} %psum.45), channel_id=1, replica_groups=mesh['y'=8,'x'=4,'zh'=2,'zl'=4,'core'=2] {'zl'}, use_global_device_ids=true, to_apply=%region_10.11 | all-reduce | flops 1 | bytes 8 | tf_op jit(solution)/shard_map/psum | solution.py:195
  306.7 10.5 %psum.47 = f32[]{:T(128)} all-reduce(f32[]{:T(128)} %psum.46), channel_id=1, replica_groups=mesh['y'=8,'x'=4,'zh'=2,'zl'=4,'core'=2] {'core'}, use_global_device_ids=true, to_apply=%region_11.12 | all-reduce | flops 1 | bytes 8 | tf_op jit(solution)/shard_map/psum | solution.py:195
  (79 shorter events, 15.5 us)
Async XLA Ops:
  7.2 250.0 %copy-start = (bf16[256,256]{1,0:T(8,128)(2,1)S(1)}, bf16[256,256]{1,0:T(8,128)(2,1)}, u32[]{:S(2)}) copy-start(bf16[256,256]{1,0:T(8,128)(2,1)} %param.23) | copy-start | bytes 393220
  7.2 7.1 %copy-start.18 = (f32[128]{0:T(128)S(1)}, f32[128]{0:T(128)}, u32[]{:S(2)}) copy-start(f32[128]{0:T(128)} %param.27) | copy-start | bytes 1540
  7.2 80.6 %reduce-scatter.4.cloned.1.call-start = ((), (), s32[]{:S(2)}) async-start(), calls=%async_computation.3 | async-start | bytes 1474560 | tf_op jit(solution)/shard_map/reduce_scatter | solution.py:102
  8.1 8.0 %copy-start.7 = (f32[1,2048]{1,0:T(1,128)}, f32[1,2048]{1,0:T(1,128)S(1)}, u32[]{:S(2)}) copy-start(f32[1,2048]{1,0:T(1,128)S(1)} %get-tuple-element.23) | copy-start | bytes 24580
  8.9 7.3 %copy-start.10 = (f32[1,512]{1,0:T(1,128)}, f32[1,512]{1,0:T(1,128)S(1)}, u32[]{:S(2)}) copy-start(f32[1,512]{1,0:T(1,128)S(1)} %get-tuple-element.34) | copy-start | bytes 6148
  8.9 7.3 %copy-start.12 = (f32[1,512]{1,0:T(1,128)}, f32[1,512]{1,0:T(1,128)S(1)}, u32[]{:S(2)}) copy-start(f32[1,512]{1,0:T(1,128)S(1)} %get-tuple-element.35) | copy-start | bytes 6148
  8.9 7.3 %copy-start.14 = (f32[1,512]{1,0:T(1,128)}, f32[1,512]{1,0:T(1,128)S(1)}, u32[]{:S(2)}) copy-start(f32[1,512]{1,0:T(1,128)S(1)} %get-tuple-element.36) | copy-start | bytes 6148
  33.8 1.3 copy-start.4
  33.8 9.3 %copy-start.2 = (bf16[2048,512]{1,0:T(8,128)(2,1)}, bf16[2048,512]{1,0:T(8,128)(2,1)S(1)}, u32[]{:S(2)}) copy-start(bf16[2048,512]{1,0:T(8,128)(2,1)S(1)} %get-tuple-element.24) | copy-start | bytes 6291460
  33.8 6.1 %copy-start.1 = (bf16[2048,256]{1,0:T(8,128)(2,1)S(1)}, bf16[2048,256]{1,0:T(8,128)(2,1)}, u32[]{:S(2)}) copy-start(bf16[2048,256]{1,0:T(8,128)(2,1)} %param.15) | copy-start | bytes 3145732
  44.3 72.9 %reduce-scatter.6.cloned.1.call-start = ((), (), s32[]{:S(2)}) async-start(), calls=%async_computation.4 | async-start | bytes 204800 | tf_op jit(solution)/shard_map/reduce_scatter | solution.py:103
  87.8 95.0 %all-gather.2.cloned.1.call-start = ((), (), s32[]{:S(2)}) async-start(), calls=%async_computation.5 | async-start | bytes 1474560 | tf_op jit(solution)/shard_map/all_gather | solution.py:106
  143.2 113.0 %reduce-scatter.8.cloned.1.call-start = ((), (), s32[]{:S(2)}) async-start(), calls=%async_computation.6 | async-start | bytes 2433024 | tf_op jit(solution)/shard_map/reduce_scatter | solution.py:176
  183.6 2.6 copy-start.8
  183.6 2.6 copy-start.9
  183.6 2.6 copy-start.11
  183.6 2.6 copy-start.13
  183.6 2.6 copy-start.15
  186.3 20.7 %copy-start.3 = (bf16[2048,512]{1,0:T(8,128)(2,1)S(1)}, bf16[2048,512]{1,0:T(8,128)(2,1)}, u32[]{:S(2)}) copy-start(bf16[2048,512]{1,0:T(8,128)(2,1)} %copy-done.2) | copy-start | bytes 6291460
  186.3 20.7 %copy-start.5 = (bf16[2048,512]{1,0:T(8,128)(2,1)S(1)}, bf16[2048,512]{1,0:T(8,128)(2,1)}, u32[]{:S(2)}) copy-start(bf16[2048,512]{1,0:T(8,128)(2,1)} %copy-done.4) | copy-start | bytes 6291460
  207.0 1.3 copy-start.6
  209.6 47.6 %copy-start.17 = (f32[256]{0:T(256)S(1)}, f32[256]{0:T(256)}, u32[]{:S(2)}) copy-start(f32[256]{0:T(256)} %param.22) | copy-start | bytes 3076
  209.7 49.5 %copy-start.16 = (f32[256]{0:T(256)S(1)}, f32[256]{0:T(256)}, u32[]{:S(2)}) copy-start(f32[256]{0:T(256)} %param.24) | copy-start | bytes 3076
Sparse Core Ops, SparseCore 0:
  44.5 43.2 reduce-scatter.3
  90.6 26.6 reduce-scatter.5
  143.3 39.4 all-gather.1
  211.4 44.7 reduce-scatter.7

commit v2 on v1

--- a/solution.py
+++ b/solution.py
@@ -1,4 +1,3 @@
-import functools
 import math
 
 import jax
@@ -14,7 +13,6 @@
 ATOM_AXES = ("y", "x", "zh")
 KA_AXES = ("zl", "core")
 ALL_AXES = ATOM_AXES + KA_AXES
-PAD_ROWS = 256
 
 
 def phase_table(positions, k_indices):
@@ -99,11 +97,23 @@
 
 
 def sum_over_atoms(payload):
-    part = lax.psum_scatter(payload, "y", scatter_dimension=0, tiled=True)
-    part = lax.psum_scatter(part, "x", scatter_dimension=0, tiled=True)
-    part = lax.psum(part, "zh")
-    part = lax.all_gather(part, "x", axis=0, tiled=True)
-    return lax.all_gather(part, "y", axis=0, tiled=True)
+    parts = lax.all_to_all(payload, ATOM_AXES, 0, 0, tiled=True)
+    reduced = jnp.sum(parts, axis=0, keepdims=True)
+    spread = jnp.broadcast_to(reduced, payload.shape)
+    return lax.all_to_all(spread, ATOM_AXES, 0, 0, tiled=True)
+
+
+def sum_over_ka(payload):
+    parts = lax.all_to_all(payload, KA_AXES, 0, 0, tiled=True)
+    return jnp.sum(parts, axis=0)
+
+
+def sum_over_all(value):
+    devices = 1
+    for axis in ALL_AXES:
+        devices *= lax.axis_size(axis)
+    copies = jnp.broadcast_to(value.reshape(1), (devices,))
+    return jnp.sum(lax.all_to_all(copies, ALL_AXES, 0, 0, tiled=True))
 
 
 def local(
@@ -144,16 +154,18 @@
         phases, masked, (((0,), (0,)), ((), ())), preferred_element_type=jnp.float32
     )
     charge_sum = jnp.dot(charge_low, phases, preferred_element_type=jnp.float32)
+    rows_each = 2 * k_width // atom_groups
     extra = jnp.concatenate(
         [
             charge_sum,
             brick_counts.astype(jnp.float32),
-            jnp.zeros((PAD_ROWS * channels - 2 * k_width - 1,), jnp.float32),
+            jnp.zeros((atom_groups * channels - 2 * k_width - 1,), jnp.float32),
         ]
-    ).reshape(PAD_ROWS, channels)
-    summed = sum_over_atoms(jnp.concatenate([factor, extra], axis=0))
-    factor = summed[: 2 * k_width]
-    extra = summed[2 * k_width :].reshape(-1)
+    ).reshape(atom_groups, 1, channels)
+    payload = jnp.concatenate([factor.reshape(atom_groups, rows_each, channels), extra], axis=1)
+    summed = sum_over_atoms(payload)
+    factor = summed[:, :rows_each].reshape(2 * k_width, channels)
+    extra = summed[:, rows_each:].reshape(-1)
     charge_sum = extra[: 2 * k_width]
     live_total = extra[2 * k_width]
     k_vectors, k_square = k_geometry(k_indices)
@@ -167,24 +179,35 @@
     cosines = phases[:, :k_width].astype(jnp.float32)
     sines = phases[:, k_width:].astype(jnp.float32)
     force_terms = sines * contracted[:, :k_width] - cosines * contracted[:, k_width:]
-    teacher_force = jnp.dot(force_terms, k_vectors.T, precision=HIGHEST_PRECISION)
+    terms_high = force_terms.astype(jnp.bfloat16)
+    terms_low = (force_terms - terms_high.astype(jnp.float32)).astype(jnp.bfloat16)
+    k_low = k_indices.astype(jnp.bfloat16)
+    teacher_force_t = TWO_PI * (
+        lax.dot_general(k_low, terms_high, (((1,), (1,)), ((), ())), preferred_element_type=jnp.float32)
+        + lax.dot_general(k_low, terms_low, (((1,), (1,)), ((), ())), preferred_element_type=jnp.float32)
+    )
     table = student_table(k_vectors, k_square, charge_sum, student_smear, inv_root, k_width)
-    student_part = jnp.dot(phases, table, preferred_element_type=jnp.float32)
-    packed = jnp.concatenate(
-        [potential, teacher_force, student_part, jnp.zeros((atom_rows, 1), jnp.float32)], axis=1
-    )
-    own = lax.psum_scatter(packed, KA_AXES, scatter_dimension=0, tiled=True)
+    student_part_t = lax.dot_general(
+        table, phases, (((0,), (1,)), ((), ())), preferred_element_type=jnp.float32
+    )
     share_rows = atom_rows // ka_groups
+    side = jnp.concatenate(
+        [teacher_force_t, student_part_t, jnp.zeros((1, atom_rows), jnp.float32)], axis=0
+    )
+    side = side.reshape(8, ka_groups, share_rows).transpose(1, 0, 2)
+    packed = jnp.concatenate([potential.reshape(ka_groups, share_rows, channels), side], axis=1)
+    own = sum_over_ka(packed)
     ka_index = lax.axis_index(KA_AXES)
     row_start = ka_index * share_rows
 
     def own_rows(values):
         return lax.dynamic_slice_in_dim(values, row_start, share_rows, 0)
 
+    own_side = own[share_rows:].T
     teacher_features, teacher_out, forces, student_energy, misfit = finish(
-        own[:, :channels],
-        own[:, channels : channels + 3],
-        own[:, channels + 3 : channels + 7],
+        own[:share_rows],
+        own_side[:, 0:3],
+        own_side[:, 3:7],
         own_rows(features),
         own_rows(charge),
         own_rows(live_mask),
@@ -192,7 +215,7 @@
         w_mix,
         w_read,
     )
-    loss_sum = functools.reduce(lambda v, axis: lax.psum(v, axis), ALL_AXES, jnp.sum(misfit))
+    loss_sum = sum_over_all(jnp.sum(misfit))
     return (teacher_features, teacher_out.T, forces.T, student_energy, loss_sum / live_total)
 
 

time: 327 us -> 264 us (0.81)
  waiting for transfers between devices: 154 us -> 84.3 us
  other arithmetic: 27.7 us -> 61.6 us
  starting transfers between devices: 0.34 us -> 26.7 us
  matrix products: 37.7 us -> 15.5 us
  blocking collectives: 79 us -> 61.6 us
  between operations: 17.9 us -> 4.77 us
    reduce_scatter x3 -> x0, waiting for transfers between devices: 117 us -> none  [the longest x1 44.2 us: local(): own = lax.psum_scatter(packed, KA_AXES, scatter_dimension=0, tiled=True)]
    all_to_all x0 -> x3, waiting for transfers between devices: none -> 84.3 us  [the longest x1 49.5 us: sum_over_ka(): parts = lax.all_to_all(payload, KA_AXES, 0, 0, tiled=True)]
    psum x6 -> x0, blocking collectives: 69.1 us -> none  [the longest x5 53 us: local(): lax.psum(v, axis)]
    all_to_all x0 -> x1, blocking collectives: none -> 61.6 us  [sum_over_atoms(): parts = lax.all_to_all(payload, ATOM_AXES, 0, 0, tiled=True)]
    all_gather x1 -> x0, waiting for transfers between devices: 36.9 us -> none  [sum_over_atoms(): return lax.all_gather(part, 'y', axis=0, tiled=True)]
    all_to_all x0 -> x3, starting transfers between devices: none -> 26.7 us  [the longest x1 10.5 us: sum_over_ka(): parts = lax.all_to_all(payload, KA_AXES, 0, 0, tiled=True)]
    dot_general x2 -> x3, matrix products: 21.8 us -> 2.48 us  [the longest x1 1.17 us: local(): lax.dot_general(table, phases, (((0,), (1,)), ((), ())), preferred_elemen...]
    another operation x3 -> x4, other arithmetic: 0.05 us -> 19 us
  transfers between devices with their start and end apart: 4 -> 3, of which waited for: 4 -> 3; matrix products, arithmetic and copies ran while one was open for 1% -> 8% of each run, Pallas kernels for 0% -> 0%
where the time goes in v2:
time: 264 us; the launch traced here: 263 us
  waiting for transfers between devices  84.3 us (32%)
  other arithmetic  61.6 us (23%)
  blocking collectives  61.6 us (23%)
  starting transfers between devices  26.7 us (10%)
  matrix products  15.5 us (6%)
  local copies, waits for them, and re-layouts  8.26 us (3%)
  between operations  4.77 us (2%)
    all_to_all x1, blocking collectives, sum_over_atoms(): parts = lax.all_to_all(payload, ATOM_AXES, 0, 0, tiled=True)  61.6 us
    all_to_all x1, waiting for transfers between devices, sum_over_ka(): parts = lax.all_to_all(payload, KA_AXES, 0, 0, tiled=True)  49.5 us
    another operation x4, other arithmetic  19 us
    all_to_all x1, waiting for transfers between devices, sum_over_atoms(): return lax.all_to_all(spread, ATOM_AXES, 0, 0, tiled=True)  18.9 us
    slice x1, other arithmetic, local(): cosines = phases[:, :k_width].astype(jnp.float32)  17.6 us
    sub x1, other arithmetic, local(): sines * contracted[:, :k_width] - cosines * contracted[:, k_width:]  17.1 us
    all_to_all x1, waiting for transfers between devices, sum_over_all(): return jnp.sum(lax.all_to_all(copies, ALL_AXES, 0, 0, tiled=True))  15.9 us
    all_to_all x1, starting transfers between devices, sum_over_ka(): parts = lax.all_to_all(payload, KA_AXES, 0, 0, tiled=True)  10.5 us
  transfers between devices with their start and end apart: 3, of which 3 were waited for; matrix products, arithmetic and copies ran while one was open for 8% of the time, Pallas kernels for 0%

profile of v2, /device:TPU:1, one launch (start us, length us, event | category | flops | bytes accessed | tf_op | source)
XLA Modules:
  0.0 262.7 jit_solution(16284474322274433248)
XLA Ops:
  3.0 1.4 fusion.22
  4.4 1.7 fusion.77
  6.1 1.7 convolution_add_fusion
  7.8 1.2 fusion.16
  9.0 17.6 %cosine_convert_fusion = (bf16[2048,512]{1,0:T(8,128)(2,1)S(1)}, bf16[2048,512]{1,0:T(8,128)(2,1)S(1)}) fusion(f32[512]{0:T(512)S(1)} %bitcast.115, f32[2048]{0:T(1024)S(1)} %bitcast.107, f32[512]{0:T(512)S(1)} %bitcast.118, f32[2048]{0:T(1024)S(1)} %bitcast.109, f32[512]{0:T(512)S(1)} %bitcast.112, f32[2048]{0:T(1024)S(1)} %bitcast.105), kind=kLoop, calls=%fused_computation.10 | loop fusion | flops 8388608 | bytes 4225024 | tf_op jit(solution)/shard_map/slice | solution.py:179
  27.3 1.7 fusion.9
  29.3 61.6 %all_to_all.21 = f32[64,17,256]{2,1,0:T(8,128)S(1)} all-to-all(f32[64,17,256]{2,1,0:T(8,128)S(1)} %pad_maximum_fusion.2), channel_id=1, replica_groups=mesh['y'=8,'x'=4,'zh'=2,'zl'=4,'core'=2] {'y','x','zh'}, dimensions={0} | all-to-all | bytes 2228224 | tf_op jit(solution)/shard_map/all_to_all | solution.py:100
  91.0 1.3 broadcast_in_dim.9
  92.3 7.1 %all-to-all-start.1 = ((f32[64,17,256]{2,1,0:T(8,128)}), f32[64,17,256]{2,1,0:T(8,128)S(1)}, u32[]{:S(2)}, u32[]{:S(2)}) async-start(f32[64,17,256]{2,1,0:T(8,128)} %broadcast_in_dim.9), calls=%async_computation.1 | async-start | bytes 3145728 | tf_op jit(solution)/shard_map/all_to_all | solution.py:103
  100.5 19.0 %cosine_convert_fusion.1 = (bf16[8,256,512]{2,1,0:T(8,128)(2,1)}, bf16[8,256,512]{2,1,0:T(8,128)(2,1)}) fusion(f32[512]{0:T(512)S(1)} %bitcast.116, f32[8,256]{1,0:T(8,128)S(1)} %mul.574, f32[512]{0:T(512)S(1)} %bitcast.119, f32[8,256]{1,0:T(8,128)S(1)} %mul.569, f32[512]{0:T(512)S(1)} %bitcast.113, f32[8,256]{1,0:T(8,128)S(1)} %mul.564), kind=kLoop, calls=%fused_computation.13 | loop fusion | flops 8388608 | bytes 4225024 | tf_op jit(solution)/shard_map/convert.12
  119.4 18.9 %all-to-all-done.1 = f32[64,17,256]{2,1,0:T(8,128)S(1)} async-done(((f32[64,17,256]{2,1,0:T(8,128)}), f32[64,17,256]{2,1,0:T(8,128)S(1)}, u32[]{:S(2)}, u32[]{:S(2)}) %all-to-all-start.1) | async-done | bytes 1114144 | tf_op jit(solution)/shard_map/all_to_all | solution.py:103
  138.6 1.3 fusion.10
  139.9 17.1 %fusion = f32[2048,512]{1,0:T(8,128)S(1)} fusion(f32[2048,1024]{1,0:T(8,128)S(1)} %fusion.10, f32[512]{0:T(512)S(1)} %bitcast.117, f32[2048]{0:T(1024)S(1)} %bitcast.108, f32[512]{0:T(512)S(1)} %bitcast.120, f32[2048]{0:T(1024)S(1)} %bitcast.110, f32[512]{0:T(512)S(1)} %bitcast.114, f32[2048]{0:T(1024)S(1)} %bitcast.106), kind=kLoop, calls=%fused_computation.1 | loop fusion | flops 13631488 | bytes 12613632 | tf_op jit(solution)/shard_map/sub | solution.py:181
  159.2 1.3 fusion.1
  161.4 1.2 fusion.7
  162.7 1.5 pad_maximum_fusion.1
  164.2 10.5 %all-to-all-start.2 = ((f32[8,264,256]{2,1,0:T(8,128)}), f32[8,264,256]{2,1,0:T(8,128)S(1)}, u32[]{:S(2)}, u32[]{:S(2)}) async-start(f32[8,264,256]{2,1,0:T(8,128)} %pad_maximum_fusion.1), calls=%async_computation.2 | async-start | bytes 4325376 | tf_op jit(solution)/shard_map/all_to_all | solution.py:107
  174.8 49.5 %all-to-all-done.2 = f32[8,264,256]{2,1,0:T(8,128)S(1)} async-done(((f32[8,264,256]{2,1,0:T(8,128)}), f32[8,264,256]{2,1,0:T(8,128)S(1)}, u32[]{:S(2)}, u32[]{:S(2)}) %all-to-all-start.2) | async-done | bytes 2162720 | tf_op jit(solution)/shard_map/all_to_all | solution.py:107
  227.6 1.9 fusion.76
  229.8 1.3 multiply_reduce_fusion.2
  231.1 1.5 broadcast_in_dim.11
  232.5 9.1 %all-to-all-start.3 = ((f32[512,1,1]{2,1,0:T(1,128)}), f32[512,1,1]{2,1,0:T(1,128)S(1)}, u32[]{:S(2)}, u32[]{:S(2)}) async-start(f32[512,1,1]{2,1,0:T(1,128)} %broadcast_in_dim.11), calls=%async_computation.3 | async-start | bytes 524288 | tf_op jit(solution)/shard_map/all_to_all | solution.py:116
  243.2 15.9 %all-to-all-done.3 = f32[512,1,1]{2,1,0:T(1,128)S(1)} async-done(((f32[512,1,1]{2,1,0:T(1,128)}), f32[512,1,1]{2,1,0:T(1,128)S(1)}, u32[]{:S(2)}, u32[]{:S(2)}) %all-to-all-start.3) | async-done | bytes 2080 | tf_op jit(solution)/shard_map/all_to_all | solution.py:116
  259.1 1.1 reduce_sum.59
  (69 shorter events, 11.7 us)
Async XLA Ops:
  0.6 227.0 %copy-start = (bf16[256,256]{1,0:T(8,128)(2,1)S(1)}, bf16[256,256]{1,0:T(8,128)(2,1)}, u32[]{:S(2)}) copy-start(bf16[256,256]{1,0:T(8,128)(2,1)} %param.23) | copy-start | bytes 393220
  0.6 7.1 %copy-start.14 = (f32[128]{0:T(128)S(1)}, f32[128]{0:T(128)}, u32[]{:S(2)}) copy-start(f32[128]{0:T(128)} %param.27) | copy-start | bytes 1540
  9.0 18.3 %copy-start.1 = (bf16[2048,256]{1,0:T(8,128)(2,1)S(1)}, bf16[2048,256]{1,0:T(8,128)(2,1)}, u32[]{:S(2)}) copy-start(bf16[2048,256]{1,0:T(8,128)(2,1)} %param.15) | copy-start | bytes 3145732
  26.7 2.4 copy-start.3
  26.7 2.4 copy-start.5
  29.3 70.8 %copy-start.10 = (f32[256]{0:T(256)S(1)}, f32[256]{0:T(256)}, u32[]{:S(2)}) copy-start(f32[256]{0:T(256)} %param.20) | copy-start | bytes 3076
  29.3 70.9 %copy-start.9 = (s32[3,512]{1,0:T(4,128)S(1)}, s32[3,512]{1,0:T(4,128)}, u32[]{:S(2)}) copy-start(s32[3,512]{1,0:T(4,128)} %param.17) | copy-start | bytes 18436
  92.3 46.0 %all-to-all-start.1 = ((f32[64,17,256]{2,1,0:T(8,128)}), f32[64,17,256]{2,1,0:T(8,128)S(1)}, u32[]{:S(2)}, u32[]{:S(2)}) async-start(f32[64,17,256]{2,1,0:T(8,128)} %broadcast_in_dim.9), calls=%async_computation.1 | async-start | bytes 3145728 | tf_op jit(solution)/shard_map/all_to_all | solution.py:103
  100.4 38.2 %copy-start.11 = (f32[256]{0:T(256)S(1)}, f32[256]{0:T(256)}, u32[]{:S(2)}) copy-start(f32[256]{0:T(256)} %param.21) | copy-start | bytes 3076
  138.3 20.0 %copy-start.2 = (f32[64,17,256]{2,1,0:T(8,128)}, f32[64,17,256]{2,1,0:T(8,128)S(1)}, u32[]{:S(2)}) copy-start(f32[64,17,256]{2,1,0:T(8,128)S(1)} %all-to-all-done.1) | copy-start | bytes 3342340
  157.0 1.6 copy-start.7
  157.0 2.2 copy-start.8
  159.2 1.6 copy-start.4
  159.2 2.2 copy-start.6
  164.2 63.4 %copy-start.13 = (f32[256]{0:T(256)S(1)}, f32[256]{0:T(256)}, u32[]{:S(2)}) copy-start(f32[256]{0:T(256)} %param.22) | copy-start | bytes 3076
  164.2 65.3 %copy-start.12 = (f32[256]{0:T(256)S(1)}, f32[256]{0:T(256)}, u32[]{:S(2)}) copy-start(f32[256]{0:T(256)} %param.24) | copy-start | bytes 3076
  164.2 60.2 %all-to-all-start.2 = ((f32[8,264,256]{2,1,0:T(8,128)}), f32[8,264,256]{2,1,0:T(8,128)S(1)}, u32[]{:S(2)}, u32[]{:S(2)}) async-start(f32[8,264,256]{2,1,0:T(8,128)} %pad_maximum_fusion.1), calls=%async_computation.2 | async-start | bytes 4325376 | tf_op jit(solution)/shard_map/all_to_all | solution.py:107
  232.5 26.6 %all-to-all-start.3 = ((f32[512,1,1]{2,1,0:T(1,128)}), f32[512,1,1]{2,1,0:T(1,128)S(1)}, u32[]{:S(2)}, u32[]{:S(2)}) async-start(f32[512,1,1]{2,1,0:T(1,128)} %broadcast_in_dim.11), calls=%async_computation.3 | async-start | bytes 524288 | tf_op jit(solution)/shard_map/all_to_all | solution.py:116

commit v3 on v2

--- a/solution.py
+++ b/solution.py
@@ -104,16 +104,18 @@
 
 
 def sum_over_ka(payload):
-    parts = lax.all_to_all(payload, KA_AXES, 0, 0, tiled=True)
+    parts = lax.all_to_all(payload, "core", 1, 1, tiled=True)
+    chip = jnp.sum(parts, axis=1)
+    parts = lax.all_to_all(chip, "zl", 0, 0, tiled=True)
     return jnp.sum(parts, axis=0)
 
 
-def sum_over_all(value):
+def sum_over_all(values):
     devices = 1
     for axis in ALL_AXES:
         devices *= lax.axis_size(axis)
-    copies = jnp.broadcast_to(value.reshape(1), (devices,))
-    return jnp.sum(lax.all_to_all(copies, ALL_AXES, 0, 0, tiled=True))
+    copies = jnp.broadcast_to(values[None, :], (devices, values.shape[0]))
+    return jnp.sum(lax.all_to_all(copies, ALL_AXES, 0, 0, tiled=True), axis=0)
 
 
 def local(
@@ -149,25 +151,20 @@
         features, species, live_mask, w_student, species_embed, w_charge, species_bias
     )
     charge_low = charge.astype(jnp.bfloat16)
-    phases = phase_table(positions, k_indices)
+    phases = lax.optimization_barrier(phase_table(positions, k_indices))
     factor = lax.dot_general(
         phases, masked, (((0,), (0,)), ((), ())), preferred_element_type=jnp.float32
     )
     charge_sum = jnp.dot(charge_low, phases, preferred_element_type=jnp.float32)
     rows_each = 2 * k_width // atom_groups
-    extra = jnp.concatenate(
-        [
-            charge_sum,
-            brick_counts.astype(jnp.float32),
-            jnp.zeros((atom_groups * channels - 2 * k_width - 1,), jnp.float32),
-        ]
-    ).reshape(atom_groups, 1, channels)
-    payload = jnp.concatenate([factor.reshape(atom_groups, rows_each, channels), extra], axis=1)
-    summed = sum_over_atoms(payload)
-    factor = summed[:, :rows_each].reshape(2 * k_width, channels)
-    extra = summed[:, rows_each:].reshape(-1)
-    charge_sum = extra[: 2 * k_width]
-    live_total = extra[2 * k_width]
+    lanes = 128
+    factor_part = factor.reshape(atom_groups, rows_each * channels // lanes, lanes)
+    charge_part = jnp.pad(
+        charge_sum.reshape(atom_groups, 1, rows_each), ((0, 0), (0, 0), (0, lanes - rows_each))
+    )
+    summed = sum_over_atoms(jnp.concatenate([factor_part, charge_part], axis=1))
+    factor = summed[:, :-1].reshape(2 * k_width, channels)
+    charge_sum = summed[:, -1, :rows_each].reshape(-1)
     k_vectors, k_square = k_geometry(k_indices)
     kernel = teacher_kernel(k_square, smearing, inv_root)
     weighted = (jnp.concatenate([kernel, kernel], axis=0) * factor).astype(jnp.bfloat16)
@@ -196,6 +193,8 @@
     )
     side = side.reshape(8, ka_groups, share_rows).transpose(1, 0, 2)
     packed = jnp.concatenate([potential.reshape(ka_groups, share_rows, channels), side], axis=1)
+    z_lo = lax.axis_size("zl")
+    packed = packed.reshape(z_lo, ka_groups // z_lo, share_rows + 8, channels)
     own = sum_over_ka(packed)
     ka_index = lax.axis_index(KA_AXES)
     row_start = ka_index * share_rows
@@ -215,8 +214,8 @@
         w_mix,
         w_read,
     )
-    loss_sum = sum_over_all(jnp.sum(misfit))
-    return (teacher_features, teacher_out.T, forces.T, student_energy, loss_sum / live_total)
+    totals = sum_over_all(jnp.stack([jnp.sum(misfit), jnp.sum(own_rows(live_mask))]))
+    return (teacher_features, teacher_out.T, forces.T, student_energy, totals[0] / totals[1])
 
 
 def solution(mesh):

time: 264 us -> 225 us (0.85)
  blocking collectives: 61.6 us -> 92.7 us
  other arithmetic: 61.6 us -> 30.6 us
  waiting for transfers between devices: 84.3 us -> 55.1 us
  starting transfers between devices: 26.7 us -> 11.8 us
  matrix products: 15.5 us -> 18.7 us
    all_to_all x2 -> x1, waiting for transfers between devices: 65.4 us -> 25.2 us  [sum_over_ka(): parts = lax.all_to_all(chip, 'zl', 0, 0, tiled=True)]
    all_to_all x0 -> x2, blocking collectives: none -> 37 us  [the longest x1 27.5 us: sum_over_all(): return jnp.sum(lax.all_to_all(copies, ALL_AXES, 0, 0, tiled=True), axis=0)]
    slice x1 -> x0, other arithmetic: 17.6 us -> none  [local(): cosines = phases[:, :k_width].astype(jnp.float32)]
    sub x1 -> x0, other arithmetic: 17.1 us -> none  [local(): sines * contracted[:, :k_width] - cosines * contracted[:, k_width:]]
    all_to_all x2 -> x1, starting transfers between devices: 19.6 us -> 4.34 us  [sum_over_ka(): parts = lax.all_to_all(chip, 'zl', 0, 0, tiled=True)]
    all_to_all x1, waiting for transfers between devices: 18.9 us -> 29.9 us  [sum_over_atoms(): return lax.all_to_all(spread, ATOM_AXES, 0, 0, tiled=True)]
    all_to_all x1, blocking collectives: 61.6 us -> 55.6 us  [sum_over_atoms(): parts = lax.all_to_all(payload, ATOM_AXES, 0, 0, tiled=True)]
    another operation x4 -> x5, other arithmetic: 19 us -> 19.1 us
  transfers between devices with their start and end apart: 3 -> 2, of which waited for: 3 -> 2; matrix products, arithmetic and copies ran while one was open for 8% -> 2% of each run, Pallas kernels for 0% -> 0%
where the time goes in v3:
time: 225 us; the launch traced here: 224 us
  blocking collectives  92.7 us (41%)
  waiting for transfers between devices  55.1 us (24%)
  other arithmetic  30.6 us (14%)
  matrix products  18.7 us (8%)
  starting transfers between devices  11.8 us (5%)
  local copies, waits for them, and re-layouts  10 us (4%)
  between operations  4.92 us (2%)
    all_to_all x1, blocking collectives, sum_over_atoms(): parts = lax.all_to_all(payload, ATOM_AXES, 0, 0, tiled=True)  55.6 us
    all_to_all x1, waiting for transfers between devices, sum_over_atoms(): return lax.all_to_all(spread, ATOM_AXES, 0, 0, tiled=True)  29.9 us
    all_to_all x1, blocking collectives, sum_over_all(): return jnp.sum(lax.all_to_all(copies, ALL_AXES, 0, 0, tiled=True), axis=0)  27.5 us
    all_to_all x1, waiting for transfers between devices, sum_over_ka(): parts = lax.all_to_all(chip, 'zl', 0, 0, tiled=True)  25.2 us
    another operation x4, other arithmetic  17.7 us
    all_to_all x1, blocking collectives, sum_over_ka(): parts = lax.all_to_all(payload, 'core', 1, 1, tiled=True)  9.59 us
    all_to_all x1, starting transfers between devices, sum_over_atoms(): return lax.all_to_all(spread, ATOM_AXES, 0, 0, tiled=True)  7.49 us
  transfers between devices with their start and end apart: 2, of which 2 were waited for; matrix products, arithmetic and copies ran while one was open for 2% of the time, Pallas kernels for 0%

profile of v3, /device:TPU:1, one launch (start us, length us, event | category | flops | bytes accessed | tf_op | source)
XLA Modules:
  0.0 223.9 jit_solution(17106036323045984366)
XLA Ops:
  2.3 17.6 %cosine_convert_fusion = (bf16[2048,512]{1,0:T(8,128)(2,1)S(1)}, bf16[2048,512]{1,0:T(8,128)(2,1)S(1)}) fusion(f32[512]{0:T(512)S(1)} %bitcast.112, f32[2048]{0:T(1024)S(1)} %bitcast.106, f32[512]{0:T(512)S(1)} %bitcast.113, f32[2048]{0:T(1024)S(1)} %bitcast.107, f32[512]{0:T(512)S(1)} %bitcast.111, f32[2048]{0:T(1024)S(1)} %bitcast.105), kind=kLoop, calls=%fused_computation.6 | loop fusion | flops 8388608 | bytes 4225024 | tf_op jit(solution)/shard_map/convert.10
  22.6 1.0 convolution_add_fusion
  23.5 1.2 fusion.8
  26.7 3.8 %fusion.15 = f32[1024,256]{1,0:T(8,128)S(1)} fusion(bf16[2048,1024]{1,0:T(8,128)(2,1)} %copy-done.1, bf16[2048,256]{1,0:T(8,128)(2,1)S(1)} %copy-done.4, bf16[2048]{0:T(1024)(128)(2,1)S(1)} %get-tuple-element.46), kind=kOutput, calls=%fused_computation.31 | convolution fusion | flops 1074266112 | bytes 6295552 | tf_op jit(solution)/shard_map/dot_general | solution.py:155
  30.8 55.6 %all_to_all.26 = f32[64,33,128]{2,1,0:T(8,128)S(1)} all-to-all(f32[64,33,128]{2,1,0:T(8,128)S(1)} %pad_maximum_fusion.2), channel_id=1, replica_groups=mesh['y'=8,'x'=4,'zh'=2,'zl'=4,'core'=2] {'y','x','zh'}, dimensions={0} | all-to-all | bytes 2162688 | tf_op jit(solution)/shard_map/all_to_all | solution.py:100
  86.5 1.2 broadcast_in_dim.6
  87.6 7.5 %all-to-all-start.1 = ((f32[64,33,128]{2,1,0:T(8,128)}), f32[64,33,128]{2,1,0:T(8,128)S(1)}, u32[]{:S(2)}, u32[]{:S(2)}) async-start(f32[64,33,128]{2,1,0:T(8,128)} %broadcast_in_dim.6), calls=%async_computation.1 | async-start | bytes 2621440 | tf_op jit(solution)/shard_map/all_to_all | solution.py:103
  96.1 1.1 pad_maximum_fusion.3
  97.1 2.3 %concatenate.24 = f32[64,32,128]{2,1,0:T(8,128)} reshape(f32[1024,256]{1,0:T(8,128)} %pad_maximum_fusion.3) | data formatting | bytes 2097152 | tf_op jit(solution)/shard_map/concatenate | solution.py:170
  100.0 29.9 %all-to-all-done.1 = f32[64,33,128]{2,1,0:T(8,128)S(1)} async-done(((f32[64,33,128]{2,1,0:T(8,128)}), f32[64,33,128]{2,1,0:T(8,128)S(1)}, u32[]{:S(2)}, u32[]{:S(2)}) %all-to-all-start.1) | async-done | bytes 1081376 | tf_op jit(solution)/shard_map/all_to_all | solution.py:103
  131.3 2.4 %multiply_convert_fusion.3 = (bf16[64,32,128]{2,1,0:T(8,128)(2,1)S(1)}, f32[64,32,128]{2,1,0:T(8,128)}) fusion(f32[64,32,128]{2,1,0:T(8,128)} %concatenate.24, f32[64,33,128]{2,1,0:T(8,128)S(1)} %all-to-all-done.1), kind=kLoop, calls=%fused_computation.22 | loop fusion | flops 524288 | bytes 3670016 | tf_op jit(solution)/shard_map/convert_element_type | solution.py:170
  133.7 1.5 reshape.338
  135.3 2.1 fusion.3
  137.5 1.4 fusion.5
  138.9 1.4 fusion.2
  140.6 3.6 %fusion.73 = f32[8,256,256]{2,1,0:T(8,128)S(1)} fusion(bf16[8,256,1024]{2,1,0:T(8,128)(2,1)} %bitcast.101, bf16[1024,256,1]{1,0,2:T(8,128)(2,1)S(1)} %reshape.347), kind=kOutput, calls=%fused_computation.118 | convolution fusion | flops 1073741824 | bytes 6815744 | tf_op jit(solution)/shard_map/dot_general | solution.py:171
  144.3 1.2 fusion.24
  145.9 9.6 %all_to_all.27 = f32[4,2,264,256]{3,2,0,1:T(8,128)S(1)} all-to-all(f32[4,2,264,256]{3,2,0,1:T(8,128)S(1)} %copy.27), channel_id=1, replica_groups=mesh['y'=8,'x'=4,'zh'=2,'zl'=4,'core'=2] {'core'}, dimensions={1} | all-to-all | bytes 4325376 | tf_op jit(solution)/shard_map/all_to_all | solution.py:107
  155.5 1.2 reduce_sum.73
  156.8 4.3 %all-to-all-start.3 = ((f32[4,264,256]{2,1,0:T(8,128)}), f32[4,264,256]{2,1,0:T(8,128)S(1)}, u32[]{:S(2)}, u32[]{:S(2)}) async-start(f32[4,264,256]{2,1,0:T(8,128)} %reduce_sum.73), calls=%async_computation.3 | async-start | bytes 2162688 | tf_op jit(solution)/shard_map/all_to_all | solution.py:109
  161.9 25.2 %all-to-all-done.3 = f32[4,264,256]{2,1,0:T(8,128)S(1)} async-done(((f32[4,264,256]{2,1,0:T(8,128)}), f32[4,264,256]{2,1,0:T(8,128)S(1)}, u32[]{:S(2)}, u32[]{:S(2)}) %all-to-all-start.3) | async-done | bytes 1081376 | tf_op jit(solution)/shard_map/all_to_all | solution.py:109
  189.1 2.1 multiply_reduce_fusion.2
  191.2 1.4 pad_maximum_fusion.5
  192.8 27.5 %all_to_all.28 = f32[512,1,2]{2,1,0:T(1,128)S(1)} all-to-all(f32[512,1,2]{2,1,0:T(1,128)S(1)} %broadcast_in_dim.8), channel_id=1, replica_groups=mesh['y'=8,'x'=4,'zh'=2,'zl'=4,'core'=2] {'y','x','zh','zl','core'}, dimensions={0} | all-to-all | bytes 8192 | tf_op jit(solution)/shard_map/all_to_all | solution.py:118
  (77 shorter events, 12.8 us)
Async XLA Ops:
  0.6 187.3 %copy-start = (bf16[256,256]{1,0:T(8,128)(2,1)S(1)}, bf16[256,256]{1,0:T(8,128)(2,1)}, u32[]{:S(2)}) copy-start(bf16[256,256]{1,0:T(8,128)(2,1)} %param.23) | copy-start | bytes 393220
  19.9 1.4 copy-start.4
  19.9 1.4 copy-start.5
  20.0 1.9 copy-start.7
  20.0 1.9 copy-start.15
  20.0 2.6 %copy-start.10 = (f32[8,128]{1,0:T(8,128)S(1)}, f32[8,128]{1,0:T(8,128)}, u32[]{:S(2)}) copy-start(f32[8,128]{1,0:T(8,128)} %param.26) | copy-start | bytes 12292
  20.6 4.7 %copy-start.1 = (bf16[2048,1024]{1,0:T(8,128)(2,1)}, bf16[2048,1024]{1,0:T(8,128)(2,1)S(1)}, u32[]{:S(2)}) copy-start(bf16[2048,1024]{1,0:T(8,128)(2,1)S(1)} %pad_maximum_fusion) | copy-start | bytes 12582916
  20.7 2.9 %copy-start.16 = (f32[128]{0:T(128)S(1)}, f32[128]{0:T(128)}, u32[]{:S(2)}) copy-start(f32[128]{0:T(128)} %param.27) | copy-start | bytes 1540
  30.7 65.1 %copy-start.11 = (f32[256]{0:T(256)S(1)}, f32[256]{0:T(256)}, u32[]{:S(2)}) copy-start(f32[256]{0:T(256)} %param.20) | copy-start | bytes 3076
  30.7 65.1 %copy-start.6 = (s32[3,512]{1,0:T(4,128)S(1)}, s32[3,512]{1,0:T(4,128)}, u32[]{:S(2)}) copy-start(s32[3,512]{1,0:T(4,128)} %param.17) | copy-start | bytes 18436
  87.6 42.3 %all-to-all-start.1 = ((f32[64,33,128]{2,1,0:T(8,128)}), f32[64,33,128]{2,1,0:T(8,128)S(1)}, u32[]{:S(2)}, u32[]{:S(2)}) async-start(f32[64,33,128]{2,1,0:T(8,128)} %broadcast_in_dim.6), calls=%async_computation.1 | async-start | bytes 2621440 | tf_op jit(solution)/shard_map/all_to_all | solution.py:103
  135.3 2.2 copy-start.2
  138.9 1.6 copy-start.9
  138.9 1.6 copy-start.8
  140.5 3.8 %copy-start.3 = (bf16[2048,1024]{1,0:T(8,128)(2,1)S(1)}, bf16[2048,1024]{1,0:T(8,128)(2,1)}, u32[]{:S(2)}) copy-start(bf16[2048,1024]{1,0:T(8,128)(2,1)} %copy-done.1) | copy-start | bytes 12582916
  140.6 4.9 %copy-start.13 = (f32[8]{0:T(128)S(1)}, f32[8]{0:T(128)}, u32[]{:S(2)}) copy-start(f32[8]{0:T(128)} %pad.11.clone) | copy-start | bytes 100
  155.5 32.4 %copy-start.14 = (f32[256]{0:T(256)S(1)}, f32[256]{0:T(256)}, u32[]{:S(2)}) copy-start(f32[256]{0:T(256)} %param.22) | copy-start | bytes 3076
  155.5 33.3 %copy-start.12 = (f32[256]{0:T(256)S(1)}, f32[256]{0:T(256)}, u32[]{:S(2)}) copy-start(f32[256]{0:T(256)} %param.24) | copy-start | bytes 3076
  156.8 30.3 %all-to-all-start.3 = ((f32[4,264,256]{2,1,0:T(8,128)}), f32[4,264,256]{2,1,0:T(8,128)S(1)}, u32[]{:S(2)}, u32[]{:S(2)}) async-start(f32[4,264,256]{2,1,0:T(8,128)} %reduce_sum.73), calls=%async_computation.3 | async-start | bytes 2162688 | tf_op jit(solution)/shard_map/all_to_all | solution.py:109

commit v4 on v3

--- a/solution.py
+++ b/solution.py
@@ -157,14 +157,13 @@
     )
     charge_sum = jnp.dot(charge_low, phases, preferred_element_type=jnp.float32)
     rows_each = 2 * k_width // atom_groups
-    lanes = 128
-    factor_part = factor.reshape(atom_groups, rows_each * channels // lanes, lanes)
-    charge_part = jnp.pad(
-        charge_sum.reshape(atom_groups, 1, rows_each), ((0, 0), (0, 0), (0, lanes - rows_each))
-    )
-    summed = sum_over_atoms(jnp.concatenate([factor_part, charge_part], axis=1))
-    factor = summed[:, :-1].reshape(2 * k_width, channels)
-    charge_sum = summed[:, -1, :rows_each].reshape(-1)
+    flat = rows_each * channels
+    payload = jnp.concatenate(
+        [factor.reshape(atom_groups, flat), charge_sum.reshape(atom_groups, rows_each)], axis=1
+    )
+    summed = sum_over_atoms(payload)
+    factor = summed[:, :flat].reshape(2 * k_width, channels)
+    charge_sum = summed[:, flat:].reshape(-1)
     k_vectors, k_square = k_geometry(k_indices)
     kernel = teacher_kernel(k_square, smearing, inv_root)
     weighted = (jnp.concatenate([kernel, kernel], axis=0) * factor).astype(jnp.bfloat16)

time: 225 us -> 214 us (0.951)
  blocking collectives: 92.7 us -> 87 us
  other arithmetic: 30.6 us -> 28.1 us
    all_to_all x1, blocking collectives: 55.6 us -> 50.3 us  [sum_over_atoms(): parts = lax.all_to_all(payload, ATOM_AXES, 0, 0, tiled=True)]
  transfers between devices with their start and end apart: 2 -> 2, of which waited for: 2 -> 2; matrix products, arithmetic and copies ran while one was open for 2% -> 1% of each run, Pallas kernels for 0% -> 0%
where the time goes in v4:
time: 214 us
  blocking collectives  87 us (41%)
  waiting for transfers between devices  53.8 us (25%)
  other arithmetic  28.1 us (13%)
  matrix products  17.9 us (8%)
  starting transfers between devices  12.3 us (6%)
  local copies, waits for them, and re-layouts  9.83 us (5%)
  between operations  4.87 us (2%)
    all_to_all x1, blocking collectives, sum_over_atoms(): parts = lax.all_to_all(payload, ATOM_AXES, 0, 0, tiled=True)  50.3 us
    all_to_all x1, waiting for transfers between devices, sum_over_atoms(): return lax.all_to_all(spread, ATOM_AXES, 0, 0, tiled=True)  27.9 us
    all_to_all x1, blocking collectives, sum_over_all(): return jnp.sum(lax.all_to_all(copies, ALL_AXES, 0, 0, tiled=True), axis=0)  27.5 us
    all_to_all x1, waiting for transfers between devices, sum_over_ka(): parts = lax.all_to_all(chip, 'zl', 0, 0, tiled=True)  25.9 us
    another operation x4, other arithmetic  17.7 us
    all_to_all x1, blocking collectives, sum_over_ka(): parts = lax.all_to_all(payload, 'core', 1, 1, tiled=True)  9.28 us
    all_to_all x1, starting transfers between devices, sum_over_atoms(): return lax.all_to_all(spread, ATOM_AXES, 0, 0, tiled=True)  8.1 us
  transfers between devices with their start and end apart: 2, of which 2 were waited for; matrix products, arithmetic and copies ran while one was open for 1% of the time, Pallas kernels for 0%

profile of v4, /device:TPU:1, one launch (start us, length us, event | category | flops | bytes accessed | tf_op | source)
XLA Modules:
  0.0 213.8 jit_solution(9168053708596755343)
XLA Ops:
  2.3 17.6 %cosine_convert_fusion = (bf16[2048,512]{1,0:T(8,128)(2,1)S(1)}, bf16[2048,512]{1,0:T(8,128)(2,1)S(1)}) fusion(f32[512]{0:T(512)S(1)} %bitcast.115, f32[2048]{0:T(1024)S(1)} %bitcast.109, f32[512]{0:T(512)S(1)} %bitcast.116, f32[2048]{0:T(1024)S(1)} %bitcast.110, f32[512]{0:T(512)S(1)} %bitcast.114, f32[2048]{0:T(1024)S(1)} %bitcast.108), kind=kLoop, calls=%fused_computation.6 | loop fusion | flops 8388608 | bytes 4225024 | tf_op jit(solution)/shard_map/convert.10
  22.6 1.0 convolution_add_fusion
  23.5 1.2 fusion.8
  25.5 3.8 %fusion.15 = f32[1024,256]{1,0:T(8,128)S(1)} fusion(bf16[2048,1024]{1,0:T(8,128)(2,1)} %copy-done.1, bf16[2048,256]{1,0:T(8,128)(2,1)S(1)} %copy-done.4, bf16[2048]{0:T(1024)(128)(2,1)S(1)} %get-tuple-element.46), kind=kOutput, calls=%fused_computation.32 | convolution fusion | flops 1074266112 | bytes 6295552 | tf_op jit(solution)/shard_map/dot_general | solution.py:155
  30.4 50.3 %all_to_all.34 = f32[64,1,4112]{2,1,0:T(1,128)S(1)} all-to-all(f32[64,1,4112]{2,1,0:T(1,128)S(1)} %all_to_all.22), channel_id=1, replica_groups=mesh['y'=8,'x'=4,'zh'=2,'zl'=4,'core'=2] {'y','x','zh'}, dimensions={0} | all-to-all | bytes 2105344 | tf_op jit(solution)/shard_map/all_to_all | solution.py:100
  81.4 1.6 broadcast_in_dim.6
  82.9 8.1 %all-to-all-start.1 = ((f32[64,1,4112]{2,1,0:T(1,128)}), f32[64,1,4112]{2,1,0:T(1,128)}, u32[]{:S(2)}, u32[]{:S(2)}) async-start(f32[64,1,4112]{2,1,0:T(1,128)} %broadcast_in_dim.6), calls=%async_computation.1 | async-start | bytes 2162688 | tf_op jit(solution)/shard_map/all_to_all | solution.py:103
  92.1 1.2 concatenate.24
  93.4 27.9 %all-to-all-done.1 = f32[64,1,4112]{2,1,0:T(1,128)} async-done(((f32[64,1,4112]{2,1,0:T(1,128)}), f32[64,1,4112]{2,1,0:T(1,128)}, u32[]{:S(2)}, u32[]{:S(2)}) %all-to-all-start.1) | async-done | bytes 1052704 | tf_op jit(solution)/shard_map/all_to_all | solution.py:103
  121.3 1.3 copy.29
  122.8 2.4 %multiply_convert_fusion.3 = (bf16[64,4096]{1,0:T(8,128)(2,1)S(1)}, f32[64,4096]{1,0:T(8,128)}) fusion(f32[64,4096]{1,0:T(8,128)} %concatenate.24, f32[64,4112]{1,0:T(8,128)S(1)} %bitcast.106), kind=kLoop, calls=%fused_computation.23 | loop fusion | flops 524288 | bytes 3670016 | tf_op jit(solution)/shard_map/convert_element_type | solution.py:169
  125.2 1.4 reshape.346
  126.6 1.3 fusion.3
  128.8 1.4 fusion.5
  130.2 1.4 fusion.2
  131.9 3.6 %fusion.74 = f32[8,256,256]{2,1,0:T(8,128)S(1)} fusion(bf16[8,256,1024]{2,1,0:T(8,128)(2,1)} %bitcast.103, bf16[1024,256,1]{1,0,2:T(8,128)(2,1)S(1)} %reshape.355), kind=kOutput, calls=%fused_computation.118 | convolution fusion | flops 1073741824 | bytes 6815744 | tf_op jit(solution)/shard_map/dot_general | solution.py:170
  135.5 1.2 fusion.24
  137.2 9.3 %all_to_all.35 = f32[4,2,264,256]{3,2,0,1:T(8,128)S(1)} all-to-all(f32[4,2,264,256]{3,2,0,1:T(8,128)S(1)} %copy.22), channel_id=1, replica_groups=mesh['y'=8,'x'=4,'zh'=2,'zl'=4,'core'=2] {'core'}, dimensions={1} | all-to-all | bytes 4325376 | tf_op jit(solution)/shard_map/all_to_all | solution.py:107
  146.5 1.2 reduce_sum.73
  147.7 4.2 %all-to-all-start.3 = ((f32[4,264,256]{2,1,0:T(8,128)}), f32[4,264,256]{2,1,0:T(8,128)S(1)}, u32[]{:S(2)}, u32[]{:S(2)}) async-start(f32[4,264,256]{2,1,0:T(8,128)} %reduce_sum.73), calls=%async_computation.3 | async-start | bytes 2162688 | tf_op jit(solution)/shard_map/all_to_all | solution.py:109
  152.0 25.9 %all-to-all-done.3 = f32[4,264,256]{2,1,0:T(8,128)S(1)} async-done(((f32[4,264,256]{2,1,0:T(8,128)}), f32[4,264,256]{2,1,0:T(8,128)S(1)}, u32[]{:S(2)}, u32[]{:S(2)}) %all-to-all-start.3) | async-done | bytes 1081376 | tf_op jit(solution)/shard_map/all_to_all | solution.py:109
  179.9 1.3 multiply_reduce_fusion.2
  181.2 1.4 pad_maximum_fusion.5
  182.7 27.5 %all_to_all.36 = f32[512,1,2]{2,1,0:T(1,128)S(1)} all-to-all(f32[512,1,2]{2,1,0:T(1,128)S(1)} %broadcast_in_dim.8), channel_id=1, replica_groups=mesh['y'=8,'x'=4,'zh'=2,'zl'=4,'core'=2] {'y','x','zh','zl','core'}, dimensions={0} | all-to-all | bytes 8192 | tf_op jit(solution)/shard_map/all_to_all | solution.py:118
  (74 shorter events, 11.5 us)
Async XLA Ops:
  0.6 178.1 %copy-start = (bf16[256,256]{1,0:T(8,128)(2,1)S(1)}, bf16[256,256]{1,0:T(8,128)(2,1)}, u32[]{:S(2)}) copy-start(bf16[256,256]{1,0:T(8,128)(2,1)} %param.23) | copy-start | bytes 393220
  19.9 1.4 copy-start.4
  19.9 1.4 copy-start.5
  20.0 1.9 copy-start.7
  20.0 1.9 copy-start.13
  20.0 2.6 %copy-start.8 = (f32[8,128]{1,0:T(8,128)S(1)}, f32[8,128]{1,0:T(8,128)}, u32[]{:S(2)}) copy-start(f32[8,128]{1,0:T(8,128)} %param.26) | copy-start | bytes 12292
  20.6 4.1 %copy-start.1 = (bf16[2048,1024]{1,0:T(8,128)(2,1)}, bf16[2048,1024]{1,0:T(8,128)(2,1)S(1)}, u32[]{:S(2)}) copy-start(bf16[2048,1024]{1,0:T(8,128)(2,1)S(1)} %pad_maximum_fusion) | copy-start | bytes 12582916
  20.7 2.9 %copy-start.14 = (f32[128]{0:T(128)S(1)}, f32[128]{0:T(128)}, u32[]{:S(2)}) copy-start(f32[128]{0:T(128)} %param.27) | copy-start | bytes 1540
  29.6 62.1 %copy-start.9 = (f32[256]{0:T(256)S(1)}, f32[256]{0:T(256)}, u32[]{:S(2)}) copy-start(f32[256]{0:T(256)} %param.20) | copy-start | bytes 3076
  29.7 62.1 %copy-start.6 = (s32[3,512]{1,0:T(4,128)S(1)}, s32[3,512]{1,0:T(4,128)}, u32[]{:S(2)}) copy-start(s32[3,512]{1,0:T(4,128)} %param.17) | copy-start | bytes 18436
  82.9 38.4 %all-to-all-start.1 = ((f32[64,1,4112]{2,1,0:T(1,128)}), f32[64,1,4112]{2,1,0:T(1,128)}, u32[]{:S(2)}, u32[]{:S(2)}) async-start(f32[64,1,4112]{2,1,0:T(1,128)} %broadcast_in_dim.6), calls=%async_computation.1 | async-start | bytes 2162688 | tf_op jit(solution)/shard_map/all_to_all | solution.py:103
  93.3 33.3 %copy-start.10 = (f32[256]{0:T(256)S(1)}, f32[256]{0:T(256)}, u32[]{:S(2)}) copy-start(f32[256]{0:T(256)} %param.21) | copy-start | bytes 3076
  126.6 2.2 %copy-start.2 = (bf16[2048,1024]{1,0:T(8,128)(2,1)S(1)}, bf16[2048,1024]{1,0:T(8,128)(2,1)}, u32[]{:S(2)}) copy-start(bf16[2048,1024]{1,0:T(8,128)(2,1)} %copy-done.1) | copy-start | bytes 12582916
  131.8 3.7 %copy-start.3 = (bf16[2048,1024]{1,0:T(8,128)(2,1)S(1)}, bf16[2048,1024]{1,0:T(8,128)(2,1)}, u32[]{:S(2)}) copy-start(bf16[2048,1024]{1,0:T(8,128)(2,1)} %copy-done.1) | copy-start | bytes 12582916
  146.5 32.2 %copy-start.12 = (f32[256]{0:T(256)S(1)}, f32[256]{0:T(256)}, u32[]{:S(2)}) copy-start(f32[256]{0:T(256)} %param.22) | copy-start | bytes 3076
  146.5 33.2 %copy-start.11 = (f32[256]{0:T(256)S(1)}, f32[256]{0:T(256)}, u32[]{:S(2)}) copy-start(f32[256]{0:T(256)} %param.24) | copy-start | bytes 3076
  147.7 30.1 %all-to-all-start.3 = ((f32[4,264,256]{2,1,0:T(8,128)}), f32[4,264,256]{2,1,0:T(8,128)S(1)}, u32[]{:S(2)}, u32[]{:S(2)}) async-start(f32[4,264,256]{2,1,0:T(8,128)} %reduce_sum.73), calls=%async_computation.3 | async-start | bytes 2162688 | tf_op jit(solution)/shard_map/all_to_all | solution.py:109

commit v5 on v4

--- a/solution.py
+++ b/solution.py
@@ -111,11 +111,13 @@
 
 
 def sum_over_all(values):
-    devices = 1
-    for axis in ALL_AXES:
-        devices *= lax.axis_size(axis)
-    copies = jnp.broadcast_to(values[None, :], (devices, values.shape[0]))
-    return jnp.sum(lax.all_to_all(copies, ALL_AXES, 0, 0, tiled=True), axis=0)
+    pair = jnp.broadcast_to(values[None, :], (lax.axis_size("core"), values.shape[0]))
+    chip = jnp.sum(lax.all_to_all(pair, "core", 0, 0, tiled=True), axis=0)
+    chips = 1
+    for axis in ALL_AXES[:-1]:
+        chips *= lax.axis_size(axis)
+    copies = jnp.broadcast_to(chip[None, :], (chips, values.shape[0]))
+    return jnp.sum(lax.all_to_all(copies, ALL_AXES[:-1], 0, 0, tiled=True), axis=0)
 
 
 def local(

time: 214 us -> 213 us (level)
    all_to_all x1 -> x2, blocking collectives: 27.5 us -> 26.7 us  [the longest x1 22 us: sum_over_all(): lax.all_to_all(copies, ALL_AXES[:-1], 0, 0, tiled=True)]
where the time goes in v5:
time: 213 us
  blocking collectives  86.3 us (41%)
  waiting for transfers between devices  53.9 us (25%)
  other arithmetic  27.7 us (13%)
  matrix products  17.9 us (8%)
  starting transfers between devices  12.3 us (6%)
  local copies, waits for them, and re-layouts  9.74 us (5%)
  between operations  4.8 us (2%)
    all_to_all x1, blocking collectives, sum_over_atoms(): parts = lax.all_to_all(payload, ATOM_AXES, 0, 0, tiled=True)  50.3 us
    all_to_all x1, waiting for transfers between devices, sum_over_atoms(): return lax.all_to_all(spread, ATOM_AXES, 0, 0, tiled=True)  28 us
    all_to_all x1, waiting for transfers between devices, sum_over_ka(): parts = lax.all_to_all(chip, 'zl', 0, 0, tiled=True)  25.9 us
    all_to_all x1, blocking collectives, sum_over_all(): lax.all_to_all(copies, ALL_AXES[:-1], 0, 0, tiled=True)  22 us
    another operation x4, other arithmetic  17.7 us
    all_to_all x1, blocking collectives, sum_over_ka(): parts = lax.all_to_all(payload, 'core', 1, 1, tiled=True)  9.28 us
    all_to_all x1, starting transfers between devices, sum_over_atoms(): return lax.all_to_all(spread, ATOM_AXES, 0, 0, tiled=True)  8.1 us
    all_to_all x1, blocking collectives, sum_over_all(): chip = jnp.sum(lax.all_to_all(pair, 'core', 0, 0, tiled=True), axis=0)  4.75 us
  transfers between devices with their start and end apart: 2, of which 2 were waited for; matrix products, arithmetic and copies ran while one was open for 1% of the time, Pallas kernels for 0%

profile of v5, /device:TPU:1, one launch (start us, length us, event | category | flops | bytes accessed | tf_op | source)
XLA Modules:
  0.0 212.5 jit_solution(5206570715401865724)
XLA Ops:
  2.3 17.6 %cosine_convert_fusion = (bf16[2048,512]{1,0:T(8,128)(2,1)S(1)}, bf16[2048,512]{1,0:T(8,128)(2,1)S(1)}) fusion(f32[512]{0:T(512)S(1)} %bitcast.116, f32[2048]{0:T(1024)S(1)} %bitcast.110, f32[512]{0:T(512)S(1)} %bitcast.117, f32[2048]{0:T(1024)S(1)} %bitcast.111, f32[512]{0:T(512)S(1)} %bitcast.115, f32[2048]{0:T(1024)S(1)} %bitcast.109), kind=kLoop, calls=%fused_computation.6 | loop fusion | flops 8388608 | bytes 4225024 | tf_op jit(solution)/shard_map/convert.10
  23.5 1.2 fusion.8
  25.5 3.8 %fusion.15 = f32[1024,256]{1,0:T(8,128)S(1)} fusion(bf16[2048,1024]{1,0:T(8,128)(2,1)} %copy-done.1, bf16[2048,256]{1,0:T(8,128)(2,1)S(1)} %copy-done.4, bf16[2048]{0:T(1024)(128)(2,1)S(1)} %get-tuple-element.46), kind=kOutput, calls=%fused_computation.32 | convolution fusion | flops 1074266112 | bytes 6295552 | tf_op jit(solution)/shard_map/dot_general | solution.py:157
  30.4 50.3 %all_to_all.40 = f32[64,1,4112]{2,1,0:T(1,128)S(1)} all-to-all(f32[64,1,4112]{2,1,0:T(1,128)S(1)} %all_to_all.26), channel_id=1, replica_groups=mesh['y'=8,'x'=4,'zh'=2,'zl'=4,'core'=2] {'y','x','zh'}, dimensions={0} | all-to-all | bytes 2105344 | tf_op jit(solution)/shard_map/all_to_all | solution.py:100
  81.4 1.6 broadcast_in_dim.8
  82.9 8.1 %all-to-all-start.1 = ((f32[64,1,4112]{2,1,0:T(1,128)}), f32[64,1,4112]{2,1,0:T(1,128)}, u32[]{:S(2)}, u32[]{:S(2)}) async-start(f32[64,1,4112]{2,1,0:T(1,128)} %broadcast_in_dim.8), calls=%async_computation.1 | async-start | bytes 2162688 | tf_op jit(solution)/shard_map/all_to_all | solution.py:103
  92.1 1.2 concatenate.24
  93.3 28.0 %all-to-all-done.1 = f32[64,1,4112]{2,1,0:T(1,128)} async-done(((f32[64,1,4112]{2,1,0:T(1,128)}), f32[64,1,4112]{2,1,0:T(1,128)}, u32[]{:S(2)}, u32[]{:S(2)}) %all-to-all-start.1) | async-done | bytes 1052704 | tf_op jit(solution)/shard_map/all_to_all | solution.py:103
  121.3 1.3 copy.30
  122.8 2.4 %multiply_convert_fusion.3 = (bf16[64,4096]{1,0:T(8,128)(2,1)S(1)}, f32[64,4096]{1,0:T(8,128)}) fusion(f32[64,4096]{1,0:T(8,128)} %concatenate.24, f32[64,4112]{1,0:T(8,128)S(1)} %bitcast.107), kind=kLoop, calls=%fused_computation.23 | loop fusion | flops 524288 | bytes 3670016 | tf_op jit(solution)/shard_map/convert_element_type | solution.py:171
  125.1 1.4 reshape.352
  126.6 1.3 fusion.3
  128.7 1.4 fusion.5
  130.1 1.4 fusion.2
  131.8 3.6 %fusion.74 = f32[8,256,256]{2,1,0:T(8,128)S(1)} fusion(bf16[8,256,1024]{2,1,0:T(8,128)(2,1)} %bitcast.104, bf16[1024,256,1]{1,0,2:T(8,128)(2,1)S(1)} %reshape.361), kind=kOutput, calls=%fused_computation.118 | convolution fusion | flops 1073741824 | bytes 6815744 | tf_op jit(solution)/shard_map/dot_general | solution.py:172
  135.5 1.2 fusion.24
  137.2 9.3 %all_to_all.41 = f32[4,2,264,256]{3,2,0,1:T(8,128)S(1)} all-to-all(f32[4,2,264,256]{3,2,0,1:T(8,128)S(1)} %copy.22), channel_id=1, replica_groups=mesh['y'=8,'x'=4,'zh'=2,'zl'=4,'core'=2] {'core'}, dimensions={1} | all-to-all | bytes 4325376 | tf_op jit(solution)/shard_map/all_to_all | solution.py:107
  146.5 1.2 reduce_sum.82
  147.7 4.2 %all-to-all-start.3 = ((f32[4,264,256]{2,1,0:T(8,128)}), f32[4,264,256]{2,1,0:T(8,128)S(1)}, u32[]{:S(2)}, u32[]{:S(2)}) async-start(f32[4,264,256]{2,1,0:T(8,128)} %reduce_sum.82), calls=%async_computation.3 | async-start | bytes 2162688 | tf_op jit(solution)/shard_map/all_to_all | solution.py:109
  151.9 25.9 %all-to-all-done.3 = f32[4,264,256]{2,1,0:T(8,128)S(1)} async-done(((f32[4,264,256]{2,1,0:T(8,128)}), f32[4,264,256]{2,1,0:T(8,128)S(1)}, u32[]{:S(2)}, u32[]{:S(2)}) %all-to-all-start.3) | async-done | bytes 1081376 | tf_op jit(solution)/shard_map/all_to_all | solution.py:109
  179.9 1.3 multiply_reduce_fusion.2
  181.2 1.3 pad_maximum_fusion.5
  182.5 4.7 %all_to_all.42 = f32[2,1,2]{2,1,0:T(1,128)S(1)} all-to-all(f32[2,1,2]{2,1,0:T(1,128)S(1)} %broadcast_in_dim.10), channel_id=1, replica_groups=mesh['y'=8,'x'=4,'zh'=2,'zl'=4,'core'=2] {'core'}, dimensions={0} | all-to-all | bytes 32 | tf_op jit(solution)/shard_map/all_to_all | solution.py:115
  187.3 22.0 %all_to_all.43 = f32[256,1,2]{2,1,0:T(1,128)S(1)} all-to-all(f32[256,1,2]{2,1,0:T(1,128)S(1)} %broadcast_in_dim.11), channel_id=1, replica_groups=mesh['y'=8,'x'=4,'zh'=2,'zl'=4,'core'=2] {'y','x','zh','zl'}, dimensions={0} | all-to-all | bytes 4096 | tf_op jit(solution)/shard_map/all_to_all | solution.py:120
  (77 shorter events, 12.1 us)
Async XLA Ops:
  0.6 178.0 %copy-start = (bf16[256,256]{1,0:T(8,128)(2,1)S(1)}, bf16[256,256]{1,0:T(8,128)(2,1)}, u32[]{:S(2)}) copy-start(bf16[256,256]{1,0:T(8,128)(2,1)} %param.23) | copy-start | bytes 393220
  19.9 1.4 copy-start.4
  19.9 1.4 copy-start.5
  20.0 1.9 copy-start.7
  20.0 1.9 copy-start.13
  20.0 2.6 %copy-start.8 = (f32[8,128]{1,0:T(8,128)S(1)}, f32[8,128]{1,0:T(8,128)}, u32[]{:S(2)}) copy-start(f32[8,128]{1,0:T(8,128)} %param.26) | copy-start | bytes 12292
  20.6 4.1 %copy-start.1 = (bf16[2048,1024]{1,0:T(8,128)(2,1)}, bf16[2048,1024]{1,0:T(8,128)(2,1)S(1)}, u32[]{:S(2)}) copy-start(bf16[2048,1024]{1,0:T(8,128)(2,1)S(1)} %pad_maximum_fusion) | copy-start | bytes 12582916
  20.7 2.9 %copy-start.14 = (f32[128]{0:T(128)S(1)}, f32[128]{0:T(128)}, u32[]{:S(2)}) copy-start(f32[128]{0:T(128)} %param.27) | copy-start | bytes 1540
  29.6 62.1 %copy-start.9 = (f32[256]{0:T(256)S(1)}, f32[256]{0:T(256)}, u32[]{:S(2)}) copy-start(f32[256]{0:T(256)} %param.20) | copy-start | bytes 3076
  29.7 62.1 %copy-start.6 = (s32[3,512]{1,0:T(4,128)S(1)}, s32[3,512]{1,0:T(4,128)}, u32[]{:S(2)}) copy-start(s32[3,512]{1,0:T(4,128)} %param.17) | copy-start | bytes 18436
  82.9 38.4 %all-to-all-start.1 = ((f32[64,1,4112]{2,1,0:T(1,128)}), f32[64,1,4112]{2,1,0:T(1,128)}, u32[]{:S(2)}, u32[]{:S(2)}) async-start(f32[64,1,4112]{2,1,0:T(1,128)} %broadcast_in_dim.8), calls=%async_computation.1 | async-start | bytes 2162688 | tf_op jit(solution)/shard_map/all_to_all | solution.py:103
  93.3 33.3 %copy-start.10 = (f32[256]{0:T(256)S(1)}, f32[256]{0:T(256)}, u32[]{:S(2)}) copy-start(f32[256]{0:T(256)} %param.21) | copy-start | bytes 3076
  126.5 2.2 %copy-start.2 = (bf16[2048,1024]{1,0:T(8,128)(2,1)S(1)}, bf16[2048,1024]{1,0:T(8,128)(2,1)}, u32[]{:S(2)}) copy-start(bf16[2048,1024]{1,0:T(8,128)(2,1)} %copy-done.1) | copy-start | bytes 12582916
  131.8 3.7 %copy-start.3 = (bf16[2048,1024]{1,0:T(8,128)(2,1)S(1)}, bf16[2048,1024]{1,0:T(8,128)(2,1)}, u32[]{:S(2)}) copy-start(bf16[2048,1024]{1,0:T(8,128)(2,1)} %copy-done.1) | copy-start | bytes 12582916
  146.5 32.2 %copy-start.12 = (f32[256]{0:T(256)S(1)}, f32[256]{0:T(256)}, u32[]{:S(2)}) copy-start(f32[256]{0:T(256)} %param.22) | copy-start | bytes 3076
  146.5 33.2 %copy-start.11 = (f32[256]{0:T(256)S(1)}, f32[256]{0:T(256)}, u32[]{:S(2)}) copy-start(f32[256]{0:T(256)} %param.24) | copy-start | bytes 3076
  147.7 30.1 %all-to-all-start.3 = ((f32[4,264,256]{2,1,0:T(8,128)}), f32[4,264,256]{2,1,0:T(8,128)S(1)}, u32[]{:S(2)}, u32[]{:S(2)}) async-start(f32[4,264,256]{2,1,0:T(8,128)} %reduce_sum.82), calls=%async_computation.3 | async-start | bytes 2162688 | tf_op jit(solution)/shard_map/all_to_all | solution.py:109

commit v6 on v5

--- a/solution.py
+++ b/solution.py
@@ -22,8 +22,28 @@
         + positions[1][:, None] * k_float[1][None, :]
         + positions[2][:, None] * k_float[2][None, :]
     )
-    angles = TWO_PI * products
-    return jnp.concatenate([jnp.cos(angles), jnp.sin(angles)], axis=1).astype(jnp.bfloat16)
+    quarters = 4.0 * products
+    quarter = jnp.round(quarters)
+    angle = (quarters - quarter) * (0.5 * math.pi)
+    square = angle * angle
+    sine = angle * (
+        1.0
+        + square
+        * (
+            -1.0 / 6.0
+            + square * (1.0 / 120.0 + square * (-1.0 / 5040.0 + square * (1.0 / 362880.0)))
+        )
+    )
+    cosine = 1.0 + square * (
+        -0.5 + square * (1.0 / 24.0 + square * (-1.0 / 720.0 + square * (1.0 / 40320.0)))
+    )
+    turn = quarter - 4.0 * jnp.floor(quarter * 0.25)
+    odd = (turn == 1.0) | (turn == 3.0)
+    cos_base = jnp.where(odd, sine, cosine)
+    sin_base = jnp.where(odd, cosine, sine)
+    cos_value = jnp.where((turn == 1.0) | (turn == 2.0), -cos_base, cos_base)
+    sin_value = jnp.where(turn >= 2.0, -sin_base, sin_base)
+    return jnp.concatenate([cos_value, sin_value], axis=1).astype(jnp.bfloat16)
 
 
 def k_geometry(k_indices):

time: 213 us -> 203 us (0.953)
  other arithmetic: 27.7 us -> 17.1 us
    another operation x4, other arithmetic: 17.7 us -> 7.13 us
where the time goes in v6:
time: 203 us; the launch traced here: 202 us
  blocking collectives  86.3 us (43%)
  waiting for transfers between devices  53.9 us (27%)
  matrix products  17.9 us (9%)
  other arithmetic  17.1 us (8%)
  starting transfers between devices  12.3 us (6%)
  local copies, waits for them, and re-layouts  9.74 us (5%)
  between operations  4.8 us (2%)
    all_to_all x1, blocking collectives, sum_over_atoms(): parts = lax.all_to_all(payload, ATOM_AXES, 0, 0, tiled=True)  50.3 us
    all_to_all x1, waiting for transfers between devices, sum_over_atoms(): return lax.all_to_all(spread, ATOM_AXES, 0, 0, tiled=True)  27.9 us
    all_to_all x1, waiting for transfers between devices, sum_over_ka(): parts = lax.all_to_all(chip, 'zl', 0, 0, tiled=True)  25.9 us
    all_to_all x1, blocking collectives, sum_over_all(): lax.all_to_all(copies, ALL_AXES[:-1], 0, 0, tiled=True)  22 us
    all_to_all x1, blocking collectives, sum_over_ka(): parts = lax.all_to_all(payload, 'core', 1, 1, tiled=True)  9.29 us
    all_to_all x1, starting transfers between devices, sum_over_atoms(): return lax.all_to_all(spread, ATOM_AXES, 0, 0, tiled=True)  8.1 us
    another operation x4, other arithmetic  7.13 us
    all_to_all x1, blocking collectives, sum_over_all(): chip = jnp.sum(lax.all_to_all(pair, 'core', 0, 0, tiled=True), axis=0)  4.75 us
  transfers between devices with their start and end apart: 2, of which 2 were waited for; matrix products, arithmetic and copies ran while one was open for 1% of the time, Pallas kernels for 0%

profile of v6, /device:TPU:1, one launch (start us, length us, event | category | flops | bytes accessed | tf_op | source)
XLA Modules:
  0.0 202.0 jit_solution(1524536025071626150)
XLA Ops:
  2.3 7.1 %fusion.3 = (bf16[2048,512]{1,0:T(8,128)(2,1)S(1)}, bf16[2048,512]{1,0:T(8,128)(2,1)S(1)}) fusion(f32[512]{0:T(512)S(1)} %bitcast.116, f32[2048]{0:T(1024)S(1)} %bitcast.110, f32[512]{0:T(512)S(1)} %bitcast.117, f32[2048]{0:T(1024)S(1)} %bitcast.111, f32[512]{0:T(512)S(1)} %bitcast.115, f32[2048]{0:T(1024)S(1)} %bitcast.109), kind=kLoop, calls=%fused_computation.8 | loop fusion | flops 47185920 | bytes 4225024 | tf_op jit(solution)/shard_map/convert.10
  13.0 1.2 fusion.15
  15.0 3.8 %fusion.22 = f32[1024,256]{1,0:T(8,128)S(1)} fusion(bf16[2048,1024]{1,0:T(8,128)(2,1)} %copy-done.1, bf16[2048,256]{1,0:T(8,128)(2,1)S(1)} %copy-done.4, bf16[2048]{0:T(1024)(128)(2,1)S(1)} %get-tuple-element.46), kind=kOutput, calls=%fused_computation.47 | convolution fusion | flops 1074266112 | bytes 6295552 | tf_op jit(solution)/shard_map/dot_general | solution.py:177
  19.9 50.3 %all_to_all.40 = f32[64,1,4112]{2,1,0:T(1,128)S(1)} all-to-all(f32[64,1,4112]{2,1,0:T(1,128)S(1)} %all_to_all.26), channel_id=1, replica_groups=mesh['y'=8,'x'=4,'zh'=2,'zl'=4,'core'=2] {'y','x','zh'}, dimensions={0} | all-to-all | bytes 2105344 | tf_op jit(solution)/shard_map/all_to_all | solution.py:120
  70.8 1.6 broadcast_in_dim.8
  72.4 8.1 %all-to-all-start.1 = ((f32[64,1,4112]{2,1,0:T(1,128)}), f32[64,1,4112]{2,1,0:T(1,128)}, u32[]{:S(2)}, u32[]{:S(2)}) async-start(f32[64,1,4112]{2,1,0:T(1,128)} %broadcast_in_dim.8), calls=%async_computation.1 | async-start | bytes 2162688 | tf_op jit(solution)/shard_map/all_to_all | solution.py:123
  81.5 1.2 concatenate.24
  82.8 27.9 %all-to-all-done.1 = f32[64,1,4112]{2,1,0:T(1,128)} async-done(((f32[64,1,4112]{2,1,0:T(1,128)}), f32[64,1,4112]{2,1,0:T(1,128)}, u32[]{:S(2)}, u32[]{:S(2)}) %all-to-all-start.1) | async-done | bytes 1052704 | tf_op jit(solution)/shard_map/all_to_all | solution.py:123
  110.7 1.3 copy.30
  112.2 2.4 %multiply_convert_fusion.3 = (bf16[64,4096]{1,0:T(8,128)(2,1)S(1)}, f32[64,4096]{1,0:T(8,128)}) fusion(f32[64,4096]{1,0:T(8,128)} %concatenate.24, f32[64,4112]{1,0:T(8,128)S(1)} %bitcast.107), kind=kLoop, calls=%fused_computation.38 | loop fusion | flops 524288 | bytes 3670016 | tf_op jit(solution)/shard_map/convert_element_type | solution.py:191
  114.6 1.4 reshape.352
  116.0 1.3 fusion.10
  118.2 1.4 fusion.12
  119.6 1.4 fusion.9
  121.3 3.6 %fusion.81 = f32[8,256,256]{2,1,0:T(8,128)S(1)} fusion(bf16[8,256,1024]{2,1,0:T(8,128)(2,1)} %bitcast.104, bf16[1024,256,1]{1,0,2:T(8,128)(2,1)S(1)} %reshape.361), kind=kOutput, calls=%fused_computation.133 | convolution fusion | flops 1073741824 | bytes 6815744 | tf_op jit(solution)/shard_map/dot_general | solution.py:192
  124.9 1.2 fusion.31
  126.6 9.3 %all_to_all.41 = f32[4,2,264,256]{3,2,0,1:T(8,128)S(1)} all-to-all(f32[4,2,264,256]{3,2,0,1:T(8,128)S(1)} %copy.22), channel_id=1, replica_groups=mesh['y'=8,'x'=4,'zh'=2,'zl'=4,'core'=2] {'core'}, dimensions={1} | all-to-all | bytes 4325376 | tf_op jit(solution)/shard_map/all_to_all | solution.py:127
  135.9 1.2 reduce_sum.82
  137.1 4.2 %all-to-all-start.3 = ((f32[4,264,256]{2,1,0:T(8,128)}), f32[4,264,256]{2,1,0:T(8,128)S(1)}, u32[]{:S(2)}, u32[]{:S(2)}) async-start(f32[4,264,256]{2,1,0:T(8,128)} %reduce_sum.82), calls=%async_computation.3 | async-start | bytes 2162688 | tf_op jit(solution)/shard_map/all_to_all | solution.py:129
  141.4 25.9 %all-to-all-done.3 = f32[4,264,256]{2,1,0:T(8,128)S(1)} async-done(((f32[4,264,256]{2,1,0:T(8,128)}), f32[4,264,256]{2,1,0:T(8,128)S(1)}, u32[]{:S(2)}, u32[]{:S(2)}) %all-to-all-start.3) | async-done | bytes 1081376 | tf_op jit(solution)/shard_map/all_to_all | solution.py:129
  169.3 1.3 multiply_reduce_fusion.2
  170.6 1.3 pad_maximum_fusion.5
  171.9 4.7 %all_to_all.42 = f32[2,1,2]{2,1,0:T(1,128)S(1)} all-to-all(f32[2,1,2]{2,1,0:T(1,128)S(1)} %broadcast_in_dim.10), channel_id=1, replica_groups=mesh['y'=8,'x'=4,'zh'=2,'zl'=4,'core'=2] {'core'}, dimensions={0} | all-to-all | bytes 32 | tf_op jit(solution)/shard_map/all_to_all | solution.py:135
  176.8 22.0 %all_to_all.43 = f32[256,1,2]{2,1,0:T(1,128)S(1)} all-to-all(f32[256,1,2]{2,1,0:T(1,128)S(1)} %broadcast_in_dim.11), channel_id=1, replica_groups=mesh['y'=8,'x'=4,'zh'=2,'zl'=4,'core'=2] {'y','x','zh','zl'}, dimensions={0} | all-to-all | bytes 4096 | tf_op jit(solution)/shard_map/all_to_all | solution.py:140
  (77 shorter events, 12.1 us)
Async XLA Ops:
  0.6 167.5 %copy-start = (bf16[256,256]{1,0:T(8,128)(2,1)S(1)}, bf16[256,256]{1,0:T(8,128)(2,1)}, u32[]{:S(2)}) copy-start(bf16[256,256]{1,0:T(8,128)(2,1)} %param.23) | copy-start | bytes 393220
  9.4 1.4 copy-start.4
  9.4 1.4 copy-start.5
  9.4 1.9 copy-start.7
  9.4 1.9 copy-start.13
  9.4 2.6 %copy-start.8 = (f32[8,128]{1,0:T(8,128)S(1)}, f32[8,128]{1,0:T(8,128)}, u32[]{:S(2)}) copy-start(f32[8,128]{1,0:T(8,128)} %param.26) | copy-start | bytes 12292
  10.1 4.1 %copy-start.1 = (bf16[2048,1024]{1,0:T(8,128)(2,1)}, bf16[2048,1024]{1,0:T(8,128)(2,1)S(1)}, u32[]{:S(2)}) copy-start(bf16[2048,1024]{1,0:T(8,128)(2,1)S(1)} %pad_maximum_fusion) | copy-start | bytes 12582916
  10.1 2.9 %copy-start.14 = (f32[128]{0:T(128)S(1)}, f32[128]{0:T(128)}, u32[]{:S(2)}) copy-start(f32[128]{0:T(128)} %param.27) | copy-start | bytes 1540
  19.1 62.1 %copy-start.9 = (f32[256]{0:T(256)S(1)}, f32[256]{0:T(256)}, u32[]{:S(2)}) copy-start(f32[256]{0:T(256)} %param.20) | copy-start | bytes 3076
  19.1 62.1 %copy-start.6 = (s32[3,512]{1,0:T(4,128)S(1)}, s32[3,512]{1,0:T(4,128)}, u32[]{:S(2)}) copy-start(s32[3,512]{1,0:T(4,128)} %param.17) | copy-start | bytes 18436
  72.4 38.3 %all-to-all-start.1 = ((f32[64,1,4112]{2,1,0:T(1,128)}), f32[64,1,4112]{2,1,0:T(1,128)}, u32[]{:S(2)}, u32[]{:S(2)}) async-start(f32[64,1,4112]{2,1,0:T(1,128)} %broadcast_in_dim.8), calls=%async_computation.1 | async-start | bytes 2162688 | tf_op jit(solution)/shard_map/all_to_all | solution.py:123
  82.7 33.3 %copy-start.10 = (f32[256]{0:T(256)S(1)}, f32[256]{0:T(256)}, u32[]{:S(2)}) copy-start(f32[256]{0:T(256)} %param.21) | copy-start | bytes 3076
  116.0 2.2 %copy-start.2 = (bf16[2048,1024]{1,0:T(8,128)(2,1)S(1)}, bf16[2048,1024]{1,0:T(8,128)(2,1)}, u32[]{:S(2)}) copy-start(bf16[2048,1024]{1,0:T(8,128)(2,1)} %copy-done.1) | copy-start | bytes 12582916
  121.2 3.7 %copy-start.3 = (bf16[2048,1024]{1,0:T(8,128)(2,1)S(1)}, bf16[2048,1024]{1,0:T(8,128)(2,1)}, u32[]{:S(2)}) copy-start(bf16[2048,1024]{1,0:T(8,128)(2,1)} %copy-done.1) | copy-start | bytes 12582916
  135.9 32.2 %copy-start.12 = (f32[256]{0:T(256)S(1)}, f32[256]{0:T(256)}, u32[]{:S(2)}) copy-start(f32[256]{0:T(256)} %param.22) | copy-start | bytes 3076
  135.9 33.2 %copy-start.11 = (f32[256]{0:T(256)S(1)}, f32[256]{0:T(256)}, u32[]{:S(2)}) copy-start(f32[256]{0:T(256)} %param.24) | copy-start | bytes 3076
  137.1 30.1 %all-to-all-start.3 = ((f32[4,264,256]{2,1,0:T(8,128)}), f32[4,264,256]{2,1,0:T(8,128)S(1)}, u32[]{:S(2)}, u32[]{:S(2)}) async-start(f32[4,264,256]{2,1,0:T(8,128)} %reduce_sum.82), calls=%async_computation.3 | async-start | bytes 2162688 | tf_op jit(solution)/shard_map/all_to_all | solution.py:129

commit v7 on v6

--- a/solution.py
+++ b/solution.py
@@ -117,10 +117,19 @@
 
 
 def sum_over_atoms(payload):
-    parts = lax.all_to_all(payload, ATOM_AXES, 0, 0, tiled=True)
+    rows = lax.axis_size("y")
+    width = payload.shape[1]
+    parts = lax.all_to_all(payload.reshape(rows, -1, width), "y", 0, 0, tiled=True)
+    along_y = jnp.sum(parts, axis=0)
+    parts = lax.all_to_all(along_y, ATOM_AXES[1:], 0, 0, tiled=True)
     reduced = jnp.sum(parts, axis=0, keepdims=True)
-    spread = jnp.broadcast_to(reduced, payload.shape)
-    return lax.all_to_all(spread, ATOM_AXES, 0, 0, tiled=True)
+    spread = lax.all_to_all(
+        jnp.broadcast_to(reduced, along_y.shape), ATOM_AXES[1:], 0, 0, tiled=True
+    )
+    spread = lax.all_to_all(
+        jnp.broadcast_to(spread[None], (rows,) + spread.shape), "y", 0, 0, tiled=True
+    )
+    return spread.reshape(payload.shape)
 
 
 def sum_over_ka(payload):

time: 203 us -> 208 us (1.025)
  blocking collectives: 86.3 us -> 103 us
  waiting for transfers between devices: 53.9 us -> 46.7 us
  starting transfers between devices: 12.3 us -> 8.11 us
    all_to_all x1 -> x3, blocking collectives: 50.3 us -> 68.8 us  [the longest x1 34 us: sum_over_atoms(): lax.all_to_all(payload.reshape(rows, -1, width), 'y', 0, 0, tiled=True)]
    all_to_all x1, waiting for transfers between devices: 27.9 us -> 20.8 us  [sum_over_atoms(): lax.all_to_all(jnp.broadcast_to(spread[None], (rows,) + spread.shape), 'y...]
    all_to_all x1, starting transfers between devices: 8.1 us -> 3.74 us  [sum_over_atoms(): lax.all_to_all(jnp.broadcast_to(spread[None], (rows,) + spread.shape), 'y...]
  transfers between devices with their start and end apart: 2 -> 2, of which waited for: 2 -> 2; matrix products, arithmetic and copies ran while one was open for 1% -> 2% of each run, Pallas kernels for 0% -> 0%
where the time goes in v7:
time: 208 us; the launch traced here: 207 us
  blocking collectives  103 us (50%)
  waiting for transfers between devices  46.7 us (22%)
  matrix products  17.9 us (9%)
  other arithmetic  17.8 us (9%)
  local copies, waits for them, and re-layouts  8.6 us (4%)
  starting transfers between devices  8.11 us (4%)
  between operations  4.86 us (2%)
    all_to_all x1, blocking collectives, sum_over_atoms(): lax.all_to_all(payload.reshape(rows, -1, width), 'y', 0, 0, tiled=True)  34 us
    all_to_all x1, waiting for transfers between devices, sum_over_ka(): parts = lax.all_to_all(chip, 'zl', 0, 0, tiled=True)  25.9 us
    all_to_all x1, blocking collectives, sum_over_atoms(): parts = lax.all_to_all(along_y, ATOM_AXES[1:], 0, 0, tiled=True)  22.9 us
    all_to_all x1, blocking collectives, sum_over_all(): lax.all_to_all(copies, ALL_AXES[:-1], 0, 0, tiled=True)  21.2 us
    all_to_all x1, waiting for transfers between devices, sum_over_atoms(): lax.all_to_all(jnp.broadcast_to(spread[None], (rows,) + spread.shape), 'y...  20.8 us
    all_to_all x1, blocking collectives, sum_over_atoms(): lax.all_to_all(jnp.broadcast_to(reduced, along_y.shape), ATOM_AXES[1:], 0...  11.9 us
    all_to_all x1, blocking collectives, sum_over_ka(): parts = lax.all_to_all(payload, 'core', 1, 1, tiled=True)  8.46 us
    another operation x4, other arithmetic  7.13 us
  transfers between devices with their start and end apart: 2, of which 2 were waited for; matrix products, arithmetic and copies ran while one was open for 2% of the time, Pallas kernels for 0%

profile of v7, /device:TPU:1, one launch (start us, length us, event | category | flops | bytes accessed | tf_op | source)
XLA Modules:
  0.0 207.1 jit_solution(7995970835294547828)
XLA Ops:
  2.3 7.1 %fusion.3 = (bf16[2048,512]{1,0:T(8,128)(2,1)S(1)}, bf16[2048,512]{1,0:T(8,128)(2,1)S(1)}) fusion(f32[512]{0:T(512)S(1)} %bitcast.118, f32[2048]{0:T(1024)S(1)} %bitcast.112, f32[512]{0:T(512)S(1)} %bitcast.119, f32[2048]{0:T(1024)S(1)} %bitcast.113, f32[512]{0:T(512)S(1)} %bitcast.117, f32[2048]{0:T(1024)S(1)} %bitcast.111), kind=kLoop, calls=%fused_computation.8 | loop fusion | flops 47185920 | bytes 4225024 | tf_op jit(solution)/shard_map/convert.10
  13.0 1.2 fusion.15
  15.0 3.8 %fusion.22 = f32[1024,256]{1,0:T(8,128)S(1)} fusion(bf16[2048,1024]{1,0:T(8,128)(2,1)} %copy-done.1, bf16[2048,256]{1,0:T(8,128)(2,1)S(1)} %copy-done.4, bf16[2048]{0:T(1024)(128)(2,1)S(1)} %get-tuple-element.46), kind=kOutput, calls=%fused_computation.46 | convolution fusion | flops 1074266112 | bytes 6295552 | tf_op jit(solution)/shard_map/dot_general | solution.py:186
  19.1 34.0 %all_to_all.47 = f32[8,8,4112]{2,1,0:T(8,128)S(1)} all-to-all(f32[8,8,4112]{2,1,0:T(8,128)S(1)} %pad_maximum_fusion.2), channel_id=1, replica_groups=mesh['y'=8,'x'=4,'zh'=2,'zl'=4,'core'=2] {'y'}, dimensions={0} | all-to-all | bytes 2105344 | tf_op jit(solution)/shard_map/all_to_all | solution.py:122
  53.3 22.9 %all_to_all.48 = f32[8,1,4112]{2,1,0:T(1,128)S(1)} all-to-all(f32[8,1,4112]{2,1,0:T(1,128)S(1)} %all_to_all.31), channel_id=1, replica_groups=mesh['y'=8,'x'=4,'zh'=2,'zl'=4,'core'=2] {'x','zh'}, dimensions={0} | all-to-all | bytes 263168 | tf_op jit(solution)/shard_map/all_to_all | solution.py:124
  76.4 11.9 %all_to_all.49 = f32[8,1,4112]{2,1,0:T(1,128)S(1)} all-to-all(f32[8,1,4112]{2,1,0:T(1,128)S(1)} %broadcast_in_dim.12), channel_id=1, replica_groups=mesh['y'=8,'x'=4,'zh'=2,'zl'=4,'core'=2] {'x','zh'}, dimensions={0} | all-to-all | bytes 263168 | tf_op jit(solution)/shard_map/all_to_all | solution.py:126
  89.3 3.7 %all-to-all-start.3 = ((f32[8,8,4112]{2,1,0:T(8,128)}), f32[8,8,4112]{2,1,0:T(8,128)S(1)}, u32[]{:S(2)}, u32[]{:S(2)}) async-start(f32[8,8,4112]{2,1,0:T(8,128)} %broadcast_in_dim.14), calls=%async_computation.3 | async-start | bytes 2162688 | tf_op jit(solution)/shard_map/all_to_all | solution.py:129
  95.1 2.4 %concatenate.29 = f32[64,4096]{1,0:T(8,128)} reshape(f32[1024,256]{1,0:T(8,128)} %pad_maximum_fusion.3) | data formatting | bytes 2097152 | tf_op jit(solution)/shard_map/concatenate | solution.py:200
  97.6 20.8 %all-to-all-done.3 = f32[8,8,4112]{2,1,0:T(8,128)S(1)} async-done(((f32[8,8,4112]{2,1,0:T(8,128)}), f32[8,8,4112]{2,1,0:T(8,128)S(1)}, u32[]{:S(2)}, u32[]{:S(2)}) %all-to-all-start.3) | async-done | bytes 1052704 | tf_op jit(solution)/shard_map/all_to_all | solution.py:129
  118.6 2.4 %multiply_convert_fusion.3 = (bf16[64,4096]{1,0:T(8,128)(2,1)S(1)}, f32[64,4096]{1,0:T(8,128)}) fusion(f32[64,4096]{1,0:T(8,128)} %concatenate.29, f32[64,4112]{1,0:T(8,128)S(1)} %bitcast.108), kind=kLoop, calls=%fused_computation.37 | loop fusion | flops 524288 | bytes 3670016 | tf_op jit(solution)/shard_map/convert_element_type | solution.py:200
  121.0 1.4 reshape.357
  122.4 1.3 fusion.10
  124.6 1.4 fusion.12
  126.0 1.4 fusion.9
  127.7 3.6 %fusion.81 = f32[8,256,256]{2,1,0:T(8,128)S(1)} fusion(bf16[8,256,1024]{2,1,0:T(8,128)(2,1)} %bitcast.105, bf16[1024,256,1]{1,0,2:T(8,128)(2,1)S(1)} %reshape.366), kind=kOutput, calls=%fused_computation.133 | convolution fusion | flops 1073741824 | bytes 6815744 | tf_op jit(solution)/shard_map/dot_general | solution.py:201
  131.3 1.2 fusion.31
  133.0 8.5 %all_to_all.50 = f32[4,2,264,256]{3,2,0,1:T(8,128)S(1)} all-to-all(f32[4,2,264,256]{3,2,0,1:T(8,128)S(1)} %copy.22), channel_id=1, replica_groups=mesh['y'=8,'x'=4,'zh'=2,'zl'=4,'core'=2] {'core'}, dimensions={1} | all-to-all | bytes 4325376 | tf_op jit(solution)/shard_map/all_to_all | solution.py:136
  141.5 1.2 reduce_sum.92
  142.7 4.4 %all-to-all-start.5 = ((f32[4,264,256]{2,1,0:T(8,128)}), f32[4,264,256]{2,1,0:T(8,128)S(1)}, u32[]{:S(2)}, u32[]{:S(2)}) async-start(f32[4,264,256]{2,1,0:T(8,128)} %reduce_sum.92), calls=%async_computation.5 | async-start | bytes 2162688 | tf_op jit(solution)/shard_map/all_to_all | solution.py:138
  147.1 25.9 %all-to-all-done.5 = f32[4,264,256]{2,1,0:T(8,128)S(1)} async-done(((f32[4,264,256]{2,1,0:T(8,128)}), f32[4,264,256]{2,1,0:T(8,128)S(1)}, u32[]{:S(2)}, u32[]{:S(2)}) %all-to-all-start.5) | async-done | bytes 1081376 | tf_op jit(solution)/shard_map/all_to_all | solution.py:138
  175.1 1.3 multiply_reduce_fusion.2
  176.4 1.3 pad_maximum_fusion.5
  177.8 4.7 %all_to_all.51 = f32[2,1,2]{2,1,0:T(1,128)S(1)} all-to-all(f32[2,1,2]{2,1,0:T(1,128)S(1)} %broadcast_in_dim.16), channel_id=1, replica_groups=mesh['y'=8,'x'=4,'zh'=2,'zl'=4,'core'=2] {'core'}, dimensions={0} | all-to-all | bytes 32 | tf_op jit(solution)/shard_map/all_to_all | solution.py:144
  182.6 21.2 %all_to_all.52 = f32[256,1,2]{2,1,0:T(1,128)S(1)} all-to-all(f32[256,1,2]{2,1,0:T(1,128)S(1)} %broadcast_in_dim.17), channel_id=1, replica_groups=mesh['y'=8,'x'=4,'zh'=2,'zl'=4,'core'=2] {'y','x','zh','zl'}, dimensions={0} | all-to-all | bytes 4096 | tf_op jit(solution)/shard_map/all_to_all | solution.py:149
  (81 shorter events, 13.1 us)
Async XLA Ops:
  0.6 173.3 %copy-start = (bf16[256,256]{1,0:T(8,128)(2,1)S(1)}, bf16[256,256]{1,0:T(8,128)(2,1)}, u32[]{:S(2)}) copy-start(bf16[256,256]{1,0:T(8,128)(2,1)} %param.23) | copy-start | bytes 393220
  9.4 1.4 copy-start.4
  9.4 1.4 copy-start.5
  9.4 1.9 copy-start.7
  9.4 1.9 copy-start.13
  9.4 2.6 %copy-start.8 = (f32[8,128]{1,0:T(8,128)S(1)}, f32[8,128]{1,0:T(8,128)}, u32[]{:S(2)}) copy-start(f32[8,128]{1,0:T(8,128)} %param.26) | copy-start | bytes 12292
  10.1 4.1 %copy-start.1 = (bf16[2048,1024]{1,0:T(8,128)(2,1)}, bf16[2048,1024]{1,0:T(8,128)(2,1)S(1)}, u32[]{:S(2)}) copy-start(bf16[2048,1024]{1,0:T(8,128)(2,1)S(1)} %pad_maximum_fusion) | copy-start | bytes 12582916
  10.1 2.9 %copy-start.14 = (f32[128]{0:T(128)S(1)}, f32[128]{0:T(128)}, u32[]{:S(2)}) copy-start(f32[128]{0:T(128)} %param.27) | copy-start | bytes 1540
  19.1 74.6 %copy-start.9 = (f32[256]{0:T(256)S(1)}, f32[256]{0:T(256)}, u32[]{:S(2)}) copy-start(f32[256]{0:T(256)} %param.20) | copy-start | bytes 3076
  19.1 74.6 %copy-start.6 = (s32[3,512]{1,0:T(4,128)S(1)}, s32[3,512]{1,0:T(4,128)}, u32[]{:S(2)}) copy-start(s32[3,512]{1,0:T(4,128)} %param.17) | copy-start | bytes 18436
  89.3 29.1 %all-to-all-start.3 = ((f32[8,8,4112]{2,1,0:T(8,128)}), f32[8,8,4112]{2,1,0:T(8,128)S(1)}, u32[]{:S(2)}, u32[]{:S(2)}) async-start(f32[8,8,4112]{2,1,0:T(8,128)} %broadcast_in_dim.14), calls=%async_computation.3 | async-start | bytes 2162688 | tf_op jit(solution)/shard_map/all_to_all | solution.py:129
  95.1 27.3 %copy-start.10 = (f32[256]{0:T(256)S(1)}, f32[256]{0:T(256)}, u32[]{:S(2)}) copy-start(f32[256]{0:T(256)} %param.21) | copy-start | bytes 3076
  122.4 2.2 %copy-start.2 = (bf16[2048,1024]{1,0:T(8,128)(2,1)S(1)}, bf16[2048,1024]{1,0:T(8,128)(2,1)}, u32[]{:S(2)}) copy-start(bf16[2048,1024]{1,0:T(8,128)(2,1)} %copy-done.1) | copy-start | bytes 12582916
  127.6 3.7 %copy-start.3 = (bf16[2048,1024]{1,0:T(8,128)(2,1)S(1)}, bf16[2048,1024]{1,0:T(8,128)(2,1)}, u32[]{:S(2)}) copy-start(bf16[2048,1024]{1,0:T(8,128)(2,1)} %copy-done.1) | copy-start | bytes 12582916
  141.5 32.4 %copy-start.12 = (f32[256]{0:T(256)S(1)}, f32[256]{0:T(256)}, u32[]{:S(2)}) copy-start(f32[256]{0:T(256)} %param.22) | copy-start | bytes 3076
  141.5 33.4 %copy-start.11 = (f32[256]{0:T(256)S(1)}, f32[256]{0:T(256)}, u32[]{:S(2)}) copy-start(f32[256]{0:T(256)} %param.24) | copy-start | bytes 3076
  142.7 30.4 %all-to-all-start.5 = ((f32[4,264,256]{2,1,0:T(8,128)}), f32[4,264,256]{2,1,0:T(8,128)S(1)}, u32[]{:S(2)}, u32[]{:S(2)}) async-start(f32[4,264,256]{2,1,0:T(8,128)} %reduce_sum.92), calls=%async_computation.5 | async-start | bytes 2162688 | tf_op jit(solution)/shard_map/all_to_all | solution.py:138

commit v8 on v6

--- a/solution.py
+++ b/solution.py
@@ -116,10 +116,10 @@
     )
 
 
-def sum_over_atoms(payload):
+def sum_over_atoms(payload, finish_chunk):
     parts = lax.all_to_all(payload, ATOM_AXES, 0, 0, tiled=True)
-    reduced = jnp.sum(parts, axis=0, keepdims=True)
-    spread = jnp.broadcast_to(reduced, payload.shape)
+    reduced = finish_chunk(jnp.sum(parts, axis=0))
+    spread = jnp.broadcast_to(reduced[None, :], payload.shape)
     return lax.all_to_all(spread, ATOM_AXES, 0, 0, tiled=True)
 
 
@@ -183,12 +183,20 @@
     payload = jnp.concatenate(
         [factor.reshape(atom_groups, flat), charge_sum.reshape(atom_groups, rows_each)], axis=1
     )
-    summed = sum_over_atoms(payload)
-    factor = summed[:, :flat].reshape(2 * k_width, channels)
+    k_vectors, k_square = k_geometry(k_indices)
+    owner = lax.axis_index(ATOM_AXES)
+    k_start = (owner * rows_each) % k_width
+
+    def weigh(chunk):
+        chunk_square = lax.dynamic_slice_in_dim(k_square, k_start, rows_each, 0)
+        chunk_kernel = teacher_kernel(chunk_square, smearing, inv_root)
+        rows = chunk[:flat].reshape(rows_each, channels)
+        rounded = (chunk_kernel * rows).astype(jnp.bfloat16).astype(jnp.float32)
+        return jnp.concatenate([rounded.reshape(-1), chunk[flat:]])
+
+    summed = sum_over_atoms(payload, weigh)
+    weighted = summed[:, :flat].reshape(2 * k_width, channels).astype(jnp.bfloat16)
     charge_sum = summed[:, flat:].reshape(-1)
-    k_vectors, k_square = k_geometry(k_indices)
-    kernel = teacher_kernel(k_square, smearing, inv_root)
-    weighted = (jnp.concatenate([kernel, kernel], axis=0) * factor).astype(jnp.bfloat16)
     potential = jnp.dot(phases, weighted, preferred_element_type=jnp.float32)
     charged = (features.astype(jnp.float32) * teacher_charge[None, :]).astype(jnp.bfloat16)
     contracted = lax.dot_general(

time: 203 us -> 197 us (0.970)
  blocking collectives: 86.3 us -> 36 us
  waiting for transfers between devices: 53.9 us -> 86.2 us
  starting transfers between devices: 12.3 us -> 31.6 us
  local copies, waits for them, and re-layouts: 9.74 us -> 7.21 us
  matrix products: 17.9 us -> 15.5 us
  other arithmetic: 17.1 us -> 14.9 us
    all_to_all x1 -> x0, blocking collectives: 50.3 us -> none  [sum_over_atoms(): parts = lax.all_to_all(payload, ATOM_AXES, 0, 0, tiled=True)]
    all_to_all x0 -> x1, waiting for transfers between devices: none -> 30.7 us  [sum_over_atoms(): parts = lax.all_to_all(payload, ATOM_AXES, 0, 0, tiled=True)]
    all_to_all x0 -> x1, starting transfers between devices: none -> 19.6 us  [sum_over_atoms(): parts = lax.all_to_all(payload, ATOM_AXES, 0, 0, tiled=True)]
    convert_element_type x1, other arithmetic: 2.38 us -> 0.01 us  [weigh(): rounded = (chunk_kernel * rows).astype(jnp.bfloat16).astype(jnp.float32)]
    dot_general x1, matrix products: 3.64 us -> 1.28 us  [local(): potential = jnp.dot(phases, weighted, preferred_element_type=jnp.float32)]
  transfers between devices with their start and end apart: 2 -> 3, of which waited for: 2 -> 3; matrix products, arithmetic and copies ran while one was open for 1% -> 0% of each run, Pallas kernels for 0% -> 0%
where the time goes in v8:
time: 197 us; the launch traced here: 196 us
  waiting for transfers between devices  86.2 us (44%)
  blocking collectives  36 us (18%)
  starting transfers between devices  31.6 us (16%)
  matrix products  15.5 us (8%)
  other arithmetic  14.9 us (8%)
  local copies, waits for them, and re-layouts  7.21 us (4%)
  between operations  4.96 us (3%)
    all_to_all x1, waiting for transfers between devices, sum_over_atoms(): parts = lax.all_to_all(payload, ATOM_AXES, 0, 0, tiled=True)  30.7 us
    all_to_all x1, waiting for transfers between devices, sum_over_atoms(): return lax.all_to_all(spread, ATOM_AXES, 0, 0, tiled=True)  29.6 us
    all_to_all x1, waiting for transfers between devices, sum_over_ka(): parts = lax.all_to_all(chip, 'zl', 0, 0, tiled=True)  25.9 us
    all_to_all x1, blocking collectives, sum_over_all(): lax.all_to_all(copies, ALL_AXES[:-1], 0, 0, tiled=True)  22 us
    all_to_all x1, starting transfers between devices, sum_over_atoms(): parts = lax.all_to_all(payload, ATOM_AXES, 0, 0, tiled=True)  19.6 us
    all_to_all x1, blocking collectives, sum_over_ka(): parts = lax.all_to_all(payload, 'core', 1, 1, tiled=True)  9.29 us
    all_to_all x1, starting transfers between devices, sum_over_atoms(): return lax.all_to_all(spread, ATOM_AXES, 0, 0, tiled=True)  7.87 us
    another operation x4, other arithmetic  7.13 us
  transfers between devices with their start and end apart: 3, of which 3 were waited for; matrix products, arithmetic and copies ran while one was open for 0% of the time, Pallas kernels for 0%

profile of v8, /device:TPU:1, one launch (start us, length us, event | category | flops | bytes accessed | tf_op | source)
XLA Modules:
  0.0 196.3 jit_solution(12651397279163864893)
XLA Ops:
  2.3 7.1 %fusion.3 = (bf16[2048,512]{1,0:T(8,128)(2,1)S(1)}, bf16[2048,512]{1,0:T(8,128)(2,1)S(1)}) fusion(f32[512]{0:T(512)S(1)} %bitcast.121, f32[2048]{0:T(1024)S(1)} %bitcast.117, f32[512]{0:T(512)S(1)} %bitcast.122, f32[2048]{0:T(1024)S(1)} %bitcast.118, f32[512]{0:T(512)S(1)} %bitcast.120, f32[2048]{0:T(1024)S(1)} %bitcast.116), kind=kLoop, calls=%fused_computation.8 | loop fusion | flops 47185920 | bytes 4225024 | tf_op jit(solution)/shard_map/convert.10
  12.0 1.0 convolution_add_fusion
  13.0 1.2 fusion.15
  15.0 3.8 %fusion.22 = f32[1024,256]{1,0:T(8,128)S(1)} fusion(bf16[2048,1024]{1,0:T(8,128)(2,1)} %copy-done.1, bf16[2048,256]{1,0:T(8,128)(2,1)S(1)} %copy-done.3, bf16[2048]{0:T(1024)(128)(2,1)S(1)} %get-tuple-element.47), kind=kOutput, calls=%fused_computation.45 | convolution fusion | flops 1074266112 | bytes 6295552 | tf_op jit(solution)/shard_map/dot_general | solution.py:177
  19.1 1.7 all_to_all.26
  20.8 19.6 %all-to-all-start = ((f32[64,1,4112]{2,1,0:T(1,128)}), f32[64,1,4112]{2,1,0:T(1,128)S(1)}, u32[]{:S(2)}, u32[]{:S(2)}) async-start(f32[64,1,4112]{2,1,0:T(1,128)} %all_to_all.26), calls=%async_computation | async-start | bytes 2162688 | tf_op jit(solution)/shard_map/all_to_all | solution.py:120
  40.7 30.7 %all-to-all-done = f32[64,1,4112]{2,1,0:T(1,128)S(1)} async-done(((f32[64,1,4112]{2,1,0:T(1,128)}), f32[64,1,4112]{2,1,0:T(1,128)S(1)}, u32[]{:S(2)}, u32[]{:S(2)}) %all-to-all-start) | async-done | bytes 1052704 | tf_op jit(solution)/shard_map/all_to_all | solution.py:120
  72.0 1.5 broadcast_in_dim.8
  73.6 7.9 %all-to-all-start.1 = ((f32[64,1,4112]{2,1,0:T(1,128)}), f32[64,1,4112]{2,1,0:T(1,128)S(1)}, u32[]{:S(2)}, u32[]{:S(2)}) async-start(f32[64,1,4112]{2,1,0:T(1,128)} %broadcast_in_dim.8), calls=%async_computation.1 | async-start | bytes 2162688 | tf_op jit(solution)/shard_map/all_to_all | solution.py:123
  82.2 29.6 %all-to-all-done.1 = f32[64,1,4112]{2,1,0:T(1,128)S(1)} async-done(((f32[64,1,4112]{2,1,0:T(1,128)}), f32[64,1,4112]{2,1,0:T(1,128)S(1)}, u32[]{:S(2)}, u32[]{:S(2)}) %all-to-all-start.1) | async-done | bytes 1052704 | tf_op jit(solution)/shard_map/all_to_all | solution.py:123
  112.6 1.3 fusion.10
  114.8 1.4 fusion.12
  116.2 1.4 fusion.9
  117.7 1.3 fusion.89
  119.0 1.2 fusion.33
  120.6 9.3 %all_to_all.40 = f32[4,2,264,256]{3,2,0,1:T(8,128)S(1)} all-to-all(f32[4,2,264,256]{3,2,0,1:T(8,128)S(1)} %copy.22), channel_id=1, replica_groups=mesh['y'=8,'x'=4,'zh'=2,'zl'=4,'core'=2] {'core'}, dimensions={1} | all-to-all | bytes 4325376 | tf_op jit(solution)/shard_map/all_to_all | solution.py:127
  129.9 1.2 reduce_sum.82
  131.2 4.2 %all-to-all-start.3 = ((f32[4,264,256]{2,1,0:T(8,128)}), f32[4,264,256]{2,1,0:T(8,128)S(1)}, u32[]{:S(2)}, u32[]{:S(2)}) async-start(f32[4,264,256]{2,1,0:T(8,128)} %reduce_sum.82), calls=%async_computation.3 | async-start | bytes 2162688 | tf_op jit(solution)/shard_map/all_to_all | solution.py:129
  135.4 25.9 %all-to-all-done.3 = f32[4,264,256]{2,1,0:T(8,128)S(1)} async-done(((f32[4,264,256]{2,1,0:T(8,128)}), f32[4,264,256]{2,1,0:T(8,128)S(1)}, u32[]{:S(2)}, u32[]{:S(2)}) %all-to-all-start.3) | async-done | bytes 1081376 | tf_op jit(solution)/shard_map/all_to_all | solution.py:129
  162.2 0.9 fusion.86
  163.4 1.4 multiply_reduce_fusion.2
  164.7 1.4 pad_maximum_fusion.4
  166.1 4.7 %all_to_all.41 = f32[2,1,2]{2,1,0:T(1,128)S(1)} all-to-all(f32[2,1,2]{2,1,0:T(1,128)S(1)} %broadcast_in_dim.10), channel_id=1, replica_groups=mesh['y'=8,'x'=4,'zh'=2,'zl'=4,'core'=2] {'core'}, dimensions={0} | all-to-all | bytes 32 | tf_op jit(solution)/shard_map/all_to_all | solution.py:135
  171.0 22.0 %all_to_all.42 = f32[256,1,2]{2,1,0:T(1,128)S(1)} all-to-all(f32[256,1,2]{2,1,0:T(1,128)S(1)} %broadcast_in_dim.11), channel_id=1, replica_groups=mesh['y'=8,'x'=4,'zh'=2,'zl'=4,'core'=2] {'y','x','zh','zl'}, dimensions={0} | all-to-all | bytes 4096 | tf_op jit(solution)/shard_map/all_to_all | solution.py:140
  (79 shorter events, 9.8 us)
Async XLA Ops:
  0.6 161.5 %copy-start = (bf16[256,256]{1,0:T(8,128)(2,1)S(1)}, bf16[256,256]{1,0:T(8,128)(2,1)}, u32[]{:S(2)}) copy-start(bf16[256,256]{1,0:T(8,128)(2,1)} %param.23) | copy-start | bytes 393220
  9.4 1.4 copy-start.3
  9.4 1.4 copy-start.4
  9.4 1.9 copy-start.6
  9.4 1.9 copy-start.12
  9.4 2.6 %copy-start.7 = (f32[8,128]{1,0:T(8,128)S(1)}, f32[8,128]{1,0:T(8,128)}, u32[]{:S(2)}) copy-start(f32[8,128]{1,0:T(8,128)} %param.26) | copy-start | bytes 12292
  10.1 4.1 %copy-start.1 = (bf16[2048,1024]{1,0:T(8,128)(2,1)}, bf16[2048,1024]{1,0:T(8,128)(2,1)S(1)}, u32[]{:S(2)}) copy-start(bf16[2048,1024]{1,0:T(8,128)(2,1)S(1)} %pad_maximum_fusion) | copy-start | bytes 12582916
  10.1 2.9 %copy-start.13 = (f32[128]{0:T(128)S(1)}, f32[128]{0:T(128)}, u32[]{:S(2)}) copy-start(f32[128]{0:T(128)} %param.27) | copy-start | bytes 1540
  18.8 21.6 %copy-start.8 = (f32[256]{0:T(256)S(1)}, f32[256]{0:T(256)}, u32[]{:S(2)}) copy-start(f32[256]{0:T(256)} %param.20) | copy-start | bytes 3076
  18.8 21.6 %copy-start.5 = (s32[3,512]{1,0:T(4,128)S(1)}, s32[3,512]{1,0:T(4,128)}, u32[]{:S(2)}) copy-start(s32[3,512]{1,0:T(4,128)} %param.17) | copy-start | bytes 18436
  20.8 50.5 %all-to-all-start = ((f32[64,1,4112]{2,1,0:T(1,128)}), f32[64,1,4112]{2,1,0:T(1,128)S(1)}, u32[]{:S(2)}, u32[]{:S(2)}) async-start(f32[64,1,4112]{2,1,0:T(1,128)} %all_to_all.26), calls=%async_computation | async-start | bytes 2162688 | tf_op jit(solution)/shard_map/all_to_all | solution.py:120
  72.0 40.6 %copy-start.9 = (f32[256]{0:T(256)S(1)}, f32[256]{0:T(256)}, u32[]{:S(2)}) copy-start(f32[256]{0:T(256)} %param.21) | copy-start | bytes 3076
  73.6 38.2 %all-to-all-start.1 = ((f32[64,1,4112]{2,1,0:T(1,128)}), f32[64,1,4112]{2,1,0:T(1,128)S(1)}, u32[]{:S(2)}, u32[]{:S(2)}) async-start(f32[64,1,4112]{2,1,0:T(1,128)} %broadcast_in_dim.8), calls=%async_computation.1 | async-start | bytes 2162688 | tf_op jit(solution)/shard_map/all_to_all | solution.py:123
  112.6 2.2 %copy-start.2 = (bf16[2048,1024]{1,0:T(8,128)(2,1)S(1)}, bf16[2048,1024]{1,0:T(8,128)(2,1)}, u32[]{:S(2)}) copy-start(bf16[2048,1024]{1,0:T(8,128)(2,1)} %copy-done.1) | copy-start | bytes 12582916
  129.9 32.2 %copy-start.11 = (f32[256]{0:T(256)S(1)}, f32[256]{0:T(256)}, u32[]{:S(2)}) copy-start(f32[256]{0:T(256)} %param.22) | copy-start | bytes 3076
  129.9 33.2 %copy-start.10 = (f32[256]{0:T(256)S(1)}, f32[256]{0:T(256)}, u32[]{:S(2)}) copy-start(f32[256]{0:T(256)} %param.24) | copy-start | bytes 3076
  131.2 30.1 %all-to-all-start.3 = ((f32[4,264,256]{2,1,0:T(8,128)}), f32[4,264,256]{2,1,0:T(8,128)S(1)}, u32[]{:S(2)}, u32[]{:S(2)}) async-start(f32[4,264,256]{2,1,0:T(8,128)} %reduce_sum.82), calls=%async_computation.3 | async-start | bytes 2162688 | tf_op jit(solution)/shard_map/all_to_all | solution.py:129

commit v9 on v8

--- a/solution.py
+++ b/solution.py
@@ -208,9 +208,12 @@
     terms_high = force_terms.astype(jnp.bfloat16)
     terms_low = (force_terms - terms_high.astype(jnp.float32)).astype(jnp.bfloat16)
     k_low = k_indices.astype(jnp.bfloat16)
-    teacher_force_t = TWO_PI * (
-        lax.dot_general(k_low, terms_high, (((1,), (1,)), ((), ())), preferred_element_type=jnp.float32)
-        + lax.dot_general(k_low, terms_low, (((1,), (1,)), ((), ())), preferred_element_type=jnp.float32)
+    terms = jnp.concatenate([terms_high, terms_low], axis=1)
+    teacher_force_t = TWO_PI * lax.dot_general(
+        jnp.concatenate([k_low, k_low], axis=1),
+        terms,
+        (((1,), (1,)), ((), ())),
+        preferred_element_type=jnp.float32,
     )
     table = student_table(k_vectors, k_square, charge_sum, student_smear, inv_root, k_width)
     student_part_t = lax.dot_general(

time: 197 us -> 197 us (level)
  local copies, waits for them, and re-layouts: 7.21 us -> 14.4 us
  waiting for transfers between devices: 86.2 us -> 79.7 us
  matrix products: 15.5 us -> 13.1 us
    all_to_all x1, waiting for transfers between devices: 29.6 us -> 23.2 us  [sum_over_atoms(): return lax.all_to_all(spread, ATOM_AXES, 0, 0, tiled=True)]
    dot_general x0 -> x1, local copies, waits for them, and re-layouts: none -> 6.44 us  [local(): potential = jnp.dot(phases, weighted, preferred_element_type=jnp.float32)]
    dot_general x2 -> x1, matrix products: 2.77 us -> 0.65 us  [local(): lax.dot_general(jnp.concatenate([k_low, k_low], axis=1), terms, (((1,), (...]
  transfers between devices with their start and end apart: 3 -> 3, of which waited for: 3 -> 3; matrix products, arithmetic and copies ran while one was open for 0% -> 3% of each run, Pallas kernels for 0% -> 0%
where the time goes in v9:
time: 197 us; the launch traced here: 196 us
  waiting for transfers between devices  79.7 us (40%)
  blocking collectives  36 us (18%)
  starting transfers between devices  31.6 us (16%)
  other arithmetic  16.5 us (8%)
  local copies, waits for them, and re-layouts  14.4 us (7%)
  matrix products  13.1 us (7%)
  between operations  4.93 us (3%)
    all_to_all x1, waiting for transfers between devices, sum_over_atoms(): parts = lax.all_to_all(payload, ATOM_AXES, 0, 0, tiled=True)  30.7 us
    all_to_all x1, waiting for transfers between devices, sum_over_ka(): parts = lax.all_to_all(chip, 'zl', 0, 0, tiled=True)  25.9 us
    all_to_all x1, waiting for transfers between devices, sum_over_atoms(): return lax.all_to_all(spread, ATOM_AXES, 0, 0, tiled=True)  23.2 us
    all_to_all x1, blocking collectives, sum_over_all(): lax.all_to_all(copies, ALL_AXES[:-1], 0, 0, tiled=True)  22 us
    all_to_all x1, starting transfers between devices, sum_over_atoms(): parts = lax.all_to_all(payload, ATOM_AXES, 0, 0, tiled=True)  19.6 us
    all_to_all x1, blocking collectives, sum_over_ka(): parts = lax.all_to_all(payload, 'core', 1, 1, tiled=True)  9.29 us
    all_to_all x1, starting transfers between devices, sum_over_atoms(): return lax.all_to_all(spread, ATOM_AXES, 0, 0, tiled=True)  7.87 us
    another operation x4, other arithmetic  7.39 us
  transfers between devices with their start and end apart: 3, of which 3 were waited for; matrix products, arithmetic and copies ran while one was open for 3% of the time, Pallas kernels for 0%

profile of v9, /device:TPU:1, one launch (start us, length us, event | category | flops | bytes accessed | tf_op | source)
XLA Modules:
  0.0 196.3 jit_solution(5357676835767303128)
XLA Ops:
  2.3 7.3 %fusion.3 = (bf16[2048,512]{0,1:T(8,128)(2,1)S(1)}, bf16[2048,512]{0,1:T(8,128)(2,1)S(1)}) fusion(f32[512]{0:T(512)S(1)} %bitcast.119, f32[2048]{0:T(1024)S(1)} %bitcast.115, f32[512]{0:T(512)S(1)} %bitcast.120, f32[2048]{0:T(1024)S(1)} %bitcast.116, f32[512]{0:T(512)S(1)} %bitcast.118, f32[2048]{0:T(1024)S(1)} %bitcast.114), kind=kLoop, calls=%fused_computation.8 | loop fusion | flops 47185920 | bytes 4225024 | tf_op jit(solution)/shard_map/convert.10
  12.2 1.0 convolution_add_fusion
  13.2 1.2 fusion.17
  14.5 1.2 fusion.93
  15.8 3.6 %fusion.24 = f32[1024,256]{1,0:T(8,128)S(1)} fusion(bf16[2048,1024]{0,1:T(8,128)(2,1)} %copy-done.1, bf16[2048,256]{1,0:T(8,128)(2,1)S(1)} %copy-done.3, bf16[2048]{0:T(1024)(128)(2,1)S(1)} %get-tuple-element.51), kind=kOutput, calls=%fused_computation.44 | convolution fusion | flops 1074266112 | bytes 6295552 | tf_op jit(solution)/shard_map/dot_general | solution.py:177
  19.6 1.7 all_to_all.26
  21.3 19.6 %all-to-all-start = ((f32[64,1,4112]{2,1,0:T(1,128)}), f32[64,1,4112]{2,1,0:T(1,128)S(1)}, u32[]{:S(2)}, u32[]{:S(2)}) async-start(f32[64,1,4112]{2,1,0:T(1,128)} %all_to_all.26), calls=%async_computation | async-start | bytes 2162688 | tf_op jit(solution)/shard_map/all_to_all | solution.py:120
  41.2 30.7 %all-to-all-done = f32[64,1,4112]{2,1,0:T(1,128)S(1)} async-done(((f32[64,1,4112]{2,1,0:T(1,128)}), f32[64,1,4112]{2,1,0:T(1,128)S(1)}, u32[]{:S(2)}, u32[]{:S(2)}) %all-to-all-start) | async-done | bytes 1052704 | tf_op jit(solution)/shard_map/all_to_all | solution.py:120
  72.5 1.6 broadcast_in_dim.8
  74.2 7.9 %all-to-all-start.1 = ((f32[64,1,4112]{2,1,0:T(1,128)}), f32[64,1,4112]{2,1,0:T(1,128)S(1)}, u32[]{:S(2)}, u32[]{:S(2)}) async-start(f32[64,1,4112]{2,1,0:T(1,128)} %broadcast_in_dim.8), calls=%async_computation.1 | async-start | bytes 2162688 | tf_op jit(solution)/shard_map/all_to_all | solution.py:123
  82.0 6.4 %copy.30 = bf16[2048,1024]{1,0:T(8,128)(2,1)} copy(bf16[2048,1024]{0,1:T(8,128)(2,1)} %copy-done.1) | data formatting | bytes 8388608 | tf_op jit(solution)/shard_map/dot_general | solution.py:200
  89.2 23.2 %all-to-all-done.1 = f32[64,1,4112]{2,1,0:T(1,128)S(1)} async-done(((f32[64,1,4112]{2,1,0:T(1,128)}), f32[64,1,4112]{2,1,0:T(1,128)S(1)}, u32[]{:S(2)}, u32[]{:S(2)}) %all-to-all-start.1) | async-done | bytes 1052704 | tf_op jit(solution)/shard_map/all_to_all | solution.py:123
  113.2 1.3 fusion.15
  115.4 1.5 subtract_convert_fusion
  117.6 1.3 fusion.94
  120.7 9.3 %all_to_all.40 = f32[4,2,264,256]{3,2,0,1:T(8,128)S(1)} all-to-all(f32[4,2,264,256]{3,2,0,1:T(8,128)S(1)} %copy.27), channel_id=1, replica_groups=mesh['y'=8,'x'=4,'zh'=2,'zl'=4,'core'=2] {'core'}, dimensions={1} | all-to-all | bytes 4325376 | tf_op jit(solution)/shard_map/all_to_all | solution.py:127
  130.0 1.2 reduce_sum.82
  131.2 4.2 %all-to-all-start.3 = ((f32[4,264,256]{2,1,0:T(8,128)}), f32[4,264,256]{2,1,0:T(8,128)S(1)}, u32[]{:S(2)}, u32[]{:S(2)}) async-start(f32[4,264,256]{2,1,0:T(8,128)} %reduce_sum.82), calls=%async_computation.3 | async-start | bytes 2162688 | tf_op jit(solution)/shard_map/all_to_all | solution.py:129
  135.5 25.9 %all-to-all-done.3 = f32[4,264,256]{2,1,0:T(8,128)S(1)} async-done(((f32[4,264,256]{2,1,0:T(8,128)}), f32[4,264,256]{2,1,0:T(8,128)S(1)}, u32[]{:S(2)}, u32[]{:S(2)}) %all-to-all-start.3) | async-done | bytes 1081376 | tf_op jit(solution)/shard_map/all_to_all | solution.py:129
  162.2 0.9 fusion.91
  163.4 1.4 multiply_reduce_fusion.2
  164.8 1.3 pad_maximum_fusion.4
  166.1 4.7 %all_to_all.41 = f32[2,1,2]{2,1,0:T(1,128)S(1)} all-to-all(f32[2,1,2]{2,1,0:T(1,128)S(1)} %broadcast_in_dim.10), channel_id=1, replica_groups=mesh['y'=8,'x'=4,'zh'=2,'zl'=4,'core'=2] {'core'}, dimensions={0} | all-to-all | bytes 32 | tf_op jit(solution)/shard_map/all_to_all | solution.py:135
  171.0 22.0 %all_to_all.42 = f32[256,1,2]{2,1,0:T(1,128)S(1)} all-to-all(f32[256,1,2]{2,1,0:T(1,128)S(1)} %broadcast_in_dim.11), channel_id=1, replica_groups=mesh['y'=8,'x'=4,'zh'=2,'zl'=4,'core'=2] {'y','x','zh','zl'}, dimensions={0} | all-to-all | bytes 4096 | tf_op jit(solution)/shard_map/all_to_all | solution.py:140
  (82 shorter events, 11.0 us)
Async XLA Ops:
  0.6 161.6 %copy-start = (bf16[256,256]{1,0:T(8,128)(2,1)S(1)}, bf16[256,256]{1,0:T(8,128)(2,1)}, u32[]{:S(2)}) copy-start(bf16[256,256]{1,0:T(8,128)(2,1)} %param.23) | copy-start | bytes 393220
  9.7 1.4 copy-start.3
  9.7 1.4 copy-start.5
  9.7 1.8 copy-start.7
  9.7 1.8 copy-start.13
  9.7 2.5 %copy-start.8 = (f32[8,128]{1,0:T(8,128)S(1)}, f32[8,128]{1,0:T(8,128)}, u32[]{:S(2)}) copy-start(f32[8,128]{1,0:T(8,128)} %param.26) | copy-start | bytes 12292
  10.3 4.1 %copy-start.1 = (bf16[2048,1024]{0,1:T(8,128)(2,1)}, bf16[2048,1024]{0,1:T(8,128)(2,1)S(1)}, u32[]{:S(2)}) copy-start(bf16[2048,1024]{0,1:T(8,128)(2,1)S(1)} %pad_maximum_fusion) | copy-start | bytes 12582916
  10.3 2.9 %copy-start.14 = (f32[128]{0:T(128)S(1)}, f32[128]{0:T(128)}, u32[]{:S(2)}) copy-start(f32[128]{0:T(128)} %param.27) | copy-start | bytes 1540
  19.3 21.6 %copy-start.10 = (f32[256]{0:T(256)S(1)}, f32[256]{0:T(256)}, u32[]{:S(2)}) copy-start(f32[256]{0:T(256)} %param.20) | copy-start | bytes 3076
  19.3 21.6 %copy-start.6 = (s32[3,512]{1,0:T(4,128)S(1)}, s32[3,512]{1,0:T(4,128)}, u32[]{:S(2)}) copy-start(s32[3,512]{1,0:T(4,128)} %param.17) | copy-start | bytes 18436
  21.3 50.5 %all-to-all-start = ((f32[64,1,4112]{2,1,0:T(1,128)}), f32[64,1,4112]{2,1,0:T(1,128)S(1)}, u32[]{:S(2)}, u32[]{:S(2)}) async-start(f32[64,1,4112]{2,1,0:T(1,128)} %all_to_all.26), calls=%async_computation | async-start | bytes 2162688 | tf_op jit(solution)/shard_map/all_to_all | solution.py:120
  74.2 38.2 %all-to-all-start.1 = ((f32[64,1,4112]{2,1,0:T(1,128)}), f32[64,1,4112]{2,1,0:T(1,128)S(1)}, u32[]{:S(2)}, u32[]{:S(2)}) async-start(f32[64,1,4112]{2,1,0:T(1,128)} %broadcast_in_dim.8), calls=%async_computation.1 | async-start | bytes 2162688 | tf_op jit(solution)/shard_map/all_to_all | solution.py:123
  88.5 24.7 %copy-start.9 = (f32[256]{0:T(256)S(1)}, f32[256]{0:T(256)}, u32[]{:S(2)}) copy-start(f32[256]{0:T(256)} %param.21) | copy-start | bytes 3076
  113.2 2.2 %copy-start.2 = (bf16[2048,1024]{0,1:T(8,128)(2,1)S(1)}, bf16[2048,1024]{0,1:T(8,128)(2,1)}, u32[]{:S(2)}) copy-start(bf16[2048,1024]{0,1:T(8,128)(2,1)} %copy-done.1) | copy-start | bytes 12582916
  115.4 2.2 %copy-start.4 = (bf16[2048,1024]{1,0:T(8,128)(2,1)S(1)}, bf16[2048,1024]{1,0:T(8,128)(2,1)}, u32[]{:S(2)}) copy-start(bf16[2048,1024]{1,0:T(8,128)(2,1)} %copy.30) | copy-start | bytes 12582916
  130.0 32.2 %copy-start.12 = (f32[256]{0:T(256)S(1)}, f32[256]{0:T(256)}, u32[]{:S(2)}) copy-start(f32[256]{0:T(256)} %param.22) | copy-start | bytes 3076
  130.0 33.2 %copy-start.11 = (f32[256]{0:T(256)S(1)}, f32[256]{0:T(256)}, u32[]{:S(2)}) copy-start(f32[256]{0:T(256)} %param.24) | copy-start | bytes 3076
  131.2 30.1 %all-to-all-start.3 = ((f32[4,264,256]{2,1,0:T(8,128)}), f32[4,264,256]{2,1,0:T(8,128)S(1)}, u32[]{:S(2)}, u32[]{:S(2)}) async-start(f32[4,264,256]{2,1,0:T(8,128)} %reduce_sum.82), calls=%async_computation.3 | async-start | bytes 2162688 | tf_op jit(solution)/shard_map/all_to_all | solution.py:129

commit v10 on v9

--- a/solution.py
+++ b/solution.py
@@ -81,17 +81,15 @@
 
 
 def student_charge(features, species, live_mask, w_student, species_embed, w_charge, species_bias):
-    onehot = (
-        species[:, None] == jnp.arange(species_embed.shape[0], dtype=jnp.int32)[None, :]
-    ).astype(jnp.float32)
-    inner_sum = jnp.dot(features, w_student, preferred_element_type=jnp.float32) + jnp.dot(
-        onehot, species_embed, precision=HIGHEST_PRECISION
-    )
+    embed = jnp.zeros((features.shape[0], species_embed.shape[1]), jnp.float32)
+    bias = jnp.zeros((features.shape[0],), jnp.float32)
+    for kind in range(species_embed.shape[0]):
+        chosen = species == kind
+        embed = embed + jnp.where(chosen[:, None], species_embed[kind][None, :], 0.0)
+        bias = bias + jnp.where(chosen, species_bias[kind], 0.0)
+    inner_sum = jnp.dot(features, w_student, preferred_element_type=jnp.float32) + embed
     hidden = jax.nn.silu(inner_sum)
-    return (
-        jnp.dot(hidden, w_charge, precision=HIGHEST_PRECISION)
-        + jnp.dot(onehot, species_bias, precision=HIGHEST_PRECISION)
-    ) * live_mask
+    return (jnp.dot(hidden, w_charge, precision=HIGHEST_PRECISION) + bias) * live_mask
 
 
 def finish(

time: 197 us -> 203 us (1.030)
  other arithmetic: 16.5 us -> 21.6 us
    convert_element_type x1, other arithmetic: 0.01 us -> 5.07 us  [local(): charge_low = charge.astype(jnp.bfloat16)]
where the time goes in v10:
time: 203 us; the launch traced here: 202 us
  waiting for transfers between devices  79.9 us (39%)
  blocking collectives  36 us (18%)
  starting transfers between devices  31.4 us (15%)
  other arithmetic  21.6 us (11%)
  local copies, waits for them, and re-layouts  15.2 us (7%)
  matrix products  13.3 us (7%)
  between operations  4.9 us (2%)
    all_to_all x1, waiting for transfers between devices, sum_over_atoms(): parts = lax.all_to_all(payload, ATOM_AXES, 0, 0, tiled=True)  30.7 us
    all_to_all x1, waiting for transfers between devices, sum_over_ka(): parts = lax.all_to_all(chip, 'zl', 0, 0, tiled=True)  25.9 us
    all_to_all x1, waiting for transfers between devices, sum_over_atoms(): return lax.all_to_all(spread, ATOM_AXES, 0, 0, tiled=True)  23.4 us
    all_to_all x1, blocking collectives, sum_over_all(): lax.all_to_all(copies, ALL_AXES[:-1], 0, 0, tiled=True)  22 us
    all_to_all x1, starting transfers between devices, sum_over_atoms(): parts = lax.all_to_all(payload, ATOM_AXES, 0, 0, tiled=True)  19.6 us
    all_to_all x1, blocking collectives, sum_over_ka(): parts = lax.all_to_all(payload, 'core', 1, 1, tiled=True)  9.29 us
    all_to_all x1, starting transfers between devices, sum_over_atoms(): return lax.all_to_all(spread, ATOM_AXES, 0, 0, tiled=True)  7.7 us
    another operation x4, other arithmetic  7.39 us
  transfers between devices with their start and end apart: 3, of which 3 were waited for; matrix products, arithmetic and copies ran while one was open for 3% of the time, Pallas kernels for 0%

profile of v10, /device:TPU:1, one launch (start us, length us, event | category | flops | bytes accessed | tf_op | source)
XLA Modules:
  0.0 202.4 jit_solution(5157223719978852708)
XLA Ops:
  2.3 7.3 %fusion.3 = (bf16[2048,512]{0,1:T(8,128)(2,1)S(1)}, bf16[2048,512]{0,1:T(8,128)(2,1)S(1)}) fusion(f32[512]{0:T(512)S(1)} %bitcast.138, f32[2048]{0:T(1024)S(1)} %bitcast.134, f32[512]{0:T(512)S(1)} %bitcast.139, f32[2048]{0:T(1024)S(1)} %bitcast.135, f32[512]{0:T(512)S(1)} %bitcast.137, f32[2048]{0:T(1024)S(1)} %bitcast.133), kind=kLoop, calls=%fused_computation.8 | loop fusion | flops 47185920 | bytes 4225024 | tf_op jit(solution)/shard_map/convert.10
  12.0 2.2 %convolution_add_fusion = f32[2048,128]{1,0:T(8,128)S(1)} fusion(bf16[2048,256]{1,0:T(8,128)(2,1)S(1)} %copy-done.4, bf16[256,128]{1,0:T(8,128)(2,1)S(1)} %copy-done.12, f32[128]{0:T(128)S(1)} %get-tuple-element.59, f32[128]{0:T(128)S(1)} %get-tuple-element.60, f32[128]{0:T(128)S(1)} %get-tuple-element.54, f32[128]{0:T(128)S(1)} %get-tuple-element.55, ...), kind=kOutput, calls=%fused_computation.27 | convolution fusion | flops 138412032 | bytes 2183168 | tf_op jit(solution)/shard_map/dot_general | solution.py:90
  14.2 1.2 fusion.17
  15.4 5.1 %fusion.80 = (bf16[2048]{0:T(1024)(128)(2,1)S(1)}, f32[2048]{0:T(1024)S(1)}) fusion(f32[2048]{0:T(1024)S(1)} %bitcast.140, pred[2048]{0:T(1024)(128)(4,1)S(1)} %get-tuple-element.48, f32[]{:T(128)} %bitcast.27, pred[2048]{0:T(1024)(128)(4,1)S(1)} %get-tuple-element.49, f32[]{:T(128)} %bitcast.26, pred[2048]{0:T(1024)(128)(4,1)S(1)} %get-tuple-element.43, ...), kind=kLoop, calls=%fused_computation.146 | loop fusion | flops 38912 | bytes 36900 | tf_op jit(solution)/shard_map/convert_element_type | solution.py:173
  20.5 1.2 fusion.89
  21.8 3.6 %fusion.23 = f32[1024,256]{1,0:T(8,128)S(1)} fusion(bf16[2048,1024]{0,1:T(8,128)(2,1)} %copy-done.1, bf16[2048,256]{1,0:T(8,128)(2,1)S(1)} %copy-done.4, bf16[2048]{0:T(1024)(128)(2,1)S(1)} %get-tuple-element.75), kind=kOutput, calls=%fused_computation.42 | convolution fusion | flops 1074266112 | bytes 6295552 | tf_op jit(solution)/shard_map/dot_general | solution.py:175
  25.7 1.7 all_to_all.26
  27.4 19.6 %all-to-all-start = ((f32[64,1,4112]{2,1,0:T(1,128)}), f32[64,1,4112]{2,1,0:T(1,128)S(1)}, u32[]{:S(2)}, u32[]{:S(2)}) async-start(f32[64,1,4112]{2,1,0:T(1,128)} %all_to_all.26), calls=%async_computation | async-start | bytes 2162688 | tf_op jit(solution)/shard_map/all_to_all | solution.py:118
  47.3 30.7 %all-to-all-done = f32[64,1,4112]{2,1,0:T(1,128)S(1)} async-done(((f32[64,1,4112]{2,1,0:T(1,128)}), f32[64,1,4112]{2,1,0:T(1,128)S(1)}, u32[]{:S(2)}, u32[]{:S(2)}) %all-to-all-start) | async-done | bytes 1052704 | tf_op jit(solution)/shard_map/all_to_all | solution.py:118
  78.6 1.6 broadcast_in_dim.220
  80.2 7.7 %all-to-all-start.1 = ((f32[64,1,4112]{2,1,0:T(1,128)}), f32[64,1,4112]{2,1,0:T(1,128)S(1)}, u32[]{:S(2)}, u32[]{:S(2)}) async-start(f32[64,1,4112]{2,1,0:T(1,128)} %broadcast_in_dim.220), calls=%async_computation.1 | async-start | bytes 2162688 | tf_op jit(solution)/shard_map/all_to_all | solution.py:121
  87.9 6.4 %copy.30 = bf16[2048,1024]{1,0:T(8,128)(2,1)} copy(bf16[2048,1024]{0,1:T(8,128)(2,1)} %copy-done.1) | data formatting | bytes 8388608 | tf_op jit(solution)/shard_map/dot_general | solution.py:198
  95.1 23.4 %all-to-all-done.1 = f32[64,1,4112]{2,1,0:T(1,128)S(1)} async-done(((f32[64,1,4112]{2,1,0:T(1,128)}), f32[64,1,4112]{2,1,0:T(1,128)S(1)}, u32[]{:S(2)}, u32[]{:S(2)}) %all-to-all-start.1) | async-done | bytes 1052704 | tf_op jit(solution)/shard_map/all_to_all | solution.py:121
  119.3 1.3 fusion.15
  121.5 1.5 subtract_convert_fusion
  123.7 1.3 fusion.90
  126.8 9.3 %all_to_all.40 = f32[4,2,264,256]{3,2,0,1:T(8,128)S(1)} all-to-all(f32[4,2,264,256]{3,2,0,1:T(8,128)S(1)} %copy.27), channel_id=1, replica_groups=mesh['y'=8,'x'=4,'zh'=2,'zl'=4,'core'=2] {'core'}, dimensions={1} | all-to-all | bytes 4325376 | tf_op jit(solution)/shard_map/all_to_all | solution.py:125
  136.1 1.2 reduce_sum.82
  137.3 4.2 %all-to-all-start.3 = ((f32[4,264,256]{2,1,0:T(8,128)}), f32[4,264,256]{2,1,0:T(8,128)S(1)}, u32[]{:S(2)}, u32[]{:S(2)}) async-start(f32[4,264,256]{2,1,0:T(8,128)} %reduce_sum.82), calls=%async_computation.3 | async-start | bytes 2162688 | tf_op jit(solution)/shard_map/all_to_all | solution.py:127
  141.6 25.9 %all-to-all-done.3 = f32[4,264,256]{2,1,0:T(8,128)S(1)} async-done(((f32[4,264,256]{2,1,0:T(8,128)}), f32[4,264,256]{2,1,0:T(8,128)S(1)}, u32[]{:S(2)}, u32[]{:S(2)}) %all-to-all-start.3) | async-done | bytes 1081376 | tf_op jit(solution)/shard_map/all_to_all | solution.py:127
  169.5 1.3 multiply_reduce_fusion.2
  170.9 1.3 pad_maximum_fusion.4
  172.2 4.7 %all_to_all.41 = f32[2,1,2]{2,1,0:T(1,128)S(1)} all-to-all(f32[2,1,2]{2,1,0:T(1,128)S(1)} %broadcast_in_dim.222), channel_id=1, replica_groups=mesh['y'=8,'x'=4,'zh'=2,'zl'=4,'core'=2] {'core'}, dimensions={0} | all-to-all | bytes 32 | tf_op jit(solution)/shard_map/all_to_all | solution.py:133
  177.1 22.0 %all_to_all.42 = f32[256,1,2]{2,1,0:T(1,128)S(1)} all-to-all(f32[256,1,2]{2,1,0:T(1,128)S(1)} %broadcast_in_dim.223), channel_id=1, replica_groups=mesh['y'=8,'x'=4,'zh'=2,'zl'=4,'core'=2] {'y','x','zh','zl'}, dimensions={0} | all-to-all | bytes 4096 | tf_op jit(solution)/shard_map/all_to_all | solution.py:138
  (83 shorter events, 11.7 us)
Async XLA Ops:
  0.6 167.7 %copy-start = (bf16[256,256]{1,0:T(8,128)(2,1)S(1)}, bf16[256,256]{1,0:T(8,128)(2,1)}, u32[]{:S(2)}) copy-start(bf16[256,256]{1,0:T(8,128)(2,1)} %param.23) | copy-start | bytes 393220
  9.7 0.7 copy-start.10
  9.7 0.7 copy-start.7
  9.7 0.7 copy-start.6
  9.7 2.2 %copy-start.4 = (bf16[2048,256]{1,0:T(8,128)(2,1)S(1)}, bf16[2048,256]{1,0:T(8,128)(2,1)}, u32[]{:S(2)}) copy-start(bf16[2048,256]{1,0:T(8,128)(2,1)} %param.15) | copy-start | bytes 3145732
  9.7 2.2 %copy-start.12 = (bf16[256,128]{1,0:T(8,128)(2,1)S(1)}, bf16[256,128]{1,0:T(8,128)(2,1)}, u32[]{:S(2)}) copy-start(bf16[256,128]{1,0:T(8,128)(2,1)} %param.25) | copy-start | bytes 196612
  10.4 10.2 %copy-start.1 = (bf16[2048,1024]{0,1:T(8,128)(2,1)}, bf16[2048,1024]{0,1:T(8,128)(2,1)S(1)}, u32[]{:S(2)}) copy-start(bf16[2048,1024]{0,1:T(8,128)(2,1)S(1)} %pad_maximum_fusion) | copy-start | bytes 12582916
  10.4 3.8 %copy-start.14 = (f32[128]{0:T(128)S(1)}, f32[128]{0:T(128)}, u32[]{:S(2)}) copy-start(f32[128]{0:T(128)} %param.27) | copy-start | bytes 1540
  25.4 21.6 %copy-start.9 = (f32[256]{0:T(256)S(1)}, f32[256]{0:T(256)}, u32[]{:S(2)}) copy-start(f32[256]{0:T(256)} %param.20) | copy-start | bytes 3076
  25.4 21.7 %copy-start.5 = (s32[3,512]{1,0:T(4,128)S(1)}, s32[3,512]{1,0:T(4,128)}, u32[]{:S(2)}) copy-start(s32[3,512]{1,0:T(4,128)} %param.17) | copy-start | bytes 18436
  27.4 50.5 %all-to-all-start = ((f32[64,1,4112]{2,1,0:T(1,128)}), f32[64,1,4112]{2,1,0:T(1,128)S(1)}, u32[]{:S(2)}, u32[]{:S(2)}) async-start(f32[64,1,4112]{2,1,0:T(1,128)} %all_to_all.26), calls=%async_computation | async-start | bytes 2162688 | tf_op jit(solution)/shard_map/all_to_all | solution.py:118
  80.2 38.2 %all-to-all-start.1 = ((f32[64,1,4112]{2,1,0:T(1,128)}), f32[64,1,4112]{2,1,0:T(1,128)S(1)}, u32[]{:S(2)}, u32[]{:S(2)}) async-start(f32[64,1,4112]{2,1,0:T(1,128)} %broadcast_in_dim.220), calls=%async_computation.1 | async-start | bytes 2162688 | tf_op jit(solution)/shard_map/all_to_all | solution.py:121
  94.4 24.9 %copy-start.8 = (f32[256]{0:T(256)S(1)}, f32[256]{0:T(256)}, u32[]{:S(2)}) copy-start(f32[256]{0:T(256)} %param.21) | copy-start | bytes 3076
  119.3 2.2 %copy-start.2 = (bf16[2048,1024]{0,1:T(8,128)(2,1)S(1)}, bf16[2048,1024]{0,1:T(8,128)(2,1)}, u32[]{:S(2)}) copy-start(bf16[2048,1024]{0,1:T(8,128)(2,1)} %copy-done.1) | copy-start | bytes 12582916
  121.5 2.2 %copy-start.3 = (bf16[2048,1024]{1,0:T(8,128)(2,1)S(1)}, bf16[2048,1024]{1,0:T(8,128)(2,1)}, u32[]{:S(2)}) copy-start(bf16[2048,1024]{1,0:T(8,128)(2,1)} %copy.30) | copy-start | bytes 12582916
  136.1 32.2 %copy-start.13 = (f32[256]{0:T(256)S(1)}, f32[256]{0:T(256)}, u32[]{:S(2)}) copy-start(f32[256]{0:T(256)} %param.22) | copy-start | bytes 3076
  136.1 33.2 %copy-start.11 = (f32[256]{0:T(256)S(1)}, f32[256]{0:T(256)}, u32[]{:S(2)}) copy-start(f32[256]{0:T(256)} %param.24) | copy-start | bytes 3076
  137.3 30.2 %all-to-all-start.3 = ((f32[4,264,256]{2,1,0:T(8,128)}), f32[4,264,256]{2,1,0:T(8,128)S(1)}, u32[]{:S(2)}, u32[]{:S(2)}) async-start(f32[4,264,256]{2,1,0:T(8,128)} %reduce_sum.82), calls=%async_computation.3 | async-start | bytes 2162688 | tf_op jit(solution)/shard_map/all_to_all | solution.py:127

commit v11 on v9

--- a/solution.py
+++ b/solution.py
@@ -89,7 +89,7 @@
     )
     hidden = jax.nn.silu(inner_sum)
     return (
-        jnp.dot(hidden, w_charge, precision=HIGHEST_PRECISION)
+        jnp.sum(hidden * w_charge[None, :], axis=1)
         + jnp.dot(onehot, species_bias, precision=HIGHEST_PRECISION)
     ) * live_mask
 

time: 197 us -> 196 us (level)
  no operation moved by 1% of the time
where the time goes in v11:
time: 196 us
  waiting for transfers between devices  79.7 us (41%)
  blocking collectives  36 us (18%)
  starting transfers between devices  31.6 us (16%)
  other arithmetic  16.6 us (8%)
  local copies, waits for them, and re-layouts  14.4 us (7%)
  matrix products  12.4 us (6%)
  between operations  4.93 us (3%)
    all_to_all x1, waiting for transfers between devices, sum_over_atoms(): parts = lax.all_to_all(payload, ATOM_AXES, 0, 0, tiled=True)  30.7 us
    all_to_all x1, waiting for transfers between devices, sum_over_ka(): parts = lax.all_to_all(chip, 'zl', 0, 0, tiled=True)  25.9 us
    all_to_all x1, waiting for transfers between devices, sum_over_atoms(): return lax.all_to_all(spread, ATOM_AXES, 0, 0, tiled=True)  23.1 us
    all_to_all x1, blocking collectives, sum_over_all(): lax.all_to_all(copies, ALL_AXES[:-1], 0, 0, tiled=True)  22 us
    all_to_all x1, starting transfers between devices, sum_over_atoms(): parts = lax.all_to_all(payload, ATOM_AXES, 0, 0, tiled=True)  19.6 us
    all_to_all x1, blocking collectives, sum_over_ka(): parts = lax.all_to_all(payload, 'core', 1, 1, tiled=True)  9.3 us
    all_to_all x1, starting transfers between devices, sum_over_atoms(): return lax.all_to_all(spread, ATOM_AXES, 0, 0, tiled=True)  7.88 us
    another operation x4, other arithmetic  7.39 us
  transfers between devices with their start and end apart: 3, of which 3 were waited for; matrix products, arithmetic and copies ran while one was open for 3% of the time, Pallas kernels for 0%

profile of v11, /device:TPU:1, one launch (start us, length us, event | category | flops | bytes accessed | tf_op | source)
XLA Modules:
  0.0 195.6 jit_solution(7379498263253738042)
XLA Ops:
  1.4 0.9 fusion.77
  2.3 7.3 %fusion.3 = (bf16[2048,512]{0,1:T(8,128)(2,1)S(1)}, bf16[2048,512]{0,1:T(8,128)(2,1)S(1)}) fusion(f32[512]{0:T(512)S(1)} %bitcast.115, f32[2048]{0:T(1024)S(1)} %bitcast.111, f32[512]{0:T(512)S(1)} %bitcast.116, f32[2048]{0:T(1024)S(1)} %bitcast.112, f32[512]{0:T(512)S(1)} %bitcast.114, f32[2048]{0:T(1024)S(1)} %bitcast.110), kind=kLoop, calls=%fused_computation.8 | loop fusion | flops 47185920 | bytes 4225024 | tf_op jit(solution)/shard_map/convert.10
  12.3 1.3 multiply_reduce_fusion
  13.6 1.2 fusion.84
  14.9 3.6 %fusion.18 = f32[1024,256]{1,0:T(8,128)S(1)} fusion(bf16[2048,1024]{0,1:T(8,128)(2,1)} %copy-done.1, bf16[2048,256]{1,0:T(8,128)(2,1)S(1)} %copy-done.3, bf16[2048]{0:T(1024)(128)(2,1)S(1)} %get-tuple-element.51), kind=kOutput, calls=%fused_computation.39 | convolution fusion | flops 1074266112 | bytes 6295552 | tf_op jit(solution)/shard_map/dot_general | solution.py:177
  18.8 1.7 all_to_all.26
  20.5 19.6 %all-to-all-start = ((f32[64,1,4112]{2,1,0:T(1,128)}), f32[64,1,4112]{2,1,0:T(1,128)S(1)}, u32[]{:S(2)}, u32[]{:S(2)}) async-start(f32[64,1,4112]{2,1,0:T(1,128)} %all_to_all.26), calls=%async_computation | async-start | bytes 2162688 | tf_op jit(solution)/shard_map/all_to_all | solution.py:120
  40.3 30.7 %all-to-all-done = f32[64,1,4112]{2,1,0:T(1,128)S(1)} async-done(((f32[64,1,4112]{2,1,0:T(1,128)}), f32[64,1,4112]{2,1,0:T(1,128)S(1)}, u32[]{:S(2)}, u32[]{:S(2)}) %all-to-all-start) | async-done | bytes 1052704 | tf_op jit(solution)/shard_map/all_to_all | solution.py:120
  71.7 1.6 broadcast_in_dim.8
  73.3 7.9 %all-to-all-start.1 = ((f32[64,1,4112]{2,1,0:T(1,128)}), f32[64,1,4112]{2,1,0:T(1,128)S(1)}, u32[]{:S(2)}, u32[]{:S(2)}) async-start(f32[64,1,4112]{2,1,0:T(1,128)} %broadcast_in_dim.8), calls=%async_computation.1 | async-start | bytes 2162688 | tf_op jit(solution)/shard_map/all_to_all | solution.py:123
  81.2 6.5 %copy.30 = bf16[2048,1024]{1,0:T(8,128)(2,1)} copy(bf16[2048,1024]{0,1:T(8,128)(2,1)} %copy-done.1) | data formatting | bytes 8388608 | tf_op jit(solution)/shard_map/dot_general | solution.py:200
  88.4 23.1 %all-to-all-done.1 = f32[64,1,4112]{2,1,0:T(1,128)S(1)} async-done(((f32[64,1,4112]{2,1,0:T(1,128)}), f32[64,1,4112]{2,1,0:T(1,128)S(1)}, u32[]{:S(2)}, u32[]{:S(2)}) %all-to-all-start.1) | async-done | bytes 1052704 | tf_op jit(solution)/shard_map/all_to_all | solution.py:123
  112.4 1.3 fusion.15
  114.6 1.5 subtract_convert_fusion
  116.8 1.3 fusion.85
  119.9 9.3 %all_to_all.40 = f32[4,2,264,256]{3,2,0,1:T(8,128)S(1)} all-to-all(f32[4,2,264,256]{3,2,0,1:T(8,128)S(1)} %copy.27), channel_id=1, replica_groups=mesh['y'=8,'x'=4,'zh'=2,'zl'=4,'core'=2] {'core'}, dimensions={1} | all-to-all | bytes 4325376 | tf_op jit(solution)/shard_map/all_to_all | solution.py:127
  129.2 1.2 reduce_sum.92
  130.4 4.2 %all-to-all-start.3 = ((f32[4,264,256]{2,1,0:T(8,128)}), f32[4,264,256]{2,1,0:T(8,128)S(1)}, u32[]{:S(2)}, u32[]{:S(2)}) async-start(f32[4,264,256]{2,1,0:T(8,128)} %reduce_sum.92), calls=%async_computation.3 | async-start | bytes 2162688 | tf_op jit(solution)/shard_map/all_to_all | solution.py:129
  134.6 25.9 %all-to-all-done.3 = f32[4,264,256]{2,1,0:T(8,128)S(1)} async-done(((f32[4,264,256]{2,1,0:T(8,128)}), f32[4,264,256]{2,1,0:T(8,128)S(1)}, u32[]{:S(2)}, u32[]{:S(2)}) %all-to-all-start.3) | async-done | bytes 1081376 | tf_op jit(solution)/shard_map/all_to_all | solution.py:129
  161.4 0.9 fusion.82
  162.6 1.4 multiply_reduce_fusion.3
  164.0 1.4 pad_maximum_fusion.4
  165.4 4.7 %all_to_all.41 = f32[2,1,2]{2,1,0:T(1,128)S(1)} all-to-all(f32[2,1,2]{2,1,0:T(1,128)S(1)} %broadcast_in_dim.10), channel_id=1, replica_groups=mesh['y'=8,'x'=4,'zh'=2,'zl'=4,'core'=2] {'core'}, dimensions={0} | all-to-all | bytes 32 | tf_op jit(solution)/shard_map/all_to_all | solution.py:135
  170.2 22.0 %all_to_all.42 = f32[256,1,2]{2,1,0:T(1,128)S(1)} all-to-all(f32[256,1,2]{2,1,0:T(1,128)S(1)} %broadcast_in_dim.11), channel_id=1, replica_groups=mesh['y'=8,'x'=4,'zh'=2,'zl'=4,'core'=2] {'y','x','zh','zl'}, dimensions={0} | all-to-all | bytes 4096 | tf_op jit(solution)/shard_map/all_to_all | solution.py:140
  (81 shorter events, 10.2 us)
Async XLA Ops:
  0.6 160.8 %copy-start = (bf16[256,256]{1,0:T(8,128)(2,1)S(1)}, bf16[256,256]{1,0:T(8,128)(2,1)}, u32[]{:S(2)}) copy-start(bf16[256,256]{1,0:T(8,128)(2,1)} %param.23) | copy-start | bytes 393220
  9.7 1.3 copy-start.3
  9.7 1.3 copy-start.5
  9.7 1.8 copy-start.10
  9.7 1.8 copy-start.13
  9.7 2.5 %copy-start.11 = (f32[8,128]{1,0:T(8,128)S(1)}, f32[8,128]{1,0:T(8,128)}, u32[]{:S(2)}) copy-start(f32[8,128]{1,0:T(8,128)} %param.26) | copy-start | bytes 12292
  9.7 2.5 %copy-start.14 = (f32[128]{0:T(128)S(1)}, f32[128]{0:T(128)}, u32[]{:S(2)}) copy-start(f32[128]{0:T(128)} %param.27) | copy-start | bytes 1540
  10.3 4.5 %copy-start.1 = (bf16[2048,1024]{0,1:T(8,128)(2,1)}, bf16[2048,1024]{0,1:T(8,128)(2,1)S(1)}, u32[]{:S(2)}) copy-start(bf16[2048,1024]{0,1:T(8,128)(2,1)S(1)} %pad_maximum_fusion) | copy-start | bytes 12582916
  18.5 21.6 %copy-start.8 = (f32[256]{0:T(256)S(1)}, f32[256]{0:T(256)}, u32[]{:S(2)}) copy-start(f32[256]{0:T(256)} %param.20) | copy-start | bytes 3076
  18.5 21.6 %copy-start.6 = (s32[3,512]{1,0:T(4,128)S(1)}, s32[3,512]{1,0:T(4,128)}, u32[]{:S(2)}) copy-start(s32[3,512]{1,0:T(4,128)} %param.17) | copy-start | bytes 18436
  20.5 50.5 %all-to-all-start = ((f32[64,1,4112]{2,1,0:T(1,128)}), f32[64,1,4112]{2,1,0:T(1,128)S(1)}, u32[]{:S(2)}, u32[]{:S(2)}) async-start(f32[64,1,4112]{2,1,0:T(1,128)} %all_to_all.26), calls=%async_computation | async-start | bytes 2162688 | tf_op jit(solution)/shard_map/all_to_all | solution.py:120
  73.3 38.2 %all-to-all-start.1 = ((f32[64,1,4112]{2,1,0:T(1,128)}), f32[64,1,4112]{2,1,0:T(1,128)S(1)}, u32[]{:S(2)}, u32[]{:S(2)}) async-start(f32[64,1,4112]{2,1,0:T(1,128)} %broadcast_in_dim.8), calls=%async_computation.1 | async-start | bytes 2162688 | tf_op jit(solution)/shard_map/all_to_all | solution.py:123
  87.7 24.7 %copy-start.7 = (f32[256]{0:T(256)S(1)}, f32[256]{0:T(256)}, u32[]{:S(2)}) copy-start(f32[256]{0:T(256)} %param.21) | copy-start | bytes 3076
  112.4 2.2 %copy-start.2 = (bf16[2048,1024]{0,1:T(8,128)(2,1)S(1)}, bf16[2048,1024]{0,1:T(8,128)(2,1)}, u32[]{:S(2)}) copy-start(bf16[2048,1024]{0,1:T(8,128)(2,1)} %copy-done.1) | copy-start | bytes 12582916
  114.6 2.2 %copy-start.4 = (bf16[2048,1024]{1,0:T(8,128)(2,1)S(1)}, bf16[2048,1024]{1,0:T(8,128)(2,1)}, u32[]{:S(2)}) copy-start(bf16[2048,1024]{1,0:T(8,128)(2,1)} %copy.30) | copy-start | bytes 12582916
  129.2 32.2 %copy-start.12 = (f32[256]{0:T(256)S(1)}, f32[256]{0:T(256)}, u32[]{:S(2)}) copy-start(f32[256]{0:T(256)} %param.22) | copy-start | bytes 3076
  129.2 33.2 %copy-start.9 = (f32[256]{0:T(256)S(1)}, f32[256]{0:T(256)}, u32[]{:S(2)}) copy-start(f32[256]{0:T(256)} %param.24) | copy-start | bytes 3076
  130.4 30.1 %all-to-all-start.3 = ((f32[4,264,256]{2,1,0:T(8,128)}), f32[4,264,256]{2,1,0:T(8,128)S(1)}, u32[]{:S(2)}, u32[]{:S(2)}) async-start(f32[4,264,256]{2,1,0:T(8,128)} %reduce_sum.92), calls=%async_computation.3 | async-start | bytes 2162688 | tf_op jit(solution)/shard_map/all_to_all | solution.py:129

commit v12 on v11

--- a/solution.py
+++ b/solution.py
@@ -101,7 +101,7 @@
     normed = (potential * lax.rsqrt(mean_square + 1e-06) * norm_gain[None, :]).astype(jnp.bfloat16)
     update = jax.nn.silu(jnp.dot(normed, w_mix, preferred_element_type=jnp.float32))
     combined = features.astype(jnp.float32) + update
-    teacher_energy = jnp.dot(combined, w_read, precision=HIGHEST_PRECISION)
+    teacher_energy = jnp.sum(combined * w_read[None, :], axis=1)
     student_energy = 0.5 * charge * student_part[:, 0]
     forces = charge[:, None] * student_part[:, 1:4]
     misfit = (student_energy - teacher_energy) ** 2 + jnp.sum(

time: 196 us -> 196 us (level)
  blocking collectives: 36 us -> 14 us
  waiting for transfers between devices: 79.7 us -> 91.1 us
  starting transfers between devices: 31.6 us -> 41.5 us
    all_to_all x1 -> x0, blocking collectives: 22 us -> none  [sum_over_all(): lax.all_to_all(copies, ALL_AXES[:-1], 0, 0, tiled=True)]
    all_to_all x0 -> x1, waiting for transfers between devices: none -> 11.5 us  [sum_over_all(): lax.all_to_all(copies, ALL_AXES[:-1], 0, 0, tiled=True)]
    all_to_all x0 -> x1, starting transfers between devices: none -> 9.9 us  [sum_over_all(): lax.all_to_all(copies, ALL_AXES[:-1], 0, 0, tiled=True)]
  transfers between devices with their start and end apart: 3 -> 4, of which waited for: 3 -> 4; matrix products, arithmetic and copies ran while one was open for 3% -> 4% of each run, Pallas kernels for 0% -> 0%
where the time goes in v12:
time: 196 us; the launch traced here: 195 us
  waiting for transfers between devices  91.1 us (46%)
  starting transfers between devices  41.5 us (21%)
  other arithmetic  16.4 us (8%)
  local copies, waits for them, and re-layouts  15.9 us (8%)
  blocking collectives  14 us (7%)
  matrix products  11.5 us (6%)
  between operations  4.83 us (2%)
    all_to_all x1, waiting for transfers between devices, sum_over_atoms(): parts = lax.all_to_all(payload, ATOM_AXES, 0, 0, tiled=True)  30.7 us
    all_to_all x1, waiting for transfers between devices, sum_over_ka(): parts = lax.all_to_all(chip, 'zl', 0, 0, tiled=True)  25.8 us
    all_to_all x1, waiting for transfers between devices, sum_over_atoms(): return lax.all_to_all(spread, ATOM_AXES, 0, 0, tiled=True)  23.2 us
    all_to_all x1, starting transfers between devices, sum_over_atoms(): parts = lax.all_to_all(payload, ATOM_AXES, 0, 0, tiled=True)  19.6 us
    all_to_all x1, waiting for transfers between devices, sum_over_all(): lax.all_to_all(copies, ALL_AXES[:-1], 0, 0, tiled=True)  11.5 us
    all_to_all x1, starting transfers between devices, sum_over_all(): lax.all_to_all(copies, ALL_AXES[:-1], 0, 0, tiled=True)  9.9 us
    all_to_all x1, blocking collectives, sum_over_ka(): parts = lax.all_to_all(payload, 'core', 1, 1, tiled=True)  9.3 us
    all_to_all x1, starting transfers between devices, sum_over_atoms(): return lax.all_to_all(spread, ATOM_AXES, 0, 0, tiled=True)  7.88 us
  transfers between devices with their start and end apart: 4, of which 4 were waited for; matrix products, arithmetic and copies ran while one was open for 4% of the time, Pallas kernels for 0%

profile of v12, /device:TPU:1, one launch (start us, length us, event | category | flops | bytes accessed | tf_op | source)
XLA Modules:
  0.0 195.3 jit_solution(13251248129560165411)
XLA Ops:
  1.4 0.9 fusion.77
  2.3 7.3 %fusion.3 = (bf16[2048,512]{0,1:T(8,128)(2,1)S(1)}, bf16[2048,512]{0,1:T(8,128)(2,1)S(1)}) fusion(f32[512]{0:T(512)S(1)} %bitcast.111, f32[2048]{0:T(1024)S(1)} %bitcast.107, f32[512]{0:T(512)S(1)} %bitcast.112, f32[2048]{0:T(1024)S(1)} %bitcast.108, f32[512]{0:T(512)S(1)} %bitcast.110, f32[2048]{0:T(1024)S(1)} %bitcast.106), kind=kLoop, calls=%fused_computation.8 | loop fusion | flops 47185920 | bytes 4225024 | tf_op jit(solution)/shard_map/convert.10
  12.3 1.3 multiply_reduce_fusion
  13.6 1.2 fusion.83
  14.9 3.6 %fusion.18 = f32[1024,256]{1,0:T(8,128)S(1)} fusion(bf16[2048,1024]{0,1:T(8,128)(2,1)} %copy-done.1, bf16[2048,256]{1,0:T(8,128)(2,1)S(1)} %copy-done.3, bf16[2048]{0:T(1024)(128)(2,1)S(1)} %get-tuple-element.77), kind=kOutput, calls=%fused_computation.39 | convolution fusion | flops 1074266112 | bytes 6295552 | tf_op jit(solution)/shard_map/dot_general | solution.py:177
  18.8 1.7 all_to_all.26
  20.5 19.6 %all-to-all-start = ((f32[64,1,4112]{2,1,0:T(1,128)}), f32[64,1,4112]{2,1,0:T(1,128)S(1)}, u32[]{:S(2)}, u32[]{:S(2)}) async-start(f32[64,1,4112]{2,1,0:T(1,128)} %all_to_all.26), calls=%async_computation | async-start | bytes 2162688 | tf_op jit(solution)/shard_map/all_to_all | solution.py:120
  40.3 30.7 %all-to-all-done = f32[64,1,4112]{2,1,0:T(1,128)S(1)} async-done(((f32[64,1,4112]{2,1,0:T(1,128)}), f32[64,1,4112]{2,1,0:T(1,128)S(1)}, u32[]{:S(2)}, u32[]{:S(2)}) %all-to-all-start) | async-done | bytes 1052704 | tf_op jit(solution)/shard_map/all_to_all | solution.py:120
  71.7 1.6 broadcast_in_dim.8
  73.3 7.9 %all-to-all-start.1 = ((f32[64,1,4112]{2,1,0:T(1,128)}), f32[64,1,4112]{2,1,0:T(1,128)S(1)}, u32[]{:S(2)}, u32[]{:S(2)}) async-start(f32[64,1,4112]{2,1,0:T(1,128)} %broadcast_in_dim.8), calls=%async_computation.1 | async-start | bytes 2162688 | tf_op jit(solution)/shard_map/all_to_all | solution.py:123
  81.2 6.4 %copy.40 = bf16[2048,1024]{1,0:T(8,128)(2,1)} copy(bf16[2048,1024]{0,1:T(8,128)(2,1)} %copy-done.1) | data formatting | bytes 8388608 | tf_op jit(solution)/shard_map/dot_general | solution.py:200
  88.4 23.2 %all-to-all-done.1 = f32[64,1,4112]{2,1,0:T(1,128)S(1)} async-done(((f32[64,1,4112]{2,1,0:T(1,128)}), f32[64,1,4112]{2,1,0:T(1,128)S(1)}, u32[]{:S(2)}, u32[]{:S(2)}) %all-to-all-start.1) | async-done | bytes 1052704 | tf_op jit(solution)/shard_map/all_to_all | solution.py:123
  112.4 1.3 fusion.15
  114.6 1.5 subtract_convert_fusion
  116.7 1.3 fusion.84
  119.8 9.3 %all_to_all.40 = f32[4,2,264,256]{3,2,0,1:T(8,128)S(1)} all-to-all(f32[4,2,264,256]{3,2,0,1:T(8,128)S(1)} %copy.36), channel_id=1, replica_groups=mesh['y'=8,'x'=4,'zh'=2,'zl'=4,'core'=2] {'core'}, dimensions={1} | all-to-all | bytes 4325376 | tf_op jit(solution)/shard_map/all_to_all | solution.py:127
  129.2 1.2 reduce_sum.101
  130.4 4.2 %all-to-all-start.3 = ((f32[4,264,256]{2,1,0:T(8,128)}), f32[4,264,256]{2,1,0:T(8,128)S(1)}, u32[]{:S(2)}, u32[]{:S(2)}) async-start(f32[4,264,256]{2,1,0:T(8,128)} %reduce_sum.101), calls=%async_computation.3 | async-start | bytes 2162688 | tf_op jit(solution)/shard_map/all_to_all | solution.py:129
  134.7 25.8 %all-to-all-done.3 = f32[4,264,256]{2,1,0:T(8,128)S(1)} async-done(((f32[4,264,256]{2,1,0:T(8,128)}), f32[4,264,256]{2,1,0:T(8,128)S(1)}, u32[]{:S(2)}, u32[]{:S(2)}) %all-to-all-start.3) | async-done | bytes 1081376 | tf_op jit(solution)/shard_map/all_to_all | solution.py:129
  161.8 1.2 multiply_reduce_fusion.4
  163.0 1.4 pad_maximum_fusion.4
  164.4 4.7 %all_to_all.41 = f32[2,1,2]{2,1,0:T(1,128)S(1)} all-to-all(f32[2,1,2]{2,1,0:T(1,128)S(1)} %broadcast_in_dim.10), channel_id=1, replica_groups=mesh['y'=8,'x'=4,'zh'=2,'zl'=4,'core'=2] {'core'}, dimensions={0} | all-to-all | bytes 32 | tf_op jit(solution)/shard_map/all_to_all | solution.py:135
  169.9 9.9 %all-to-all-start.5 = ((f32[256,1,2]{2,1,0:T(1,128)}), f32[256,1,2]{2,1,0:T(1,128)S(1)}, u32[]{:S(2)}, u32[]{:S(2)}) async-start(f32[256,1,2]{2,1,0:T(1,128)} %broadcast_in_dim.11), calls=%async_computation.5 | async-start | bytes 262144 | tf_op jit(solution)/shard_map/all_to_all | solution.py:140
  180.5 11.5 %all-to-all-done.5 = f32[256,1,2]{2,1,0:T(1,128)S(1)} async-done(((f32[256,1,2]{2,1,0:T(1,128)}), f32[256,1,2]{2,1,0:T(1,128)S(1)}, u32[]{:S(2)}, u32[]{:S(2)}) %all-to-all-start.5) | async-done | bytes 2080 | tf_op jit(solution)/shard_map/all_to_all | solution.py:140
  (84 shorter events, 11.8 us)
Async XLA Ops:
  0.6 160.7 %copy-start = (bf16[256,256]{1,0:T(8,128)(2,1)S(1)}, bf16[256,256]{1,0:T(8,128)(2,1)}, u32[]{:S(2)}) copy-start(bf16[256,256]{1,0:T(8,128)(2,1)} %param.23) | copy-start | bytes 393220
  9.7 1.3 copy-start.3
  9.7 1.3 copy-start.5
  9.7 1.8 copy-start.9
  9.7 1.8 copy-start.13
  9.7 2.5 %copy-start.10 = (f32[8,128]{1,0:T(8,128)S(1)}, f32[8,128]{1,0:T(8,128)}, u32[]{:S(2)}) copy-start(f32[8,128]{1,0:T(8,128)} %param.26) | copy-start | bytes 12292
  9.7 2.5 %copy-start.14 = (f32[128]{0:T(128)S(1)}, f32[128]{0:T(128)}, u32[]{:S(2)}) copy-start(f32[128]{0:T(128)} %param.27) | copy-start | bytes 1540
  10.3 4.5 %copy-start.1 = (bf16[2048,1024]{0,1:T(8,128)(2,1)}, bf16[2048,1024]{0,1:T(8,128)(2,1)S(1)}, u32[]{:S(2)}) copy-start(bf16[2048,1024]{0,1:T(8,128)(2,1)S(1)} %pad_maximum_fusion) | copy-start | bytes 12582916
  18.5 21.6 %copy-start.8 = (f32[256]{0:T(256)S(1)}, f32[256]{0:T(256)}, u32[]{:S(2)}) copy-start(f32[256]{0:T(256)} %param.20) | copy-start | bytes 3076
  18.5 21.6 %copy-start.6 = (s32[3,512]{1,0:T(4,128)S(1)}, s32[3,512]{1,0:T(4,128)}, u32[]{:S(2)}) copy-start(s32[3,512]{1,0:T(4,128)} %param.17) | copy-start | bytes 18436
  20.5 50.5 %all-to-all-start = ((f32[64,1,4112]{2,1,0:T(1,128)}), f32[64,1,4112]{2,1,0:T(1,128)S(1)}, u32[]{:S(2)}, u32[]{:S(2)}) async-start(f32[64,1,4112]{2,1,0:T(1,128)} %all_to_all.26), calls=%async_computation | async-start | bytes 2162688 | tf_op jit(solution)/shard_map/all_to_all | solution.py:120
  73.3 38.2 %all-to-all-start.1 = ((f32[64,1,4112]{2,1,0:T(1,128)}), f32[64,1,4112]{2,1,0:T(1,128)S(1)}, u32[]{:S(2)}, u32[]{:S(2)}) async-start(f32[64,1,4112]{2,1,0:T(1,128)} %broadcast_in_dim.8), calls=%async_computation.1 | async-start | bytes 2162688 | tf_op jit(solution)/shard_map/all_to_all | solution.py:123
  87.6 24.7 %copy-start.7 = (f32[256]{0:T(256)S(1)}, f32[256]{0:T(256)}, u32[]{:S(2)}) copy-start(f32[256]{0:T(256)} %param.21) | copy-start | bytes 3076
  112.4 2.2 %copy-start.2 = (bf16[2048,1024]{0,1:T(8,128)(2,1)S(1)}, bf16[2048,1024]{0,1:T(8,128)(2,1)}, u32[]{:S(2)}) copy-start(bf16[2048,1024]{0,1:T(8,128)(2,1)} %copy-done.1) | copy-start | bytes 12582916
  114.6 2.2 %copy-start.4 = (bf16[2048,1024]{1,0:T(8,128)(2,1)S(1)}, bf16[2048,1024]{1,0:T(8,128)(2,1)}, u32[]{:S(2)}) copy-start(bf16[2048,1024]{1,0:T(8,128)(2,1)} %copy.40) | copy-start | bytes 12582916
  129.1 32.2 %copy-start.11 = (f32[256]{0:T(256)S(1)}, f32[256]{0:T(256)}, u32[]{:S(2)}) copy-start(f32[256]{0:T(256)} %param.24) | copy-start | bytes 3076
  129.2 32.2 %copy-start.12 = (f32[256]{0:T(256)S(1)}, f32[256]{0:T(256)}, u32[]{:S(2)}) copy-start(f32[256]{0:T(256)} %param.22) | copy-start | bytes 3076
  130.4 30.1 %all-to-all-start.3 = ((f32[4,264,256]{2,1,0:T(8,128)}), f32[4,264,256]{2,1,0:T(8,128)S(1)}, u32[]{:S(2)}, u32[]{:S(2)}) async-start(f32[4,264,256]{2,1,0:T(8,128)} %reduce_sum.101), calls=%async_computation.3 | async-start | bytes 2162688 | tf_op jit(solution)/shard_map/all_to_all | solution.py:129
  169.9 22.2 %all-to-all-start.5 = ((f32[256,1,2]{2,1,0:T(1,128)}), f32[256,1,2]{2,1,0:T(1,128)S(1)}, u32[]{:S(2)}, u32[]{:S(2)}) async-start(f32[256,1,2]{2,1,0:T(1,128)} %broadcast_in_dim.11), calls=%async_computation.5 | async-start | bytes 262144 | tf_op jit(solution)/shard_map/all_to_all | solution.py:140

commit v13 on v12

--- a/solution.py
+++ b/solution.py
@@ -131,13 +131,11 @@
 
 
 def sum_over_all(values):
-    pair = jnp.broadcast_to(values[None, :], (lax.axis_size("core"), values.shape[0]))
-    chip = jnp.sum(lax.all_to_all(pair, "core", 0, 0, tiled=True), axis=0)
-    chips = 1
-    for axis in ALL_AXES[:-1]:
-        chips *= lax.axis_size(axis)
-    copies = jnp.broadcast_to(chip[None, :], (chips, values.shape[0]))
-    return jnp.sum(lax.all_to_all(copies, ALL_AXES[:-1], 0, 0, tiled=True), axis=0)
+    devices = 1
+    for axis in ALL_AXES:
+        devices *= lax.axis_size(axis)
+    copies = jnp.broadcast_to(values[None, :], (devices, values.shape[0]))
+    return jnp.sum(lax.all_to_all(copies, ALL_AXES, 0, 0, tiled=True), axis=0)
 
 
 def local(

time: 196 us -> 197 us (level)
  waiting for transfers between devices: 91.1 us -> 96.3 us
  blocking collectives: 14 us -> 9.3 us
    all_to_all x1, waiting for transfers between devices: 11.5 us -> 16.7 us  [sum_over_all(): return jnp.sum(lax.all_to_all(copies, ALL_AXES, 0, 0, tiled=True), axis=0)]
    all_to_all x1 -> x0, blocking collectives: 4.74 us -> none  [sum_over_all(): chip = jnp.sum(lax.all_to_all(pair, 'core', 0, 0, tiled=True), axis=0)]
where the time goes in v13:
time: 197 us; the launch traced here: 196 us
  waiting for transfers between devices  96.3 us (49%)
  starting transfers between devices  41.2 us (21%)
  other arithmetic  16.7 us (8%)
  local copies, waits for them, and re-layouts  16 us (8%)
  matrix products  11.5 us (6%)
  blocking collectives  9.3 us (5%)
  between operations  4.9 us (2%)
    all_to_all x1, waiting for transfers between devices, sum_over_atoms(): parts = lax.all_to_all(payload, ATOM_AXES, 0, 0, tiled=True)  30.7 us
    all_to_all x1, waiting for transfers between devices, sum_over_ka(): parts = lax.all_to_all(chip, 'zl', 0, 0, tiled=True)  25.8 us
    all_to_all x1, waiting for transfers between devices, sum_over_atoms(): return lax.all_to_all(spread, ATOM_AXES, 0, 0, tiled=True)  23.2 us
    all_to_all x1, starting transfers between devices, sum_over_atoms(): parts = lax.all_to_all(payload, ATOM_AXES, 0, 0, tiled=True)  19.6 us
    all_to_all x1, waiting for transfers between devices, sum_over_all(): return jnp.sum(lax.all_to_all(copies, ALL_AXES, 0, 0, tiled=True), axis=0)  16.7 us
    all_to_all x1, starting transfers between devices, sum_over_all(): return jnp.sum(lax.all_to_all(copies, ALL_AXES, 0, 0, tiled=True), axis=0)  9.59 us
    all_to_all x1, blocking collectives, sum_over_ka(): parts = lax.all_to_all(payload, 'core', 1, 1, tiled=True)  9.3 us
    all_to_all x1, starting transfers between devices, sum_over_atoms(): return lax.all_to_all(spread, ATOM_AXES, 0, 0, tiled=True)  7.88 us
  transfers between devices with their start and end apart: 4, of which 4 were waited for; matrix products, arithmetic and copies ran while one was open for 4% of the time, Pallas kernels for 0%

profile of v13, /device:TPU:1, one launch (start us, length us, event | category | flops | bytes accessed | tf_op | source)
XLA Modules:
  0.0 195.9 jit_solution(10878592179886281424)
XLA Ops:
  1.4 0.9 fusion.77
  2.3 7.3 %fusion.3 = (bf16[2048,512]{0,1:T(8,128)(2,1)S(1)}, bf16[2048,512]{0,1:T(8,128)(2,1)S(1)}) fusion(f32[512]{0:T(512)S(1)} %bitcast.110, f32[2048]{0:T(1024)S(1)} %bitcast.106, f32[512]{0:T(512)S(1)} %bitcast.111, f32[2048]{0:T(1024)S(1)} %bitcast.107, f32[512]{0:T(512)S(1)} %bitcast.109, f32[2048]{0:T(1024)S(1)} %bitcast.105), kind=kLoop, calls=%fused_computation.8 | loop fusion | flops 47185920 | bytes 4225024 | tf_op jit(solution)/shard_map/convert.10
  12.3 1.3 multiply_reduce_fusion
  13.6 1.2 fusion.83
  14.9 3.6 %fusion.18 = f32[1024,256]{1,0:T(8,128)S(1)} fusion(bf16[2048,1024]{0,1:T(8,128)(2,1)} %copy-done.1, bf16[2048,256]{1,0:T(8,128)(2,1)S(1)} %copy-done.3, bf16[2048]{0:T(1024)(128)(2,1)S(1)} %get-tuple-element.77), kind=kOutput, calls=%fused_computation.39 | convolution fusion | flops 1074266112 | bytes 6295552 | tf_op jit(solution)/shard_map/dot_general | solution.py:175
  18.8 1.7 all_to_all.22
  20.5 19.6 %all-to-all-start = ((f32[64,1,4112]{2,1,0:T(1,128)}), f32[64,1,4112]{2,1,0:T(1,128)S(1)}, u32[]{:S(2)}, u32[]{:S(2)}) async-start(f32[64,1,4112]{2,1,0:T(1,128)} %all_to_all.22), calls=%async_computation | async-start | bytes 2162688 | tf_op jit(solution)/shard_map/all_to_all | solution.py:120
  40.3 30.7 %all-to-all-done = f32[64,1,4112]{2,1,0:T(1,128)S(1)} async-done(((f32[64,1,4112]{2,1,0:T(1,128)}), f32[64,1,4112]{2,1,0:T(1,128)S(1)}, u32[]{:S(2)}, u32[]{:S(2)}) %all-to-all-start) | async-done | bytes 1052704 | tf_op jit(solution)/shard_map/all_to_all | solution.py:120
  71.7 1.6 broadcast_in_dim.6
  73.3 7.9 %all-to-all-start.1 = ((f32[64,1,4112]{2,1,0:T(1,128)}), f32[64,1,4112]{2,1,0:T(1,128)S(1)}, u32[]{:S(2)}, u32[]{:S(2)}) async-start(f32[64,1,4112]{2,1,0:T(1,128)} %broadcast_in_dim.6), calls=%async_computation.1 | async-start | bytes 2162688 | tf_op jit(solution)/shard_map/all_to_all | solution.py:123
  81.2 6.4 %copy.39 = bf16[2048,1024]{1,0:T(8,128)(2,1)} copy(bf16[2048,1024]{0,1:T(8,128)(2,1)} %copy-done.1) | data formatting | bytes 8388608 | tf_op jit(solution)/shard_map/dot_general | solution.py:198
  88.4 23.2 %all-to-all-done.1 = f32[64,1,4112]{2,1,0:T(1,128)S(1)} async-done(((f32[64,1,4112]{2,1,0:T(1,128)}), f32[64,1,4112]{2,1,0:T(1,128)S(1)}, u32[]{:S(2)}, u32[]{:S(2)}) %all-to-all-start.1) | async-done | bytes 1052704 | tf_op jit(solution)/shard_map/all_to_all | solution.py:123
  112.4 1.3 fusion.15
  113.7 0.9 copy-done.2
  114.6 1.5 subtract_convert_fusion
  116.8 1.3 fusion.84
  119.9 9.3 %all_to_all.34 = f32[4,2,264,256]{3,2,0,1:T(8,128)S(1)} all-to-all(f32[4,2,264,256]{3,2,0,1:T(8,128)S(1)} %copy.36), channel_id=1, replica_groups=mesh['y'=8,'x'=4,'zh'=2,'zl'=4,'core'=2] {'core'}, dimensions={1} | all-to-all | bytes 4325376 | tf_op jit(solution)/shard_map/all_to_all | solution.py:127
  129.2 1.2 reduce_sum.92
  130.4 4.2 %all-to-all-start.3 = ((f32[4,264,256]{2,1,0:T(8,128)}), f32[4,264,256]{2,1,0:T(8,128)S(1)}, u32[]{:S(2)}, u32[]{:S(2)}) async-start(f32[4,264,256]{2,1,0:T(8,128)} %reduce_sum.92), calls=%async_computation.3 | async-start | bytes 2162688 | tf_op jit(solution)/shard_map/all_to_all | solution.py:129
  134.8 25.8 %all-to-all-done.3 = f32[4,264,256]{2,1,0:T(8,128)S(1)} async-done(((f32[4,264,256]{2,1,0:T(8,128)}), f32[4,264,256]{2,1,0:T(8,128)S(1)}, u32[]{:S(2)}, u32[]{:S(2)}) %all-to-all-start.3) | async-done | bytes 1081376 | tf_op jit(solution)/shard_map/all_to_all | solution.py:129
  161.8 1.2 multiply_reduce_fusion.4
  163.0 1.4 pad_maximum_fusion.4
  165.2 9.6 %all-to-all-start.4 = ((f32[512,1,2]{2,1,0:T(1,128)}), f32[512,1,2]{2,1,0:T(1,128)S(1)}, u32[]{:S(2)}, u32[]{:S(2)}) async-start(f32[512,1,2]{2,1,0:T(1,128)} %broadcast_in_dim.8), calls=%async_computation.4 | async-start | bytes 524288 | tf_op jit(solution)/shard_map/all_to_all | solution.py:138
  175.6 16.7 %all-to-all-done.4 = f32[512,1,2]{2,1,0:T(1,128)S(1)} async-done(((f32[512,1,2]{2,1,0:T(1,128)}), f32[512,1,2]{2,1,0:T(1,128)S(1)}, u32[]{:S(2)}, u32[]{:S(2)}) %all-to-all-start.4) | async-done | bytes 4128 | tf_op jit(solution)/shard_map/all_to_all | solution.py:138
  (81 shorter events, 11.3 us)
Async XLA Ops:
  0.6 160.8 %copy-start = (bf16[256,256]{1,0:T(8,128)(2,1)S(1)}, bf16[256,256]{1,0:T(8,128)(2,1)}, u32[]{:S(2)}) copy-start(bf16[256,256]{1,0:T(8,128)(2,1)} %param.23) | copy-start | bytes 393220
  9.7 1.3 copy-start.3
  9.7 1.3 copy-start.5
  9.7 1.8 copy-start.9
  9.7 1.8 copy-start.13
  9.7 2.5 %copy-start.10 = (f32[8,128]{1,0:T(8,128)S(1)}, f32[8,128]{1,0:T(8,128)}, u32[]{:S(2)}) copy-start(f32[8,128]{1,0:T(8,128)} %param.26) | copy-start | bytes 12292
  9.7 2.5 %copy-start.14 = (f32[128]{0:T(128)S(1)}, f32[128]{0:T(128)}, u32[]{:S(2)}) copy-start(f32[128]{0:T(128)} %param.27) | copy-start | bytes 1540
  10.3 4.5 %copy-start.1 = (bf16[2048,1024]{0,1:T(8,128)(2,1)}, bf16[2048,1024]{0,1:T(8,128)(2,1)S(1)}, u32[]{:S(2)}) copy-start(bf16[2048,1024]{0,1:T(8,128)(2,1)S(1)} %pad_maximum_fusion) | copy-start | bytes 12582916
  18.5 21.6 %copy-start.8 = (f32[256]{0:T(256)S(1)}, f32[256]{0:T(256)}, u32[]{:S(2)}) copy-start(f32[256]{0:T(256)} %param.20) | copy-start | bytes 3076
  18.5 21.6 %copy-start.6 = (s32[3,512]{1,0:T(4,128)S(1)}, s32[3,512]{1,0:T(4,128)}, u32[]{:S(2)}) copy-start(s32[3,512]{1,0:T(4,128)} %param.17) | copy-start | bytes 18436
  20.5 50.5 %all-to-all-start = ((f32[64,1,4112]{2,1,0:T(1,128)}), f32[64,1,4112]{2,1,0:T(1,128)S(1)}, u32[]{:S(2)}, u32[]{:S(2)}) async-start(f32[64,1,4112]{2,1,0:T(1,128)} %all_to_all.22), calls=%async_computation | async-start | bytes 2162688 | tf_op jit(solution)/shard_map/all_to_all | solution.py:120
  73.3 38.2 %all-to-all-start.1 = ((f32[64,1,4112]{2,1,0:T(1,128)}), f32[64,1,4112]{2,1,0:T(1,128)S(1)}, u32[]{:S(2)}, u32[]{:S(2)}) async-start(f32[64,1,4112]{2,1,0:T(1,128)} %broadcast_in_dim.6), calls=%async_computation.1 | async-start | bytes 2162688 | tf_op jit(solution)/shard_map/all_to_all | solution.py:123
  87.6 24.7 %copy-start.7 = (f32[256]{0:T(256)S(1)}, f32[256]{0:T(256)}, u32[]{:S(2)}) copy-start(f32[256]{0:T(256)} %param.21) | copy-start | bytes 3076
  112.4 2.2 %copy-start.2 = (bf16[2048,1024]{0,1:T(8,128)(2,1)S(1)}, bf16[2048,1024]{0,1:T(8,128)(2,1)}, u32[]{:S(2)}) copy-start(bf16[2048,1024]{0,1:T(8,128)(2,1)} %copy-done.1) | copy-start | bytes 12582916
  114.6 2.2 %copy-start.4 = (bf16[2048,1024]{1,0:T(8,128)(2,1)S(1)}, bf16[2048,1024]{1,0:T(8,128)(2,1)}, u32[]{:S(2)}) copy-start(bf16[2048,1024]{1,0:T(8,128)(2,1)} %copy.39) | copy-start | bytes 12582916
  129.2 32.2 %copy-start.11 = (f32[256]{0:T(256)S(1)}, f32[256]{0:T(256)}, u32[]{:S(2)}) copy-start(f32[256]{0:T(256)} %param.24) | copy-start | bytes 3076
  129.2 32.2 %copy-start.12 = (f32[256]{0:T(256)S(1)}, f32[256]{0:T(256)}, u32[]{:S(2)}) copy-start(f32[256]{0:T(256)} %param.22) | copy-start | bytes 3076
  130.4 30.1 %all-to-all-start.3 = ((f32[4,264,256]{2,1,0:T(8,128)}), f32[4,264,256]{2,1,0:T(8,128)S(1)}, u32[]{:S(2)}, u32[]{:S(2)}) async-start(f32[4,264,256]{2,1,0:T(8,128)} %reduce_sum.92), calls=%async_computation.3 | async-start | bytes 2162688 | tf_op jit(solution)/shard_map/all_to_all | solution.py:129
  165.2 27.1 %all-to-all-start.4 = ((f32[512,1,2]{2,1,0:T(1,128)}), f32[512,1,2]{2,1,0:T(1,128)S(1)}, u32[]{:S(2)}, u32[]{:S(2)}) async-start(f32[512,1,2]{2,1,0:T(1,128)} %broadcast_in_dim.8), calls=%async_computation.4 | async-start | bytes 524288 | tf_op jit(solution)/shard_map/all_to_all | solution.py:138
